TPU v7x, 256 devices: a whole 4x4x8 slice. The times are simulated.
256 devices in a mesh: circ: 8 (over y_lo, x), span: 32 (over y_hi, z, core).
Axes of the slice: x: 4, y: 4 (y_hi: 2, y_lo: 2; y = y_hi * 2 + y_lo), z: 8, core: 2. Of those that a mesh axis runs over, the one named last changes fastest.
Arguments:
- q_old: float32 [5, 32, 4096, 128], P(None, 'circ', 'span'), may hold values from -6 to 6
- pseudo_rate: float32 [32, 4096, 128], P('circ', 'span'), may hold values from 0.15 to 0.45
- flux_jacobians: float32 [3, 5, 5], replicated, may hold values from -2.5 to 2.5
- rotor_face: float32 [5, 32, 4096], P(None, 'circ', 'span'), may hold values from -6 to 6
- offsets: int32 [4096], P('span'), may hold values from 0 to 31
- owners: int32 [8, 128, 4], P('circ', 'span'), may hold values from 0 to 31, all different within a row; in each aligned block of 4 rows (0 to 3, 4 to 7, ..., all dimensions but the last counted through in order) at most 2 rows name the same one
- slots: int32 [8, 128, 4], P('circ', 'span'), may hold values from 0 to 3
- weight_idx: int32 [8, 128, 4], P('circ', 'span'), may hold values from 0 to 15
- weight_table: float32 [16], replicated, may hold values from 0.3 to 1
Outputs:
- q_new: float32 [5, 32, 4096, 128], P(None, 'circ', 'span')
Inputs may be any that keep to these rules, and one draw needn't show every extreme that they name: The 4 owners of one rotor panel differ; among the 4 rotor panels of one device in one circumferential block, no owner is named more than 2 times, and that count is reached.
All inputs are finite; a program needn't handle non-finite values.
Results may differ from a plain program's by a relative error of at most 0.000068.
Values sent between devices are 32-bit elements; how exact they have to be, the bound alone decides.
No kernel may reach another device: no remote copies, remote signals or barrier semaphores. Data moves between devices by JAX's collectives and lax.ppermute only.
A program may use at most 64 MiB of HBM per device.

v0:
```python
import jax
import jax.numpy as jnp
from jax import lax
from jax.experimental import pallas as pl
from jax.experimental.pallas import tpu as pltpu
from jax.sharding import PartitionSpec as P

NF = 5
KP_DEV = 4
PW = 32


inv_step = 0.5
viscosity = 0.1


def with_halo(block, sides, width):
    for axis, dim in sides:
        count = lax.axis_size(axis)
        forward = [(i, i + 1) for i in range(count - 1)]
        forward.append((count - 1, 0))
        backward = [(target, source) for source, target in forward]
        low = lax.ppermute(
            lax.slice_in_dim(block, block.shape[dim] - width, None, axis=dim), axis, forward
        )
        high = lax.ppermute(lax.slice_in_dim(block, 0, width, axis=dim), axis, backward)
        block = jnp.concatenate([low, block, high], axis=dim)
    return block


def halo_parts(block):
    parts = []
    for axis, dim in (("circ", 1), ("span", 2)):
        count = lax.axis_size(axis)
        forward = [(i, (i + 1) % count) for i in range(count)]
        backward = [(target, source) for source, target in forward]
        low = lax.ppermute(lax.slice_in_dim(block, block.shape[dim] - 1, None, axis=dim), axis, forward)
        high = lax.ppermute(lax.slice_in_dim(block, 0, 1, axis=dim), axis, backward)
        parts += [low, high]
    span_index = lax.axis_index("span")
    span_last = lax.axis_size("span") - 1
    parts[2] = parts[2] * (span_index != 0).astype(block.dtype)
    parts[3] = parts[3] * (span_index != span_last).astype(block.dtype)
    return parts


def lateral_of(block, parts):
    circ_low, circ_high, span_low, span_high = parts
    return (
        jnp.concatenate([block[:, 1:], circ_high], axis=1),
        jnp.concatenate([circ_low, block[:, :-1]], axis=1),
        jnp.concatenate([block[:, :, 1:], span_high], axis=2),
        jnp.concatenate([span_low, block[:, :, :-1]], axis=2),
    )


def stencil_kernel(j_ref, c_ref, cu_ref, cd_ref, su_ref, sd_ref, prev_ref, rate_ref, out_ref):
    lane = lax.broadcasted_iota(jnp.int32, (8, 128), 1)
    probe = pltpu.roll(lane, 1, 1)
    numpy_order = probe == (lane + 127) % 128

    def chunk(i, carry):
        rows = pl.ds(pl.multiple_of(i * 8, 8), 8)
        cur = [c_ref[g, 0, rows, :] for g in range(NF)]
        cu = [cu_ref[g, 0, rows, :] for g in range(NF)]
        cd = [cd_ref[g, 0, rows, :] for g in range(NF)]
        su = [su_ref[g, 0, rows, :] for g in range(NF)]
        sd = [sd_ref[g, 0, rows, :] for g in range(NF)]
        au, ad = [], []
        for g in range(NF):
            one = pltpu.roll(cur[g], 1, 1)
            other = pltpu.roll(cur[g], 127, 1)
            down = jnp.where(numpy_order, one, other)
            up = jnp.where(numpy_order, other, one)
            ad.append(jnp.where(lane == 0, 0.0, down))
            au.append(jnp.where(lane == 127, 0.0, up))
        dc = [cu[g] - cd[g] for g in range(NF)]
        ds = [su[g] - sd[g] for g in range(NF)]
        da = [au[g] - ad[g] for g in range(NF)]
        rate = rate_ref[0, rows, :]
        for f in range(NF):
            convection = None
            for d, diff in enumerate((dc, ds, da)):
                term = j_ref[d * NF * NF + f * NF] * diff[0]
                for g in range(1, NF):
                    term = term + j_ref[d * NF * NF + f * NF + g] * diff[g]
                convection = term if convection is None else convection + term
            laplacian = cu[f] + cd[f] + (su[f] + sd[f]) + (au[f] + ad[f]) - 6.0 * cur[f]
            residual = (
                inv_step * (cur[f] - prev_ref[f, 0, rows, :])
                + 0.5 * convection
                - viscosity * laplacian
            )
            out_ref[f, 0, rows, :] = cur[f] - rate * residual
        return carry

    lax.fori_loop(0, c_ref.shape[2] // 8, chunk, 0)


def bulk_sweep(current, previous, rate_cells, jacobians):
    parts = halo_parts(current)
    circ_low, circ_high, span_low, span_high = parts
    padded = jnp.concatenate([circ_low, current, circ_high], axis=1)
    span_up = jnp.concatenate([current[:, :, 1:], span_high], axis=2)
    span_down = jnp.concatenate([span_low, current[:, :, :-1]], axis=2)
    nf, rows, span, axial = current.shape
    block = (nf, 1, span, axial)
    spec = lambda shift: pl.BlockSpec(block, lambda t: (0, t + shift, 0, 0))
    out = pl.pallas_call(
        stencil_kernel,
        grid=(rows,),
        in_specs=[
            pl.BlockSpec(memory_space=pltpu.SMEM),
            spec(1),
            spec(2),
            spec(0),
            spec(0),
            spec(0),
            spec(0),
            pl.BlockSpec((1, span, axial), lambda t: (t, 0, 0)),
        ],
        out_specs=spec(0),
        out_shape=jax.ShapeDtypeStruct(current.shape, current.dtype),
    )(jacobians.reshape(-1), padded, padded, padded, span_up, span_down, previous, rate_cells)
    return out, parts


def contract(matrix, values):
    total = matrix[:, 0, None, None, None] * values[0][None]
    for g in range(1, matrix.shape[1]):
        total = total + matrix[:, g, None, None, None] * values[g][None]
    return total


def update(current, previous, rate_cells, neighbours, jacobians):
    circ_up, circ_down, span_up, span_down, axial_up, axial_down = neighbours
    convection = contract(jacobians[0], circ_up - circ_down)
    convection = convection + contract(jacobians[1], span_up - span_down)
    convection = convection + contract(jacobians[2], axial_up - axial_down)
    laplacian = (
        circ_up + circ_down + (span_up + span_down) + (axial_up + axial_down) - 6.0 * current
    )
    residual = inv_step * (current - previous) + 0.5 * convection - viscosity * laplacian
    return current - rate_cells[None] * residual


def lateral(padded):
    return (
        padded[:, 2:, 1:-1],
        padded[:, :-2, 1:-1],
        padded[:, 1:-1, 2:],
        padded[:, 1:-1, :-2],
    )


def advance(padded, current, previous, rate_cells, jacobians):
    zero_column = jnp.zeros_like(current[..., :1])
    axial_up = jnp.concatenate([current[..., 1:], zero_column], axis=-1)
    axial_down = jnp.concatenate([zero_column, current[..., :-1]], axis=-1)
    neighbours = lateral(padded) + (axial_up, axial_down)
    return update(current, previous, rate_cells, neighbours, jacobians)


def wall_zero(field_array, width):
    span_index = lax.axis_index("span")
    span_count = lax.axis_size("span")
    length = field_array.shape[2]
    position = jnp.arange(length, dtype=jnp.int32)
    at_hub = jnp.logical_and(span_index == 0, position < width)
    at_tip = jnp.logical_and(span_index == span_count - 1, position >= length - width)
    keeping = jnp.logical_not(jnp.logical_or(at_hub, at_tip)).astype(field_array.dtype)
    keeping = keeping.reshape(1, 1, length, 1)
    return field_array * keeping


def body(
    q_old, pseudo_rate, flux_jacobians, rotor_face, offsets, owners, slots, weight_idx, weight_table
):
    circ_count = lax.axis_size("circ")
    rows_local = rotor_face.shape[1]
    total_rows = rows_local * circ_count
    row_iota = jnp.arange(rows_local, dtype=jnp.int32)
    copies = jnp.broadcast_to(rotor_face[None], (circ_count,) + rotor_face.shape)
    gathered = lax.all_to_all(copies, "circ", 0, 0, tiled=True)
    all_rows = jnp.transpose(gathered, (1, 0, 2, 3)).reshape(NF, total_rows, rotor_face.shape[2])
    first_row = lax.axis_index("circ") * rows_local
    source_rows = (first_row + row_iota[:, None] - offsets[None, :]) % total_rows
    rotated = jnp.take_along_axis(all_rows, source_rows[None], axis=1)
    panels = rotated.reshape(NF, rows_local, KP_DEV, PW)
    table_ids = jnp.arange(weight_table.shape[0], dtype=jnp.int32)
    weights = jnp.sum(jnp.where(weight_idx[..., None] == table_ids, weight_table, 0.0), axis=-1)
    targets = owners[0] * KP_DEV + slots[0]
    local_weights = weights[0]
    panel_ids = jnp.arange(KP_DEV * lax.axis_size("span"), dtype=jnp.int32)
    mixing = jnp.sum(
        jnp.where(targets[None] == panel_ids[:, None, None], local_weights[None], 0.0), axis=-1
    )
    span_count = lax.axis_size("span")
    contributions = jnp.einsum("gk,ftkp->gftp", mixing, panels, precision=lax.Precision.HIGHEST)
    contributions = contributions.reshape((span_count, KP_DEV) + contributions.shape[1:])
    received = lax.all_to_all(contributions, "span", 0, 0, tiled=True)
    own_panels = jnp.sum(received, axis=0)
    inlet_plane = jnp.transpose(own_panels, (1, 2, 0, 3)).reshape(NF, rows_local, KP_DEV * PW)

    mid_bulk, old_parts = bulk_sweep(q_old, q_old, pseudo_rate, flux_jacobians)
    new_bulk, mid_parts = bulk_sweep(mid_bulk, q_old, pseudo_rate, flux_jacobians)

    inlet = inlet_plane[..., None]
    old_edge = lateral_of(q_old[..., :1], [p[..., :1] for p in old_parts]) + (
        q_old[..., 1:2],
        inlet,
    )
    mid_first = update(
        q_old[..., :1], q_old[..., :1], pseudo_rate[..., :1], old_edge, flux_jacobians
    )
    mid_pair = jnp.concatenate([mid_first, mid_bulk[..., 1:2]], axis=-1)
    mid_edge = lateral_of(mid_pair, halo_parts(mid_pair)) + (
        mid_bulk[..., 1:3],
        jnp.concatenate([inlet, mid_first], axis=-1),
    )
    new_pair = update(mid_pair, q_old[..., :2], pseudo_rate[..., :2], mid_edge, flux_jacobians)
    return jnp.concatenate([new_pair, new_bulk[..., 2:]], axis=-1)


def solution(mesh):
    return jax.shard_map(
        body,
        mesh=mesh,
        in_specs=(
            P(None, "circ", "span", None),
            P("circ", "span", None),
            P(),
            P(None, "circ", "span"),
            P("span"),
            P("circ", "span", None),
            P("circ", "span", None),
            P("circ", "span", None),
            P(),
        ),
        out_specs=P(None, "circ", "span", None),
        check_vma=False,
    )
```

profile of v0, /device:TPU:6, one launch (start us, length us, event | category | flops | bytes accessed | tf_op | source)
XLA Modules:
  0.0 138.7 jit_solution(12194699541017028427)
XLA Ops:
  0.0 1.7 %fusion.21 = (f32[5,4,1,128]{3,2,1,0:T(1,128)}, f32[5,4,1,128]{3,2,1,0:T(1,128)}) fusion(f32[5,4,128,128]{3,2,1,0:T(8,128)} %prev_ref.3), kind=kLoop, calls=%fused_computation.129 | loop fusion | bytes 40960 | tf_op jit(solution)/shard_map/slice | solution.py:37
  1.7 7.9 %collective-permute-start.2 = (f32[5,4,1,128]{3,2,1,0:T(1,128)}, f32[5,4,1,128]{3,2,1,0:T(1,128)}, u32[]{:S(2)}, u32[]{:S(2)}) collective-permute-start(f32[5,4,1,128]{3,2,1,0:T(1,128)} %get-tuple-element.69), channel_id=1, source_target_pairs={{1,0},{2,1},{3,2},{4,3},{5,4},{6,5},{7,6},{8,7},{9,8},{10,9},{11,1... | collective-permute-start | bytes 30728 | tf_op jit(solution)/shard_map/ppermute | solution.py:38
  9.6 2.0 %fusion.23 = (f32[5,1,128,128]{3,2,1,0:T(8,128)}, f32[5,1,128,128]{3,2,1,0:T(8,128)}) fusion(f32[5,4,128,128]{3,2,1,0:T(8,128)} %prev_ref.3), kind=kLoop, calls=%fused_computation.131 | loop fusion | bytes 1310720 | tf_op jit(solution)/shard_map/slice | solution.py:37
  14.3 6.5 %all-to-all-start = ((f32[8,5,4,128]{3,2,1,0:T(4,128)}), f32[8,5,4,128]{3,2,1,0:T(4,128)}, u32[]{:S(2)}, u32[]{:S(2)}) async-start(f32[8,5,4,128]{3,2,1,0:T(4,128)} %broadcast_in_dim.48), calls=%async_computation | async-start | bytes 163840 | tf_op jit(solution)/shard_map/all_to_all | solution.py:184
  22.1 1.6 %fusion.17 = (f32[5,3,128,1]{3,2,1,0:T(8,128)}, f32[5,3,128,1]{3,2,1,0:T(8,128)}) fusion(f32[5,4,128,128]{3,2,1,0:T(8,128)S(1)} %copy-done), kind=kLoop, calls=%fused_computation.125 | loop fusion | bytes 30720 | tf_op jit(solution)/shard_map/slice | solution.py:50
  24.5 1.8 %fusion.22 = (f32[5,4,127,128]{3,2,1,0:T(8,128)}, f32[5,4,127,128]{3,2,1,0:T(8,128)}) fusion(f32[5,4,128,128]{3,2,1,0:T(8,128)S(1)} %copy-done), kind=kLoop, calls=%fused_computation.130 | loop fusion | bytes 5201920 | tf_op jit(solution)/shard_map/slice | solution.py:105
  31.1 2.7 %pad_maximum_fusion.6.su_ref = f32[5,4,128,128]{3,2,1,0:T(8,128)} fusion(f32[5,4,1,128]{3,2,1,0:T(1,128)S(1)} %broadcast_multiply_fusion.5, f32[5,4,127,128]{3,2,1,0:T(8,128)} %get-tuple-element.71), kind=kLoop, calls=%fused_computation.9 | loop fusion | flops 327680 | bytes 2621440 | tf_op jit(solution)/shard_map/concatenate | solution.py:104
  37.6 2.9 %copy.161 = f32[5,8,4,128]{0,3,2,1:T(8,128)} copy(f32[5,8,4,128]{3,2,0,1:T(4,128)} %bitcast.6) | data formatting | bytes 163840 | tf_op jit(solution)/shard_map/transpose | solution.py:185
  40.5 5.5 %gather_fusion = f32[512,5]{1,0:T(8,128)S(1)} fusion(f32[5,32,128]{0,2,1:T(8,128)} %bitcast.65, s32[512]{0:T(512)S(1)} %fusion.15), kind=kCustom, calls=%fused_computation | custom fusion | bytes 24576 | tf_op jit(solution)/shard_map/jit(take_along_axis)/gather | solution.py:188
  50.1 6.5 %all-to-all-start.1 = ((f32[32,1,2560]{2,1,0:T(1,128)}), f32[32,1,2560]{2,1,0:T(1,128)S(1)}, u32[]{:S(2)}, u32[]{:S(2)}) async-start(f32[32,1,2560]{2,1,0:T(1,128)} %reshape.628), calls=%async_computation.1 | async-start | bytes 655360 | tf_op jit(solution)/shard_map/all_to_all | solution.py:201
  58.2 8.7 %shard_map.91 = f32[5,4,128,128]{3,2,1,0:T(8,128)} custom-call(f32[75]{0:T(128)} %reshape.588.j_ref, f32[5,6,128,128]{3,2,1,0:T(8,128)} %pad_maximum_fusion.c_ref.cu_ref.cd_ref, f32[5,6,128,128]{3,2,1,0:T(8,128)} %pad_maximum_fusion.c_ref.cu_ref.cd_ref, f32[5,6,128,128]{3,2,1,0:T(8,128)} %pad_maximum_fusion.c_ref.cu_ref.cd_ref, ...), custom_call_target="tpu_custom_call" | custom-call | tf_op jit(solution)/shard_map/pallas_call | solution.py:109
  74.1 4.7 %collective-permute-start.10 = (f32[5,4,1,128]{3,2,1,0:T(1,128)S(1)}, f32[5,4,1,128]{3,2,1,0:T(1,128)S(1)}, u32[]{:S(2)}, u32[]{:S(2)}) collective-permute-start(f32[5,4,1,128]{3,2,1,0:T(1,128)S(1)} %get-tuple-element.63), channel_id=1, source_target_pairs={{1,0},{2,1},{3,2},{4,3},{5,4},{6,5},{7,6},{8,7},{9,8},{10,9},{11,1... | collective-permute-start | bytes 30728 | tf_op jit(solution)/shard_map/ppermute | solution.py:38
  82.7 2.6 %collective-permute-done.9 = f32[5,1,128,128]{3,2,1,0:T(8,128)S(1)} collective-permute-done((f32[5,1,128,128]{3,2,1,0:T(8,128)S(1)}, f32[5,1,128,128]{3,2,1,0:T(8,128)S(1)}, u32[]{:S(2)}, u32[]{:S(2)}) %collective-permute-start.9) | collective-permute-done | bytes 327712 | tf_op jit(solution)/shard_map/ppermute | solution.py:38
  86.8 8.7 %shard_map.92 = f32[5,4,128,128]{3,2,1,0:T(8,128)} custom-call(f32[75]{0:T(128)} %reshape.588.j_ref, f32[5,6,128,128]{3,2,1,0:T(8,128)} %pad_maximum_fusion.1.c_ref.cu_ref.cd_ref, f32[5,6,128,128]{3,2,1,0:T(8,128)} %pad_maximum_fusion.1.c_ref.cu_ref.cd_ref, f32[5,6,128,128]{3,2,1,0:T(8,128)} %pad_maximum_fusion.1.c_ref.cu_ref.cd_ref, ...), custom_call_target="tpu_custom_call" | custom-call | tf_op jit(solution)/shard_map/pallas_call | solution.py:109
  95.5 2.8 %slice.423 = f32[5,4,128,126]{3,2,1,0:T(8,128)} slice(f32[5,4,128,128]{3,2,1,0:T(8,128)} %shard_map.92), slice={[0:5], [0:4], [0:128], [2:128]} | slice | bytes 2580480 | tf_op jit(solution)/shard_map/slice | solution.py:222
  100.3 1.8 %reshape.629 = f32[32,4,5,4,32]{4,3,2,1,0:T(4,128)} reshape(f32[32,2560]{1,0:T(8,128)S(1)} %reduce.63) | data formatting | bytes 655360
  102.0 1.7 %reduce_sum.29 = f32[4,5,4,32]{3,2,1,0:T(4,128)S(1)} reduce(f32[32,4,5,4,32]{4,3,2,1,0:T(4,128)} %reshape.629, f32[]{:T(128)} %constant.26.clone.1), dimensions={0}, to_apply=%region_2.3 | reduce | flops 79360 | bytes 337924 | tf_op jit(solution)/shard_map/reduce_sum | solution.py:202
  103.8 2.4 %broadcast_in_dim_reshape.4 = f32[5,4,128,1]{3,2,1,0:T(8,128)} reshape(f32[5,4,4,32]{3,2,1,0:T(4,128)S(1)} %copy.166) | data formatting | bytes 20480 | tf_op jit(solution)/shard_map/broadcast_in_dim;reshape | solution.py:208
  106.2 1.9 %slice_subtract_fusion.1 = f32[5,4,128,1]{3,2,1,0:T(8,128)S(1)} fusion(f32[5,4,128,1]{3,2,1,0:T(8,128)} %broadcast_in_dim_reshape.4, f32[5,4,128,128]{3,2,1,0:T(8,128)S(1)} %copy-done.1), kind=kLoop, calls=%fused_computation.22 | loop fusion | flops 2560 | bytes 30720 | tf_op jit(solution)/shard_map/sub | solution.py:139
  109.7 4.8 %multiply_subtract_fusion.1 = f32[5,4,128,1]{3,2,1,0:T(8,128)S(1)} fusion(f32[5,4,128,1]{3,2,1,0:T(8,128)S(1)} %copy-done.4, f32[5,4,128,128]{3,2,1,0:T(8,128)S(1)} %copy-done.1, f32[5,3,128,1]{3,2,1,0:T(8,128)} %get-tuple-element.61, f32[5,1,128,1]{3,2,1,0:T(8,128)S(1)} %bitcast.62, f32[5,1,128,1]{3,2,1,0:T(8,128)S(1)} %bitcast.64, ...), kind=kLoop, calls=%fused_computation.20 | loop fusion | flops 120320 | bytes 114988 | tf_op jit(solution)/shard_map/sub | solution.py:144
  116.5 4.1 %collective-permute-start.5 = (f32[5,1,128,2]{3,2,1,0:T(8,128)S(1)}, f32[5,1,128,2]{3,2,1,0:T(8,128)S(1)}, u32[]{:S(2)}, u32[]{:S(2)}) collective-permute-start(f32[5,1,128,2]{3,2,1,0:T(8,128)S(1)} %get-tuple-element.42), channel_id=1, source_target_pairs={{0,32},{32,64},{64,96},{96,128},{128,160},{160,192},{192,224},{224... | collective-permute-start | bytes 15368 | tf_op jit(solution)/shard_map/ppermute | solution.py:37
  120.6 3.3 %collective-permute-start.6 = (f32[5,4,1,2]{3,2,1,0:T(1,128)S(1)}, f32[5,4,1,2]{3,2,1,0:T(1,128)S(1)}, u32[]{:S(2)}, u32[]{:S(2)}) collective-permute-start(f32[5,4,1,2]{3,2,1,0:T(1,128)S(1)} %get-tuple-element.37), channel_id=1, source_target_pairs={{1,0},{2,1},{3,2},{4,3},{5,4},{6,5},{7,6},{8,7},{9,8},{10,9},{11,1... | collective-permute-start | bytes 488 | tf_op jit(solution)/shard_map/ppermute | solution.py:38
  125.3 6.1 %collective-permute-done.7 = f32[5,4,1,2]{3,2,1,0:T(1,128)S(1)} collective-permute-done((f32[5,4,1,2]{3,2,1,0:T(1,128)S(1)}, f32[5,4,1,2]{3,2,1,0:T(1,128)S(1)}, u32[]{:S(2)}, u32[]{:S(2)}) %collective-permute-start.7) | collective-permute-done | bytes 192 | tf_op jit(solution)/shard_map/ppermute | solution.py:37
  132.9 4.2 %multiply_subtract_fusion = f32[5,4,128,2]{3,2,1,0:T(8,128)S(1)} fusion(f32[5,4,128,128]{3,2,1,0:T(8,128)S(1)} %copy-done.1, f32[5,4,128,128]{3,2,1,0:T(8,128)S(1)} %copy-done.2, f32[5,3,128,2]{3,2,1,0:T(8,128)S(1)} %get-tuple-element.40, f32[5,1,128,2]{3,2,1,0:T(8,128)S(1)} %collective-permute-done.5, f32[5,1,128,2]{3,2,1,0:T(8,128)S(1)} %collective-permute-done.4, ...), kind=kLoop, calls=%fused_computation.19 | loop fusion | flops 250880 | bytes 239916 | tf_op jit(solution)/shard_map/sub | solution.py:144
  (171 shorter events, 41.0 us)
Async XLA Ops:
  0.0 20.7 %copy-start = (f32[5,4,128,128]{3,2,1,0:T(8,128)S(1)}, f32[5,4,128,128]{3,2,1,0:T(8,128)}, u32[]{:S(2)}) copy-start(f32[5,4,128,128]{3,2,1,0:T(8,128)} %prev_ref.3) | copy-start | bytes 3932164
  0.0 13.6 %copy-start.20 = (f32[5,4,128]{2,1,0:T(4,128)S(1)}, f32[5,4,128]{2,1,0:T(4,128)}, u32[]{:S(2)}) copy-start(f32[5,4,128]{2,1,0:T(4,128)} %param.12) | copy-start | bytes 30724
  1.7 32.1 %collective-permute-start.3 = (f32[5,4,1,128]{3,2,1,0:T(1,128)}, f32[5,4,1,128]{3,2,1,0:T(1,128)}, u32[]{:S(2)}, u32[]{:S(2)}) collective-permute-start(f32[5,4,1,128]{3,2,1,0:T(1,128)} %get-tuple-element.68), channel_id=1, source_target_pairs={{0,1},{1,2},{2,3},{3,4},{4,5},{5,6},{6,7},{7,8},{8,9},{9,10},{10,1... | collective-permute-start | bytes 30728 | tf_op jit(solution)/shard_map/ppermute | solution.py:37
  1.7 28.7 %collective-permute-start.2 = (f32[5,4,1,128]{3,2,1,0:T(1,128)}, f32[5,4,1,128]{3,2,1,0:T(1,128)}, u32[]{:S(2)}, u32[]{:S(2)}) collective-permute-start(f32[5,4,1,128]{3,2,1,0:T(1,128)} %get-tuple-element.69), channel_id=1, source_target_pairs={{1,0},{2,1},{3,2},{4,3},{5,4},{6,5},{7,6},{8,7},{9,8},{10,9},{11,1... | collective-permute-start | bytes 30728 | tf_op jit(solution)/shard_map/ppermute | solution.py:38
  11.6 45.1 %collective-permute-start.1 = (f32[5,1,128,128]{3,2,1,0:T(8,128)}, f32[5,1,128,128]{3,2,1,0:T(8,128)S(1)}, u32[]{:S(2)}, u32[]{:S(2)}) collective-permute-start(f32[5,1,128,128]{3,2,1,0:T(8,128)} %get-tuple-element.72), channel_id=1, source_target_pairs={{0,32},{32,64},{64,96},{96,128},{128,160},{160,192},{192,224},{224... | collective-permute-start | bytes 983048 | tf_op jit(solution)/shard_map/ppermute | solution.py:37
  12.2 44.5 %collective-permute-start = (f32[5,1,128,128]{3,2,1,0:T(8,128)}, f32[5,1,128,128]{3,2,1,0:T(8,128)S(1)}, u32[]{:S(2)}, u32[]{:S(2)}) collective-permute-start(f32[5,1,128,128]{3,2,1,0:T(8,128)} %get-tuple-element.73), channel_id=1, source_target_pairs={{32,0},{64,32},{96,64},{128,96},{160,128},{192,160},{224,192},{0,2... | collective-permute-start | bytes 983048 | tf_op jit(solution)/shard_map/ppermute | solution.py:38
  14.3 23.3 %all-to-all-start = ((f32[8,5,4,128]{3,2,1,0:T(4,128)}), f32[8,5,4,128]{3,2,1,0:T(4,128)}, u32[]{:S(2)}, u32[]{:S(2)}) async-start(f32[8,5,4,128]{3,2,1,0:T(4,128)} %broadcast_in_dim.48), calls=%async_computation | async-start | bytes 163840 | tf_op jit(solution)/shard_map/all_to_all | solution.py:184
  22.0 13.7 %copy-start.5 = (f32[5,4,127,1]{3,2,1,0:T(8,128)}, f32[5,4,127,1]{3,2,1,0:T(8,128)S(1)}, u32[]{:S(2)}) copy-start(f32[5,4,127,1]{3,2,1,0:T(8,128)S(1)} %get-tuple-element.58) | copy-start | bytes 30484
  24.4 3.5 %copy-start.43 = (s32[1,4,4]{2,1,0:T(4,128)S(1)}, s32[1,4,4]{2,1,0:T(4,128)}, u32[]{:S(2)}) copy-start(s32[1,4,4]{2,1,0:T(4,128)} %param.14) | copy-start | bytes 196
  24.4 3.5 %copy-start.44 = (s32[1,4,4]{2,1,0:T(4,128)S(1)}, s32[1,4,4]{2,1,0:T(4,128)}, u32[]{:S(2)}) copy-start(s32[1,4,4]{2,1,0:T(4,128)} %param.16) | copy-start | bytes 196
  37.6 8.5 %copy-start.45 = (pred[4,128]{1,0:T(4,128)(4,1)S(1)}, pred[4,128]{1,0:T(4,128)(4,1)}, u32[]{:S(2)}) copy-start(pred[4,128]{1,0:T(4,128)(4,1)} %compare_and_fusion) | copy-start | bytes 1540
  37.6 8.8 %copy-start.18 = (f32[32,4,4,1,1]{0,2,4,3,1:T(4,128)S(1)}, f32[32,4,4,1,1]{0,2,4,3,1:T(4,128)}, u32[]{:S(2)}) copy-start(f32[32,4,4,1,1]{0,2,4,3,1:T(4,128)} %copy.171) | copy-start | bytes 6148
  50.1 48.2 %all-to-all-start.1 = ((f32[32,1,2560]{2,1,0:T(1,128)}), f32[32,1,2560]{2,1,0:T(1,128)S(1)}, u32[]{:S(2)}, u32[]{:S(2)}) async-start(f32[32,1,2560]{2,1,0:T(1,128)} %reshape.628), calls=%async_computation.1 | async-start | bytes 655360 | tf_op jit(solution)/shard_map/all_to_all | solution.py:201
  68.7 10.0 %collective-permute-start.11 = (f32[5,4,1,128]{3,2,1,0:T(1,128)S(1)}, f32[5,4,1,128]{3,2,1,0:T(1,128)S(1)}, u32[]{:S(2)}, u32[]{:S(2)}) collective-permute-start(f32[5,4,1,128]{3,2,1,0:T(1,128)S(1)} %get-tuple-element.62), channel_id=1, source_target_pairs={{0,1},{1,2},{2,3},{3,4},{4,5},{5,6},{6,7},{7,8},{8,9},{9,10},{10,1... | collective-permute-start | bytes 30728 | tf_op jit(solution)/shard_map/ppermute | solution.py:37
  72.1 10.6 %collective-permute-start.8 = (f32[5,1,128,128]{3,2,1,0:T(8,128)S(1)}, f32[5,1,128,128]{3,2,1,0:T(8,128)S(1)}, u32[]{:S(2)}, u32[]{:S(2)}) collective-permute-start(f32[5,1,128,128]{3,2,1,0:T(8,128)S(1)} %get-tuple-element.66), channel_id=1, source_target_pairs={{0,32},{32,64},{64,96},{96,128},{128,160},{160,192},{192,224},{224... | collective-permute-start | bytes 983048 | tf_op jit(solution)/shard_map/ppermute | solution.py:37
  72.9 12.4 %collective-permute-start.9 = (f32[5,1,128,128]{3,2,1,0:T(8,128)S(1)}, f32[5,1,128,128]{3,2,1,0:T(8,128)S(1)}, u32[]{:S(2)}, u32[]{:S(2)}) collective-permute-start(f32[5,1,128,128]{3,2,1,0:T(8,128)S(1)} %get-tuple-element.67), channel_id=1, source_target_pairs={{32,0},{64,32},{96,64},{128,96},{160,128},{192,160},{224,192},{0,2... | collective-permute-start | bytes 983048 | tf_op jit(solution)/shard_map/ppermute | solution.py:38
  74.1 6.0 %collective-permute-start.10 = (f32[5,4,1,128]{3,2,1,0:T(1,128)S(1)}, f32[5,4,1,128]{3,2,1,0:T(1,128)S(1)}, u32[]{:S(2)}, u32[]{:S(2)}) collective-permute-start(f32[5,4,1,128]{3,2,1,0:T(1,128)S(1)} %get-tuple-element.63), channel_id=1, source_target_pairs={{1,0},{2,1},{3,2},{4,3},{5,4},{6,5},{7,6},{8,7},{9,8},{10,9},{11,1... | collective-permute-start | bytes 30728 | tf_op jit(solution)/shard_map/ppermute | solution.py:38
  102.0 4.2 %copy-start.1 = (f32[5,4,128,128]{3,2,1,0:T(8,128)S(1)}, f32[5,4,128,128]{3,2,1,0:T(8,128)}, u32[]{:S(2)}) copy-start(f32[5,4,128,128]{3,2,1,0:T(8,128)} %prev_ref.3) | copy-start | bytes 3932164
  109.7 4.8 %copy-start.3 = (f32[5,4,128,1]{3,2,1,0:T(8,128)S(1)}, f32[5,4,128,1]{3,2,1,0:T(8,128)}, u32[]{:S(2)}) copy-start(f32[5,4,128,1]{3,2,1,0:T(8,128)} %slice.384) | copy-start | bytes 30724
  116.4 15.4 %collective-permute-start.4 = (f32[5,1,128,2]{3,2,1,0:T(8,128)S(1)}, f32[5,1,128,2]{3,2,1,0:T(8,128)S(1)}, u32[]{:S(2)}, u32[]{:S(2)}) collective-permute-start(f32[5,1,128,2]{3,2,1,0:T(8,128)S(1)} %get-tuple-element.41), channel_id=1, source_target_pairs={{32,0},{64,32},{96,64},{128,96},{160,128},{192,160},{224,192},{0,2... | collective-permute-start | bytes 15368 | tf_op jit(solution)/shard_map/ppermute | solution.py:38
  116.5 15.3 %collective-permute-start.5 = (f32[5,1,128,2]{3,2,1,0:T(8,128)S(1)}, f32[5,1,128,2]{3,2,1,0:T(8,128)S(1)}, u32[]{:S(2)}, u32[]{:S(2)}) collective-permute-start(f32[5,1,128,2]{3,2,1,0:T(8,128)S(1)} %get-tuple-element.42), channel_id=1, source_target_pairs={{0,32},{32,64},{64,96},{96,128},{128,160},{160,192},{192,224},{224... | collective-permute-start | bytes 15368 | tf_op jit(solution)/shard_map/ppermute | solution.py:37
  120.6 4.7 %collective-permute-start.6 = (f32[5,4,1,2]{3,2,1,0:T(1,128)S(1)}, f32[5,4,1,2]{3,2,1,0:T(1,128)S(1)}, u32[]{:S(2)}, u32[]{:S(2)}) collective-permute-start(f32[5,4,1,2]{3,2,1,0:T(1,128)S(1)} %get-tuple-element.37), channel_id=1, source_target_pairs={{1,0},{2,1},{3,2},{4,3},{5,4},{6,5},{7,6},{8,7},{9,8},{10,9},{11,1... | collective-permute-start | bytes 488 | tf_op jit(solution)/shard_map/ppermute | solution.py:38
  124.6 6.8 %collective-permute-start.7 = (f32[5,4,1,2]{3,2,1,0:T(1,128)S(1)}, f32[5,4,1,2]{3,2,1,0:T(1,128)S(1)}, u32[]{:S(2)}, u32[]{:S(2)}) collective-permute-start(f32[5,4,1,2]{3,2,1,0:T(1,128)S(1)} %get-tuple-element.38), channel_id=1, source_target_pairs={{0,1},{1,2},{2,3},{3,4},{4,5},{5,6},{6,7},{7,8},{8,9},{9,10},{10,1... | collective-permute-start | bytes 488 | tf_op jit(solution)/shard_map/ppermute | solution.py:37
  132.9 4.3 %copy-start.13 = (f32[5,4,128,126]{3,2,1,0:T(8,128)S(1)}, f32[5,4,128,126]{3,2,1,0:T(8,128)}, u32[]{:S(2)}) copy-start(f32[5,4,128,126]{3,2,1,0:T(8,128)} %slice.423) | copy-start | bytes 3870724
  (38 other events, 63.9 us)
where the time goes:
time: 139 us
  local copies, waits for them, and re-layouts  39.9 us (29%)
  starting transfers between devices  37.8 us (27%)
  other arithmetic  30.7 us (22%)
  Pallas kernels  17.4 us (13%)
  waiting for transfers between devices  10.8 us (8%)
    ppermute x6, starting transfers between devices, halo_parts(): high = lax.ppermute(lax.slice_in_dim(block, 0, 1, axis=dim), axis, backward)  18.6 us
    pallas_call x2, Pallas kernels, bulk_sweep(): pl.pallas_call(stencil_kernel, grid=(rows,), in_specs=[pl.BlockSpec(memor...  17.4 us
    sub x2, other arithmetic, update(): return current - rate_cells[None] * residual  9.01 us
    unnamed x99, local copies, waits for them, and re-layouts  6.7 us
    all_to_all x1, starting transfers between devices, body(): received = lax.all_to_all(contributions, 'span', 0, 0, tiled=True)  6.53 us
    all_to_all x1, starting transfers between devices, body(): gathered = lax.all_to_all(copies, 'circ', 0, 0, tiled=True)  6.45 us
    ppermute x6, waiting for transfers between devices, halo_parts(): lax.ppermute(lax.slice_in_dim(block, block.shape[dim] - 1, None, axis=dim...  6.17 us
    ppermute x6, starting transfers between devices, halo_parts(): lax.ppermute(lax.slice_in_dim(block, block.shape[dim] - 1, None, axis=dim...  6.15 us
  transfers between devices with their start and end apart: 14, of which 5 were waited for; matrix products, arithmetic and copies ran while one was open for 32% of the time, Pallas kernels for 13%

commit v1 on v0

--- a/solution.py
+++ b/solution.py
@@ -126,9 +126,10 @@
 
 
 def contract(matrix, values):
-    total = matrix[:, 0, None, None, None] * values[0][None]
+    column = lambda g: matrix[:, g].reshape((-1,) + (1,) * (values.ndim - 1))
+    total = column(0) * values[0][None]
     for g in range(1, matrix.shape[1]):
-        total = total + matrix[:, g, None, None, None] * values[g][None]
+        total = total + column(g) * values[g][None]
     return total
 
 
@@ -177,49 +178,53 @@
     q_old, pseudo_rate, flux_jacobians, rotor_face, offsets, owners, slots, weight_idx, weight_table
 ):
     circ_count = lax.axis_size("circ")
+    span_count = lax.axis_size("span")
     rows_local = rotor_face.shape[1]
     total_rows = rows_local * circ_count
-    row_iota = jnp.arange(rows_local, dtype=jnp.int32)
     copies = jnp.broadcast_to(rotor_face[None], (circ_count,) + rotor_face.shape)
     gathered = lax.all_to_all(copies, "circ", 0, 0, tiled=True)
-    all_rows = jnp.transpose(gathered, (1, 0, 2, 3)).reshape(NF, total_rows, rotor_face.shape[2])
+    row_iota = jnp.arange(rows_local, dtype=jnp.int32)
     first_row = lax.axis_index("circ") * rows_local
     source_rows = (first_row + row_iota[:, None] - offsets[None, :]) % total_rows
-    rotated = jnp.take_along_axis(all_rows, source_rows[None], axis=1)
+    global_rows = jnp.arange(total_rows, dtype=jnp.int32).reshape(circ_count, rows_local)
+    picks = global_rows[:, None, :, None, None] == source_rows[None, None, None]
+    rotated = jnp.sum(
+        jnp.where(picks, gathered[:, :, :, None, :], 0.0), axis=(0, 2)
+    )
     panels = rotated.reshape(NF, rows_local, KP_DEV, PW)
     table_ids = jnp.arange(weight_table.shape[0], dtype=jnp.int32)
     weights = jnp.sum(jnp.where(weight_idx[..., None] == table_ids, weight_table, 0.0), axis=-1)
     targets = owners[0] * KP_DEV + slots[0]
     local_weights = weights[0]
-    panel_ids = jnp.arange(KP_DEV * lax.axis_size("span"), dtype=jnp.int32)
+    panel_ids = jnp.arange(KP_DEV * span_count, dtype=jnp.int32)
     mixing = jnp.sum(
         jnp.where(targets[None] == panel_ids[:, None, None], local_weights[None], 0.0), axis=-1
-    )
-    span_count = lax.axis_size("span")
-    contributions = jnp.einsum("gk,ftkp->gftp", mixing, panels, precision=lax.Precision.HIGHEST)
-    contributions = contributions.reshape((span_count, KP_DEV) + contributions.shape[1:])
+    ).reshape(span_count, KP_DEV, KP_DEV)
+    contributions = jnp.einsum(
+        "ogk,ftkp->oftgp", mixing, panels, precision=lax.Precision.HIGHEST
+    ).reshape(span_count, NF, rows_local, KP_DEV * PW)
     received = lax.all_to_all(contributions, "span", 0, 0, tiled=True)
-    own_panels = jnp.sum(received, axis=0)
-    inlet_plane = jnp.transpose(own_panels, (1, 2, 0, 3)).reshape(NF, rows_local, KP_DEV * PW)
+    inlet_plane = jnp.sum(received, axis=0)
 
     mid_bulk, old_parts = bulk_sweep(q_old, q_old, pseudo_rate, flux_jacobians)
     new_bulk, mid_parts = bulk_sweep(mid_bulk, q_old, pseudo_rate, flux_jacobians)
 
-    inlet = inlet_plane[..., None]
-    old_edge = lateral_of(q_old[..., :1], [p[..., :1] for p in old_parts]) + (
-        q_old[..., 1:2],
-        inlet,
-    )
+    old_first, old_second = q_old[..., 0], q_old[..., 1]
+    rate_first, rate_second = pseudo_rate[..., 0], pseudo_rate[..., 1]
+    mid_second, mid_third = mid_bulk[..., 1], mid_bulk[..., 2]
+    old_lateral = lateral_of(old_first, [p[..., 0] for p in old_parts])
     mid_first = update(
-        q_old[..., :1], q_old[..., :1], pseudo_rate[..., :1], old_edge, flux_jacobians
-    )
-    mid_pair = jnp.concatenate([mid_first, mid_bulk[..., 1:2]], axis=-1)
-    mid_edge = lateral_of(mid_pair, halo_parts(mid_pair)) + (
-        mid_bulk[..., 1:3],
-        jnp.concatenate([inlet, mid_first], axis=-1),
-    )
-    new_pair = update(mid_pair, q_old[..., :2], pseudo_rate[..., :2], mid_edge, flux_jacobians)
-    return jnp.concatenate([new_pair, new_bulk[..., 2:]], axis=-1)
+        old_first, old_first, rate_first, old_lateral + (old_second, inlet_plane), flux_jacobians
+    )
+    first_lateral = lateral_of(mid_first, halo_parts(mid_first))
+    new_first = update(
+        mid_first, old_first, rate_first, first_lateral + (mid_second, inlet_plane), flux_jacobians
+    )
+    second_lateral = lateral_of(mid_second, [p[..., 1] for p in mid_parts])
+    new_second = update(
+        mid_second, old_second, rate_second, second_lateral + (mid_third, mid_first), flux_jacobians
+    )
+    return new_bulk.at[..., 0].set(new_first).at[..., 1].set(new_second)
 
 
 def solution(mesh):

time: 139 us -> 153 us (1.10)
  local copies, waits for them, and re-layouts: 39.9 us -> 57.5 us
  waiting for transfers between devices: 10.8 us -> 0.04 us
  starting transfers between devices: 37.8 us -> 40.9 us
  other arithmetic: 30.7 us -> 33.5 us
    concatenate x0 -> x18, local copies, waits for them, and re-layouts: none -> 18.2 us  [the longest x4 4.84 us: lateral_of(): jnp.concatenate([span_low, block[:, :, :-1]], axis=2)]
    scatter x0 -> x2, local copies, waits for them, and re-layouts: none -> 9.56 us  [body(): return new_bulk.at[..., 0].set(new_first).at[..., 1].set(new_second)]
    sub x2, other arithmetic: 9.01 us -> 17.8 us  [update(): return current - rate_cells[None] * residual]
    unnamed x99 -> x121, local copies, waits for them, and re-layouts: 6.7 us -> 0.26 us
    ppermute x6, waiting for transfers between devices: 6.17 us -> 0.02 us  [halo_parts(): lax.ppermute(lax.slice_in_dim(block, block.shape[dim] - 1, None, axis=dim...]
    gather x1 -> x0, local copies, waits for them, and re-layouts: 5.53 us -> none  [body(): rotated = jnp.take_along_axis(all_rows, source_rows[None], axis=1)]
    ppermute x6, waiting for transfers between devices: 4.61 us -> 0.02 us  [halo_parts(): high = lax.ppermute(lax.slice_in_dim(block, 0, 1, axis=dim), axis, backward)]
    mul x3 -> x11, local copies, waits for them, and re-layouts: 0.3 us -> 3.9 us  [the longest x9 3.68 us: contract(): total = column(0) * values[0][None]]
  transfers between devices with their start and end apart: 14 -> 14, of which waited for: 5 -> 0; matrix products, arithmetic and copies ran while one was open for 32% -> 48% of each run, Pallas kernels for 13% -> 12%
where the time goes in v1:
time: 153 us; the launch traced here: 152 us
  local copies, waits for them, and re-layouts  57.5 us (38%)
  starting transfers between devices  40.9 us (27%)
  other arithmetic  33.5 us (22%)
  Pallas kernels  17.5 us (11%)
    ppermute x6, starting transfers between devices, halo_parts(): high = lax.ppermute(lax.slice_in_dim(block, 0, 1, axis=dim), axis, backward)  20.9 us
    sub x2, other arithmetic, update(): return current - rate_cells[None] * residual  17.8 us
    pallas_call x2, Pallas kernels, bulk_sweep(): pl.pallas_call(stencil_kernel, grid=(rows,), in_specs=[pl.BlockSpec(memor...  17.5 us
    scatter x2, local copies, waits for them, and re-layouts, body(): return new_bulk.at[..., 0].set(new_first).at[..., 1].set(new_second)  9.56 us
    ppermute x6, starting transfers between devices, halo_parts(): lax.ppermute(lax.slice_in_dim(block, block.shape[dim] - 1, None, axis=dim...  8.01 us
    all_to_all x1, starting transfers between devices, body(): received = lax.all_to_all(contributions, 'span', 0, 0, tiled=True)  6.18 us
    all_to_all x1, starting transfers between devices, body(): gathered = lax.all_to_all(copies, 'circ', 0, 0, tiled=True)  5.86 us
    slice x6, local copies, waits for them, and re-layouts, halo_parts(): lax.slice_in_dim(block, block.shape[dim] - 1, None, axis=dim)  5.26 us
  transfers between devices with their start and end apart: 14, of which 0 were waited for; matrix products, arithmetic and copies ran while one was open for 48% of the time, Pallas kernels for 12%

profile of v1, /device:TPU:6, one launch (start us, length us, event | category | flops | bytes accessed | tf_op | source)
XLA Modules:
  0.0 151.8 jit_solution(14728345892950568423)
XLA Ops:
  1.1 8.0 %collective-permute-start.2 = (f32[5,4,1,128]{3,2,1,0:T(1,128)S(1)}, f32[5,4,1,128]{3,2,1,0:T(1,128)S(1)}, u32[]{:S(2)}, u32[]{:S(2)}) collective-permute-start(f32[5,4,1,128]{3,2,1,0:T(1,128)S(1)} %get-tuple-element.61), channel_id=1, source_target_pairs={{1,0},{2,1},{3,2},{4,3},{5,4},{6,5},{7,6},{8,7},{9,8},{10,9},{11,1... | collective-permute-start | bytes 30728 | tf_op jit(solution)/shard_map/ppermute | solution.py:38
  9.1 2.0 %fusion.33 = (f32[5,1,128,128]{3,2,1,0:T(8,128)}, f32[5,1,128,128]{3,2,1,0:T(8,128)}) fusion(f32[5,4,128,128]{3,2,1,0:T(8,128)} %prev_ref.3), kind=kLoop, calls=%fused_computation.158 | loop fusion | bytes 1310720 | tf_op jit(solution)/shard_map/slice | solution.py:37
  13.7 5.9 %all-to-all-start = ((f32[8,5,4,128]{3,2,1,0:T(4,128)}), f32[8,5,4,128]{3,2,1,0:T(4,128)S(1)}, u32[]{:S(2)}, u32[]{:S(2)}) async-start(f32[8,5,4,128]{3,2,1,0:T(4,128)} %broadcast_in_dim.55), calls=%async_computation | async-start | bytes 163840 | tf_op jit(solution)/shard_map/all_to_all | solution.py:185
  32.0 2.5 %pad_maximum_fusion.2.su_ref = f32[5,4,128,128]{3,2,1,0:T(8,128)} fusion(f32[5,4,1,128]{3,2,1,0:T(1,128)S(1)} %broadcast_multiply_fusion.5, f32[5,4,127,128]{3,2,1,0:T(8,128)} %get-tuple-element.63), kind=kLoop, calls=%fused_computation.2 | loop fusion | flops 327680 | bytes 2621440 | tf_op jit(solution)/shard_map/concatenate | solution.py:104
  39.4 6.2 %all-to-all-start.1 = ((f32[32,5,4,128]{3,2,1,0:T(4,128)}), f32[32,5,4,128]{3,2,1,0:T(4,128)S(1)}, u32[]{:S(2)}, u32[]{:S(2)}) async-start(f32[32,5,4,128]{3,2,1,0:T(4,128)} %copy.691), calls=%async_computation.1 | async-start | bytes 655360 | tf_op jit(solution)/shard_map/all_to_all | solution.py:206
  45.6 2.5 %pad_maximum_fusion.c_ref.cu_ref.cd_ref = f32[5,6,128,128]{3,2,1,0:T(8,128)} fusion(f32[5,1,128,128]{3,2,1,0:T(8,128)} %collective-permute-done.1, f32[5,4,128,128]{3,2,1,0:T(8,128)S(1)} %copy-done, f32[5,1,128,128]{3,2,1,0:T(8,128)S(1)} %collective-permute-done), kind=kLoop, calls=%fused_computation | loop fusion | flops 983040 | bytes 3932160 | tf_op jit(solution)/shard_map/concatenate | solution.py:103
  48.1 8.7 %shard_map.91 = f32[5,4,128,128]{3,2,1,0:T(8,128)} custom-call(f32[75]{0:T(128)} %reshape.594.j_ref, f32[5,6,128,128]{3,2,1,0:T(8,128)} %pad_maximum_fusion.c_ref.cu_ref.cd_ref, f32[5,6,128,128]{3,2,1,0:T(8,128)} %pad_maximum_fusion.c_ref.cu_ref.cd_ref, f32[5,6,128,128]{3,2,1,0:T(8,128)} %pad_maximum_fusion.c_ref.cu_ref.cd_ref, ...), custom_call_target="tpu_custom_call" | custom-call | tf_op jit(solution)/shard_map/pallas_call | solution.py:109
  56.8 3.3 %slice_reduce_fusion = (f32[5,4,128]{2,1,0:T(4,128)S(1)}, f32[5,4,128]{2,1,0:T(4,128)S(1)}) fusion(f32[5,4,128,128]{3,2,1,0:T(8,128)} %shard_map.91), kind=kLoop, calls=%fused_computation.33 | loop fusion | bytes 40960 | tf_op jit(solution)/shard_map/slice | solution.py:214
  63.1 1.7 %fusion.34 = (f32[5,1,128,1]{3,2,1,0:T(8,128)}, f32[5,128]{1,0:T(8,128)S(1)}) fusion(f32[5,1,128,128]{3,2,1,0:T(8,128)} %collective-permute-done.1), kind=kLoop, calls=%fused_computation.159 | loop fusion | bytes 7680 | tf_op jit(solution)/shard_map/slice | solution.py:215
  65.6 5.2 %collective-permute-start.6 = (f32[5,4,1,128]{3,2,1,0:T(1,128)}, f32[5,4,1,128]{3,2,1,0:T(1,128)}, u32[]{:S(2)}, u32[]{:S(2)}) collective-permute-start(f32[5,4,1,128]{3,2,1,0:T(1,128)} %get-tuple-element.55), channel_id=1, source_target_pairs={{1,0},{2,1},{3,2},{4,3},{5,4},{6,5},{7,6},{8,7},{9,8},{10,9},{11,1... | collective-permute-start | bytes 30728 | tf_op jit(solution)/shard_map/ppermute | solution.py:38
  72.3 3.3 %collective-permute-start.4 = (f32[5,1,128,128]{3,2,1,0:T(8,128)}, f32[5,1,128,128]{3,2,1,0:T(8,128)}, u32[]{:S(2)}, u32[]{:S(2)}) collective-permute-start(f32[5,1,128,128]{3,2,1,0:T(8,128)} %get-tuple-element.58), channel_id=1, source_target_pairs={{0,32},{32,64},{64,96},{96,128},{128,160},{160,192},{192,224},{224... | collective-permute-start | bytes 983048 | tf_op jit(solution)/shard_map/ppermute | solution.py:37
  75.6 1.6 %copy.714 = f32[5,4,127,1]{3,2,1,0:T(8,128)} copy(f32[5,4,127,1]{2,1,0,3:T(4,128)S(1)} %get-tuple-element.129) | data formatting | bytes 20320 | tf_op jit(solution)/shard_map/concatenate | solution.py:52
  77.1 1.6 %copy.715 = f32[5,4,127,1]{3,2,1,0:T(8,128)} copy(f32[5,4,127,1]{2,1,0,3:T(4,128)S(1)} %get-tuple-element.130) | data formatting | bytes 20320 | tf_op jit(solution)/shard_map/concatenate | solution.py:53
  84.1 2.6 %pad_maximum_fusion.5.sd_ref = f32[5,4,128,128]{3,2,1,0:T(8,128)} fusion(f32[5,4,127,128]{3,2,1,0:T(8,128)} %get-tuple-element.56, f32[5,4,1,128]{3,2,1,0:T(1,128)S(1)} %broadcast_multiply_fusion.2), kind=kLoop, calls=%fused_computation.5 | loop fusion | flops 327680 | bytes 2621440 | tf_op jit(solution)/shard_map/concatenate | solution.py:105
  88.9 1.9 %slice_reduce_fusion.21 = (f32[5,128]{1,0:T(8,128)S(1)}, f32[5,1,128,1]{3,2,1,0:T(8,128)}) fusion(f32[5,1,128,128]{3,2,1,0:T(8,128)} %collective-permute-done.4), kind=kLoop, calls=%fused_computation.148 | loop fusion | bytes 7680 | tf_op jit(solution)/shard_map/slice | solution.py:223
  90.7 2.5 %pad_maximum_fusion.1.c_ref.cu_ref.cd_ref = f32[5,6,128,128]{3,2,1,0:T(8,128)} fusion(f32[5,1,128,128]{3,2,1,0:T(8,128)S(1)} %collective-permute-done.5, f32[5,4,128,128]{3,2,1,0:T(8,128)S(1)} %copy-done.2, f32[5,1,128,128]{3,2,1,0:T(8,128)} %collective-permute-done.4), kind=kLoop, calls=%fused_computation.1 | loop fusion | flops 983040 | bytes 3932160 | tf_op jit(solution)/shard_map/concatenate | solution.py:103
  93.5 8.8 %shard_map.92 = f32[5,4,128,128]{3,2,1,0:T(8,128)} custom-call(f32[75]{0:T(128)} %reshape.594.j_ref, f32[5,6,128,128]{3,2,1,0:T(8,128)} %pad_maximum_fusion.1.c_ref.cu_ref.cd_ref, f32[5,6,128,128]{3,2,1,0:T(8,128)} %pad_maximum_fusion.1.c_ref.cu_ref.cd_ref, f32[5,6,128,128]{3,2,1,0:T(8,128)} %pad_maximum_fusion.1.c_ref.cu_ref.cd_ref, ...), custom_call_target="tpu_custom_call" | custom-call | tf_op jit(solution)/shard_map/pallas_call | solution.py:109
  104.2 4.1 %collective-permute-start.9 = (f32[5,1,128]{2,1,0:T(1,128)}, f32[5,1,128]{2,1,0:T(1,128)S(1)}, u32[]{:S(2)}, u32[]{:S(2)}) collective-permute-start(f32[5,1,128]{2,1,0:T(1,128)} %get-tuple-element.104), channel_id=1, source_target_pairs={{0,32},{32,64},{64,96},{96,128},{128,160},{160,192},{192,224},{224... | collective-permute-start | bytes 7688 | tf_op jit(solution)/shard_map/ppermute | solution.py:37
  108.3 5.4 %collective-permute-start.10 = (f32[5,4,1]{2,1,0:T(4,128)S(1)}, f32[5,4,1]{2,1,0:T(4,128)S(1)}, u32[]{:S(2)}, u32[]{:S(2)}) collective-permute-start(f32[5,4,1]{2,1,0:T(4,128)S(1)} %get-tuple-element.103), channel_id=1, source_target_pairs={{1,0},{2,1},{3,2},{4,3},{5,4},{6,5},{7,6},{8,7},{9,8},{10,9},{11,1... | collective-permute-start | bytes 248 | tf_op jit(solution)/shard_map/ppermute | solution.py:38
  117.5 1.6 %copy.706 = f32[5,4,127,1]{3,2,1,0:T(8,128)} copy(f32[5,4,127,1]{2,1,0,3:T(4,128)S(1)} %get-tuple-element.93) | data formatting | bytes 20320 | tf_op jit(solution)/shard_map/concatenate | solution.py:53
  121.1 11.1 %fusion.20 = (f32[5,4,128,1]{3,2,1,0:T(8,128)}, f32[5,4,128,1]{3,2,1,0:T(8,128)}) fusion(f32[5,1,128,1]{3,2,1,0:T(8,128)} %get-tuple-element.73, f32[5,3,128,1]{3,2,1,0:T(8,128)} %copy.712, f32[5,3,128,1]{3,2,1,0:T(8,128)} %copy.713, f32[5,1,128,1]{3,2,1,0:T(8,128)} %get-tuple-element.71, f32[5,4,1,1]{3,2,1,0:T(1,128)S(1)} %slice.572, ...), kind=kLoop, calls=%fused_computation.31 | loop fusion | flops 240640 | bytes 219436 | tf_op jit(solution)/shard_map/sub | solution.py:145
  135.5 6.7 %fusion.13 = f32[5,4,128,1]{3,2,1,0:T(8,128)} fusion(f32[5,4,128,1]{3,2,1,0:T(8,128)} %get-tuple-element.51, f32[5,1,128,1]{3,2,1,0:T(8,128)S(1)} %copy.698, f32[5,3,128,1]{3,2,1,0:T(8,128)} %copy.697, f32[5,3,128,1]{3,2,1,0:T(8,128)} %copy.700, f32[5,1,128,1]{3,2,1,0:T(8,128)S(1)} %copy.699, f32[5,4,1,1]{3,2,1,0:T(1,128)S(1)} %copy.703, ...), kind=kLoop, calls=%fused_computation.22 | loop fusion | flops 120320 | bytes 125228 | tf_op jit(solution)/shard_map/sub | solution.py:145
  142.2 4.4 %scatter.6 = f32[5,4,128,128]{3,2,1,0:T(8,128)} dynamic-update-slice(f32[5,4,128,128]{3,2,1,0:T(8,128)} %shard_map.92, f32[5,4,128,1]{3,2,1,0:T(8,128)} %fusion.13, s32[]{:T(128)} %constant.84.clone.1, s32[]{:T(128)} %constant.84.clone.1, s32[]{:T(128)} %constant.84.clone.1, s32[]{:T(128)} %constant.84.clone.1) | dynamic-update-slice | bytes 20484 | tf_op jit(solution)/shard_map/scatter | solution.py:227
  146.6 5.2 %scatter.9 = f32[5,4,128,128]{3,2,1,0:T(8,128)} dynamic-update-slice(f32[5,4,128,128]{3,2,1,0:T(8,128)} %scatter.6, f32[5,4,128,1]{3,2,1,0:T(8,128)S(1)} %copy-done.3, s32[]{:T(128)} %constant.84.clone.1, s32[]{:T(128)} %constant.84.clone.1, s32[]{:T(128)} %constant.84.clone.1, s32[]{:T(128)} %constant.93.clone.1) | dynamic-update-slice | bytes 20484 | tf_op jit(solution)/shard_map/scatter | solution.py:227
  (234 shorter events, 44.1 us)
Async XLA Ops:
  0.0 19.6 %copy-start = (f32[5,4,128,128]{3,2,1,0:T(8,128)S(1)}, f32[5,4,128,128]{3,2,1,0:T(8,128)}, u32[]{:S(2)}) copy-start(f32[5,4,128,128]{3,2,1,0:T(8,128)} %prev_ref.3) | copy-start | bytes 3932164
  0.0 13.1 %copy-start.22 = (f32[5,4,128]{2,1,0:T(4,128)S(1)}, f32[5,4,128]{2,1,0:T(4,128)}, u32[]{:S(2)}) copy-start(f32[5,4,128]{2,1,0:T(4,128)} %param.16) | copy-start | bytes 30724
  1.1 30.9 %collective-permute-start.2 = (f32[5,4,1,128]{3,2,1,0:T(1,128)S(1)}, f32[5,4,1,128]{3,2,1,0:T(1,128)S(1)}, u32[]{:S(2)}, u32[]{:S(2)}) collective-permute-start(f32[5,4,1,128]{3,2,1,0:T(1,128)S(1)} %get-tuple-element.61), channel_id=1, source_target_pairs={{1,0},{2,1},{3,2},{4,3},{5,4},{6,5},{7,6},{8,7},{9,8},{10,9},{11,1... | collective-permute-start | bytes 30728 | tf_op jit(solution)/shard_map/ppermute | solution.py:38
  9.1 25.7 %collective-permute-start.3 = (f32[5,4,1,128]{3,2,1,0:T(1,128)S(1)}, f32[5,4,1,128]{3,2,1,0:T(1,128)S(1)}, u32[]{:S(2)}, u32[]{:S(2)}) collective-permute-start(f32[5,4,1,128]{3,2,1,0:T(1,128)S(1)} %get-tuple-element.60), channel_id=1, source_target_pairs={{0,1},{1,2},{2,3},{3,4},{4,5},{5,6},{6,7},{7,8},{8,9},{9,10},{10,1... | collective-permute-start | bytes 30728 | tf_op jit(solution)/shard_map/ppermute | solution.py:37
  11.1 34.5 %collective-permute-start = (f32[5,1,128,128]{3,2,1,0:T(8,128)}, f32[5,1,128,128]{3,2,1,0:T(8,128)S(1)}, u32[]{:S(2)}, u32[]{:S(2)}) collective-permute-start(f32[5,1,128,128]{3,2,1,0:T(8,128)} %get-tuple-element.64), channel_id=1, source_target_pairs={{0,32},{32,64},{64,96},{96,128},{128,160},{160,192},{192,224},{224... | collective-permute-start | bytes 983048 | tf_op jit(solution)/shard_map/ppermute | solution.py:37
  11.7 34.0 %collective-permute-start.1 = (f32[5,1,128,128]{3,2,1,0:T(8,128)}, f32[5,1,128,128]{3,2,1,0:T(8,128)}, u32[]{:S(2)}, u32[]{:S(2)}) collective-permute-start(f32[5,1,128,128]{3,2,1,0:T(8,128)} %get-tuple-element.65), channel_id=1, source_target_pairs={{32,0},{64,32},{96,64},{128,96},{160,128},{192,160},{224,192},{0,2... | collective-permute-start | bytes 983048 | tf_op jit(solution)/shard_map/ppermute | solution.py:38
  13.7 23.1 %all-to-all-start = ((f32[8,5,4,128]{3,2,1,0:T(4,128)}), f32[8,5,4,128]{3,2,1,0:T(4,128)S(1)}, u32[]{:S(2)}, u32[]{:S(2)}) async-start(f32[8,5,4,128]{3,2,1,0:T(4,128)} %broadcast_in_dim.55), calls=%async_computation | async-start | bytes 163840 | tf_op jit(solution)/shard_map/all_to_all | solution.py:185
  39.4 63.4 %all-to-all-start.1 = ((f32[32,5,4,128]{3,2,1,0:T(4,128)}), f32[32,5,4,128]{3,2,1,0:T(4,128)S(1)}, u32[]{:S(2)}, u32[]{:S(2)}) async-start(f32[32,5,4,128]{3,2,1,0:T(4,128)} %copy.691), calls=%async_computation.1 | async-start | bytes 655360 | tf_op jit(solution)/shard_map/all_to_all | solution.py:206
  65.6 13.1 %copy-start.8 = (f32[5,1,128]{2,1,0:T(1,128)}, f32[5,1,128]{2,1,0:T(1,128)S(1)}, u32[]{:S(2)}) copy-start(f32[5,1,128]{2,1,0:T(1,128)S(1)} %squeeze.56) | copy-start | bytes 7684
  65.6 15.8 %collective-permute-start.6 = (f32[5,4,1,128]{3,2,1,0:T(1,128)}, f32[5,4,1,128]{3,2,1,0:T(1,128)}, u32[]{:S(2)}, u32[]{:S(2)}) collective-permute-start(f32[5,4,1,128]{3,2,1,0:T(1,128)} %get-tuple-element.55), channel_id=1, source_target_pairs={{1,0},{2,1},{3,2},{4,3},{5,4},{6,5},{7,6},{8,7},{9,8},{10,9},{11,1... | collective-permute-start | bytes 30728 | tf_op jit(solution)/shard_map/ppermute | solution.py:38
  71.4 11.0 %collective-permute-start.7 = (f32[5,4,1,128]{3,2,1,0:T(1,128)S(1)}, f32[5,4,1,128]{3,2,1,0:T(1,128)}, u32[]{:S(2)}, u32[]{:S(2)}) collective-permute-start(f32[5,4,1,128]{3,2,1,0:T(1,128)S(1)} %get-tuple-element.54), channel_id=1, source_target_pairs={{0,1},{1,2},{2,3},{3,4},{4,5},{5,6},{6,7},{7,8},{8,9},{9,10},{10,1... | collective-permute-start | bytes 30728 | tf_op jit(solution)/shard_map/ppermute | solution.py:37
  71.4 16.5 %collective-permute-start.5 = (f32[5,1,128,128]{3,2,1,0:T(8,128)}, f32[5,1,128,128]{3,2,1,0:T(8,128)S(1)}, u32[]{:S(2)}, u32[]{:S(2)}) collective-permute-start(f32[5,1,128,128]{3,2,1,0:T(8,128)} %get-tuple-element.59), channel_id=1, source_target_pairs={{32,0},{64,32},{96,64},{128,96},{160,128},{192,160},{224,192},{0,2... | collective-permute-start | bytes 983048 | tf_op jit(solution)/shard_map/ppermute | solution.py:38
  72.3 16.6 %collective-permute-start.4 = (f32[5,1,128,128]{3,2,1,0:T(8,128)}, f32[5,1,128,128]{3,2,1,0:T(8,128)}, u32[]{:S(2)}, u32[]{:S(2)}) collective-permute-start(f32[5,1,128,128]{3,2,1,0:T(8,128)} %get-tuple-element.58), channel_id=1, source_target_pairs={{0,32},{32,64},{64,96},{96,128},{128,160},{160,192},{192,224},{224... | collective-permute-start | bytes 983048 | tf_op jit(solution)/shard_map/ppermute | solution.py:37
  93.2 9.8 %copy-start.12 = (f32[4,128]{1,0:T(4,128)S(1)}, f32[4,128]{1,0:T(4,128)}, u32[]{:S(2)}) copy-start(f32[4,128]{1,0:T(4,128)} %get-tuple-element.144) | copy-start | bytes 6148
  93.2 9.8 %copy-start.13 = (f32[4,128]{1,0:T(4,128)S(1)}, f32[4,128]{1,0:T(4,128)}, u32[]{:S(2)}) copy-start(f32[4,128]{1,0:T(4,128)} %get-tuple-element.145) | copy-start | bytes 6148
  93.2 9.8 %copy-start.14 = (f32[4,128]{1,0:T(4,128)S(1)}, f32[4,128]{1,0:T(4,128)}, u32[]{:S(2)}) copy-start(f32[4,128]{1,0:T(4,128)} %get-tuple-element.146) | copy-start | bytes 6148
  93.3 9.8 %copy-start.15 = (f32[4,128]{1,0:T(4,128)S(1)}, f32[4,128]{1,0:T(4,128)}, u32[]{:S(2)}) copy-start(f32[4,128]{1,0:T(4,128)} %get-tuple-element.137) | copy-start | bytes 6148
  93.3 9.8 %copy-start.16 = (f32[4,128]{1,0:T(4,128)S(1)}, f32[4,128]{1,0:T(4,128)}, u32[]{:S(2)}) copy-start(f32[4,128]{1,0:T(4,128)} %get-tuple-element.138) | copy-start | bytes 6148
  93.3 9.8 %copy-start.17 = (f32[4,128]{1,0:T(4,128)S(1)}, f32[4,128]{1,0:T(4,128)}, u32[]{:S(2)}) copy-start(f32[4,128]{1,0:T(4,128)} %get-tuple-element.139) | copy-start | bytes 6148
  93.3 9.8 %copy-start.18 = (f32[4,128]{1,0:T(4,128)S(1)}, f32[4,128]{1,0:T(4,128)}, u32[]{:S(2)}) copy-start(f32[4,128]{1,0:T(4,128)} %get-tuple-element.140) | copy-start | bytes 6148
  104.2 30.8 %collective-permute-start.8 = (f32[5,1,128]{2,1,0:T(1,128)}, f32[5,1,128]{2,1,0:T(1,128)S(1)}, u32[]{:S(2)}, u32[]{:S(2)}) collective-permute-start(f32[5,1,128]{2,1,0:T(1,128)} %get-tuple-element.105), channel_id=1, source_target_pairs={{32,0},{64,32},{96,64},{128,96},{160,128},{192,160},{224,192},{0,2... | collective-permute-start | bytes 7688 | tf_op jit(solution)/shard_map/ppermute | solution.py:38
  104.2 30.8 %collective-permute-start.9 = (f32[5,1,128]{2,1,0:T(1,128)}, f32[5,1,128]{2,1,0:T(1,128)S(1)}, u32[]{:S(2)}, u32[]{:S(2)}) collective-permute-start(f32[5,1,128]{2,1,0:T(1,128)} %get-tuple-element.104), channel_id=1, source_target_pairs={{0,32},{32,64},{64,96},{96,128},{128,160},{160,192},{192,224},{224... | collective-permute-start | bytes 7688 | tf_op jit(solution)/shard_map/ppermute | solution.py:37
  108.3 25.4 %collective-permute-start.11 = (f32[5,4,1]{2,1,0:T(4,128)S(1)}, f32[5,4,1]{2,1,0:T(4,128)}, u32[]{:S(2)}, u32[]{:S(2)}) collective-permute-start(f32[5,4,1]{2,1,0:T(4,128)S(1)} %get-tuple-element.102), channel_id=1, source_target_pairs={{0,1},{1,2},{2,3},{3,4},{4,5},{5,6},{6,7},{7,8},{8,9},{9,10},{10,1... | collective-permute-start | bytes 248 | tf_op jit(solution)/shard_map/ppermute | solution.py:37
  108.3 26.1 %collective-permute-start.10 = (f32[5,4,1]{2,1,0:T(4,128)S(1)}, f32[5,4,1]{2,1,0:T(4,128)S(1)}, u32[]{:S(2)}, u32[]{:S(2)}) collective-permute-start(f32[5,4,1]{2,1,0:T(4,128)S(1)} %get-tuple-element.103), channel_id=1, source_target_pairs={{1,0},{2,1},{3,2},{4,3},{5,4},{6,5},{7,6},{8,7},{9,8},{10,9},{11,1... | collective-permute-start | bytes 248 | tf_op jit(solution)/shard_map/ppermute | solution.py:38
  (50 other events, 288.1 us)

commit v2 on v1

--- a/solution.py
+++ b/solution.py
@@ -54,7 +54,7 @@
     )
 
 
-def stencil_kernel(j_ref, c_ref, cu_ref, cd_ref, su_ref, sd_ref, prev_ref, rate_ref, out_ref):
+def stencil_kernel(j_ref, c_ref, cu_ref, cd_ref, su_ref, sd_ref, prev_ref, rate_ref, inlet_ref, out_ref):
     lane = lax.broadcasted_iota(jnp.int32, (8, 128), 1)
     probe = pltpu.roll(lane, 1, 1)
     numpy_order = probe == (lane + 127) % 128
@@ -72,7 +72,7 @@
             other = pltpu.roll(cur[g], 127, 1)
             down = jnp.where(numpy_order, one, other)
             up = jnp.where(numpy_order, other, one)
-            ad.append(jnp.where(lane == 0, 0.0, down))
+            ad.append(jnp.where(lane == 0, inlet_ref[g, 0, rows, :], down))
             au.append(jnp.where(lane == 127, 0.0, up))
         dc = [cu[g] - cd[g] for g in range(NF)]
         ds = [su[g] - sd[g] for g in range(NF)]
@@ -97,7 +97,7 @@
     lax.fori_loop(0, c_ref.shape[2] // 8, chunk, 0)
 
 
-def bulk_sweep(current, previous, rate_cells, jacobians):
+def sweep(current, previous, rate_cells, inlet_column, jacobians):
     parts = halo_parts(current)
     circ_low, circ_high, span_low, span_high = parts
     padded = jnp.concatenate([circ_low, current, circ_high], axis=1)
@@ -118,10 +118,11 @@
             spec(0),
             spec(0),
             pl.BlockSpec((1, span, axial), lambda t: (t, 0, 0)),
+            pl.BlockSpec((nf, 1, span, 1), lambda t: (0, t, 0, 0)),
         ],
         out_specs=spec(0),
         out_shape=jax.ShapeDtypeStruct(current.shape, current.dtype),
-    )(jacobians.reshape(-1), padded, padded, padded, span_up, span_down, previous, rate_cells)
+    )(jacobians.reshape(-1), padded, padded, padded, span_up, span_down, previous, rate_cells, inlet_column)
     return out, parts
 
 
@@ -206,25 +207,10 @@
     received = lax.all_to_all(contributions, "span", 0, 0, tiled=True)
     inlet_plane = jnp.sum(received, axis=0)
 
-    mid_bulk, old_parts = bulk_sweep(q_old, q_old, pseudo_rate, flux_jacobians)
-    new_bulk, mid_parts = bulk_sweep(mid_bulk, q_old, pseudo_rate, flux_jacobians)
-
-    old_first, old_second = q_old[..., 0], q_old[..., 1]
-    rate_first, rate_second = pseudo_rate[..., 0], pseudo_rate[..., 1]
-    mid_second, mid_third = mid_bulk[..., 1], mid_bulk[..., 2]
-    old_lateral = lateral_of(old_first, [p[..., 0] for p in old_parts])
-    mid_first = update(
-        old_first, old_first, rate_first, old_lateral + (old_second, inlet_plane), flux_jacobians
-    )
-    first_lateral = lateral_of(mid_first, halo_parts(mid_first))
-    new_first = update(
-        mid_first, old_first, rate_first, first_lateral + (mid_second, inlet_plane), flux_jacobians
-    )
-    second_lateral = lateral_of(mid_second, [p[..., 1] for p in mid_parts])
-    new_second = update(
-        mid_second, old_second, rate_second, second_lateral + (mid_third, mid_first), flux_jacobians
-    )
-    return new_bulk.at[..., 0].set(new_first).at[..., 1].set(new_second)
+    inlet_column = inlet_plane[..., None]
+    mid, _ = sweep(q_old, q_old, pseudo_rate, inlet_column, flux_jacobians)
+    new, _ = sweep(mid, q_old, pseudo_rate, inlet_column, flux_jacobians)
+    return new
 
 
 def solution(mesh):

time: 153 us -> 90.4 us (0.59)
  the two profiles are of different devices: /device:TPU:6 before, /device:TPU:1 now
where the time goes in v2:
time: 90.4 us; the launch traced here: 89.9 us
  starting transfers between devices  28.8 us (32%)
  Pallas kernels  18.1 us (20%)
  waiting for transfers between devices  16.7 us (18%)
  local copies, waits for them, and re-layouts  13 us (14%)
  other arithmetic  10.8 us (12%)
  matrix products  2.32 us (3%)
    pallas_call x2, Pallas kernels, sweep(): pl.pallas_call(stencil_kernel, grid=(rows,), in_specs=[pl.BlockSpec(memor...  18.1 us
    all_to_all x1, starting transfers between devices, body(): received = lax.all_to_all(contributions, 'span', 0, 0, tiled=True)  12.5 us
    ppermute x4, starting transfers between devices, halo_parts(): high = lax.ppermute(lax.slice_in_dim(block, 0, 1, axis=dim), axis, backward)  8.96 us
    all_to_all x1, waiting for transfers between devices, body(): received = lax.all_to_all(contributions, 'span', 0, 0, tiled=True)  8.19 us
    concatenate x2, other arithmetic, sweep(): padded = jnp.concatenate([circ_low, current, circ_high], axis=1)  4.11 us
    ppermute x4, starting transfers between devices, halo_parts(): lax.ppermute(lax.slice_in_dim(block, block.shape[dim] - 1, None, axis=dim...  3.92 us
    slice x4, local copies, waits for them, and re-layouts, halo_parts(): lax.slice_in_dim(block, block.shape[dim] - 1, None, axis=dim)  3.9 us
    concatenate x2, other arithmetic, sweep(): span_up = jnp.concatenate([current[:, :, 1:], span_high], axis=2)  3.69 us
  transfers between devices with their start and end apart: 10, of which 4 were waited for; matrix products, arithmetic and copies ran while one was open for 21% of the time, Pallas kernels for 0%

profile of v2, /device:TPU:1, one launch (start us, length us, event | category | flops | bytes accessed | tf_op | source)
XLA Modules:
  0.0 89.9 jit_solution(15988956568741714766)
XLA Ops:
  1.1 3.3 %collective-permute-start.2 = (f32[5,4,1,128]{3,2,1,0:T(1,128)S(1)}, f32[5,4,1,128]{3,2,1,0:T(1,128)S(1)}, u32[]{:S(2)}, u32[]{:S(2)}) collective-permute-start(f32[5,4,1,128]{3,2,1,0:T(1,128)S(1)} %get-tuple-element.12), channel_id=1, source_target_pairs={{1,0},{2,1},{3,2},{4,3},{5,4},{6,5},{7,6},{8,7},{9,8},{10,9},{11,1... | collective-permute-start | bytes 30728 | tf_op jit(solution)/shard_map/ppermute | solution.py:38
  4.3 1.8 %fusion.8 = (f32[5,1,128,128]{3,2,1,0:T(8,128)}, f32[5,1,128,128]{3,2,1,0:T(8,128)S(1)}) fusion(f32[5,4,128,128]{3,2,1,0:T(8,128)} %prev_ref.3), kind=kLoop, calls=%fused_computation.32 | loop fusion | bytes 1310720 | tf_op jit(solution)/shard_map/slice | solution.py:37
  7.3 2.5 %collective-permute-start.1 = (f32[5,1,128,128]{3,2,1,0:T(8,128)S(1)}, f32[5,1,128,128]{3,2,1,0:T(8,128)}, u32[]{:S(2)}, u32[]{:S(2)}) collective-permute-start(f32[5,1,128,128]{3,2,1,0:T(8,128)S(1)} %get-tuple-element.16), channel_id=1, source_target_pairs={{32,0},{64,32},{96,64},{128,96},{160,128},{192,160},{224,192},{0,2... | collective-permute-start | bytes 983048 | tf_op jit(solution)/shard_map/ppermute | solution.py:38
  10.4 3.4 %all-to-all-start = ((f32[8,5,4,128]{3,2,1,0:T(4,128)}), f32[8,5,4,128]{3,2,1,0:T(4,128)S(1)}, u32[]{:S(2)}, u32[]{:S(2)}) async-start(f32[8,5,4,128]{3,2,1,0:T(4,128)} %broadcast_in_dim.58), calls=%async_computation | async-start | bytes 163840 | tf_op jit(solution)/shard_map/all_to_all | solution.py:186
  13.9 1.3 %fusion.7 = (f32[5,4,127,128]{3,2,1,0:T(8,128)S(1)}, f32[5,4,127,128]{3,2,1,0:T(8,128)}) fusion(f32[5,4,128,128]{3,2,1,0:T(8,128)S(1)} %copy-done), kind=kLoop, calls=%fused_computation.31 | loop fusion | bytes 5201920 | tf_op jit(solution)/shard_map/slice | solution.py:105
  16.5 2.9 %all-to-all-done = f32[8,5,4,128]{3,2,1,0:T(4,128)S(1)} async-done(((f32[8,5,4,128]{3,2,1,0:T(4,128)}), f32[8,5,4,128]{3,2,1,0:T(4,128)S(1)}, u32[]{:S(2)}, u32[]{:S(2)}) %all-to-all-start) | async-done | bytes 81952 | tf_op jit(solution)/shard_map/all_to_all | solution.py:186
  19.6 2.3 %fusion = f32[5,4,32,32,4]{3,2,4,1,0:T(8,128)} fusion(f32[32,4,4,1,1]{0,2,1,4,3:T(4,128)S(1)} %copy.32, f32[5,4,4,32,1]{3,2,1,0,4:T(4,128)S(1)} %reshape.99), kind=kOutput, calls=%fused_computation.7 | convolution fusion | flops 3932160 | bytes 339968 | tf_op jit(solution)/shard_map/ogk,ftkp->oftgp/dot_general | solution.py:204
  21.9 2.4 %copy.28 = f32[32,5,4,128]{3,2,1,0:T(4,128)} copy(f32[32,5,4,128]{0,3,2,1:T(8,128)} %bitcast.14) | data formatting | bytes 655360 | tf_op jit(solution)/shard_map/reshape | solution.py:206
  24.4 12.5 %all-to-all-start.1 = ((f32[32,5,4,128]{3,2,1,0:T(4,128)}), f32[32,5,4,128]{3,2,1,0:T(4,128)S(1)}, u32[]{:S(2)}, u32[]{:S(2)}) async-start(f32[32,5,4,128]{3,2,1,0:T(4,128)} %copy.28), calls=%async_computation.1 | async-start | bytes 655360 | tf_op jit(solution)/shard_map/all_to_all | solution.py:207
  36.9 2.5 %pad_maximum_fusion.2.su_ref = f32[5,4,128,128]{3,2,1,0:T(8,128)} fusion(f32[5,4,1,128]{3,2,1,0:T(1,128)S(1)} %broadcast_multiply_fusion.3, f32[5,4,127,128]{3,2,1,0:T(8,128)} %get-tuple-element.14), kind=kLoop, calls=%fused_computation.2 | loop fusion | flops 327680 | bytes 2621440 | tf_op jit(solution)/shard_map/concatenate | solution.py:104
  39.5 1.2 %pad_maximum_fusion.3.sd_ref = f32[5,4,128,128]{3,2,1,0:T(8,128)} fusion(f32[5,4,127,128]{3,2,1,0:T(8,128)S(1)} %get-tuple-element.13, f32[5,4,1,128]{3,2,1,0:T(1,128)S(1)} %broadcast_multiply_fusion.1), kind=kLoop, calls=%fused_computation.3 | loop fusion | flops 327680 | bytes 2621440 | tf_op jit(solution)/shard_map/concatenate | solution.py:105
  40.6 2.6 %pad_maximum_fusion.c_ref.cu_ref.cd_ref = f32[5,6,128,128]{3,2,1,0:T(8,128)} fusion(f32[5,1,128,128]{3,2,1,0:T(8,128)} %collective-permute-done.1, f32[5,4,128,128]{3,2,1,0:T(8,128)S(1)} %copy-done, f32[5,1,128,128]{3,2,1,0:T(8,128)} %collective-permute-done), kind=kLoop, calls=%fused_computation | loop fusion | flops 983040 | bytes 3932160 | tf_op jit(solution)/shard_map/concatenate | solution.py:103
  43.2 8.2 %all-to-all-done.1 = f32[32,5,4,128]{3,2,1,0:T(4,128)S(1)} async-done(((f32[32,5,4,128]{3,2,1,0:T(4,128)}), f32[32,5,4,128]{3,2,1,0:T(4,128)S(1)}, u32[]{:S(2)}, u32[]{:S(2)}) %all-to-all-start.1) | async-done | bytes 327712 | tf_op jit(solution)/shard_map/all_to_all | solution.py:207
  51.5 1.5 %copy.29.inlet_ref = f32[5,4,128,1]{3,2,1,0:T(8,128)} copy(f32[5,4,128,1]{2,1,0,3:T(4,128)S(1)} %bitcast.16) | data formatting | bytes 20480 | tf_op jit(solution)/shard_map/broadcast_in_dim | solution.py:210
  53.0 9.0 %shard_map.91 = f32[5,4,128,128]{3,2,1,0:T(8,128)} custom-call(f32[75]{0:T(128)} %reshape.95.j_ref, f32[5,6,128,128]{3,2,1,0:T(8,128)} %pad_maximum_fusion.c_ref.cu_ref.cd_ref, f32[5,6,128,128]{3,2,1,0:T(8,128)} %pad_maximum_fusion.c_ref.cu_ref.cd_ref, f32[5,6,128,128]{3,2,1,0:T(8,128)} %pad_maximum_fusion.c_ref.cu_ref.cd_ref, ...), custom_call_target="tpu_custom_call" | custom-call | tf_op jit(solution)/shard_map/pallas_call | solution.py:109
  63.0 2.2 %fusion.4 = (f32[5,4,127,128]{3,2,1,0:T(8,128)S(1)}, f32[5,4,127,128]{3,2,1,0:T(8,128)S(1)}) fusion(f32[5,4,128,128]{3,2,1,0:T(8,128)} %shard_map.91), kind=kLoop, calls=%fused_computation.28 | loop fusion | bytes 5201920 | tf_op jit(solution)/shard_map/slice | solution.py:105
  65.2 2.2 %collective-permute-start.7 = (f32[5,4,1,128]{3,2,1,0:T(1,128)S(1)}, f32[5,4,1,128]{3,2,1,0:T(1,128)S(1)}, u32[]{:S(2)}, u32[]{:S(2)}) collective-permute-start(f32[5,4,1,128]{3,2,1,0:T(1,128)S(1)} %get-tuple-element.5), channel_id=1, source_target_pairs={{0,1},{1,2},{2,3},{3,4},{4,5},{5,6},{6,7},{7,8},{8,9},{9,10},{10,1... | collective-permute-start | bytes 30728 | tf_op jit(solution)/shard_map/ppermute | solution.py:37
  68.1 3.1 %collective-permute-start.5 = (f32[5,1,128,128]{3,2,1,0:T(8,128)S(1)}, f32[5,1,128,128]{3,2,1,0:T(8,128)S(1)}, u32[]{:S(2)}, u32[]{:S(2)}) collective-permute-start(f32[5,1,128,128]{3,2,1,0:T(8,128)S(1)} %get-tuple-element.10), channel_id=1, source_target_pairs={{32,0},{64,32},{96,64},{128,96},{160,128},{192,160},{224,192},{0,2... | collective-permute-start | bytes 983048 | tf_op jit(solution)/shard_map/ppermute | solution.py:38
  71.3 3.2 %collective-permute-done.6 = f32[5,4,1,128]{3,2,1,0:T(1,128)S(1)} collective-permute-done((f32[5,4,1,128]{3,2,1,0:T(1,128)S(1)}, f32[5,4,1,128]{3,2,1,0:T(1,128)S(1)}, u32[]{:S(2)}, u32[]{:S(2)}) %collective-permute-start.6) | collective-permute-done | bytes 10272 | tf_op jit(solution)/shard_map/ppermute | solution.py:38
  74.6 1.2 %pad_maximum_fusion.5.sd_ref = f32[5,4,128,128]{3,2,1,0:T(8,128)} fusion(f32[5,4,127,128]{3,2,1,0:T(8,128)S(1)} %get-tuple-element.7, f32[5,4,1,128]{3,2,1,0:T(1,128)S(1)} %broadcast_multiply_fusion), kind=kLoop, calls=%fused_computation.5 | loop fusion | flops 327680 | bytes 2621440 | tf_op jit(solution)/shard_map/concatenate | solution.py:105
  75.8 1.2 %pad_maximum_fusion.4.su_ref = f32[5,4,128,128]{3,2,1,0:T(8,128)} fusion(f32[5,4,1,128]{3,2,1,0:T(1,128)S(1)} %broadcast_multiply_fusion.2, f32[5,4,127,128]{3,2,1,0:T(8,128)S(1)} %get-tuple-element.8), kind=kLoop, calls=%fused_computation.4 | loop fusion | flops 327680 | bytes 2621440 | tf_op jit(solution)/shard_map/concatenate | solution.py:104
  77.0 2.4 %collective-permute-done.4 = f32[5,1,128,128]{3,2,1,0:T(8,128)S(1)} collective-permute-done((f32[5,1,128,128]{3,2,1,0:T(8,128)S(1)}, f32[5,1,128,128]{3,2,1,0:T(8,128)S(1)}, u32[]{:S(2)}, u32[]{:S(2)}) %collective-permute-start.4) | collective-permute-done | bytes 327712 | tf_op jit(solution)/shard_map/ppermute | solution.py:37
  79.4 1.5 %pad_maximum_fusion.1.c_ref.cu_ref.cd_ref = f32[5,6,128,128]{3,2,1,0:T(8,128)} fusion(f32[5,1,128,128]{3,2,1,0:T(8,128)S(1)} %collective-permute-done.5, f32[5,4,128,128]{3,2,1,0:T(8,128)S(1)} %copy-done.1, f32[5,1,128,128]{3,2,1,0:T(8,128)S(1)} %collective-permute-done.4), kind=kLoop, calls=%fused_computation.1 | loop fusion | flops 983040 | bytes 3932160 | tf_op jit(solution)/shard_map/concatenate | solution.py:103
  80.9 9.0 %shard_map.92 = f32[5,4,128,128]{3,2,1,0:T(8,128)} custom-call(f32[75]{0:T(128)} %reshape.95.j_ref, f32[5,6,128,128]{3,2,1,0:T(8,128)} %pad_maximum_fusion.1.c_ref.cu_ref.cd_ref, f32[5,6,128,128]{3,2,1,0:T(8,128)} %pad_maximum_fusion.1.c_ref.cu_ref.cd_ref, f32[5,6,128,128]{3,2,1,0:T(8,128)} %pad_maximum_fusion.1.c_ref.cu_ref.cd_ref, ...), custom_call_target="tpu_custom_call" | custom-call | tf_op jit(solution)/shard_map/pallas_call | solution.py:109
  (51 shorter events, 6.1 us)
Async XLA Ops:
  0.0 13.8 %copy-start = (f32[5,4,128,128]{3,2,1,0:T(8,128)S(1)}, f32[5,4,128,128]{3,2,1,0:T(8,128)}, u32[]{:S(2)}) copy-start(f32[5,4,128,128]{3,2,1,0:T(8,128)} %prev_ref.3) | copy-start | bytes 3932164
  0.0 9.8 %copy-start.3 = (f32[5,4,128]{2,1,0:T(4,128)S(1)}, f32[5,4,128]{2,1,0:T(4,128)}, u32[]{:S(2)}) copy-start(f32[5,4,128]{2,1,0:T(4,128)} %param.12) | copy-start | bytes 30724
  1.1 15.4 %collective-permute-start.2 = (f32[5,4,1,128]{3,2,1,0:T(1,128)S(1)}, f32[5,4,1,128]{3,2,1,0:T(1,128)S(1)}, u32[]{:S(2)}, u32[]{:S(2)}) collective-permute-start(f32[5,4,1,128]{3,2,1,0:T(1,128)S(1)} %get-tuple-element.12), channel_id=1, source_target_pairs={{1,0},{2,1},{3,2},{4,3},{5,4},{6,5},{7,6},{8,7},{9,8},{10,9},{11,1... | collective-permute-start | bytes 30728 | tf_op jit(solution)/shard_map/ppermute | solution.py:38
  4.3 32.6 %collective-permute-start.3 = (f32[5,4,1,128]{3,2,1,0:T(1,128)S(1)}, f32[5,4,1,128]{3,2,1,0:T(1,128)S(1)}, u32[]{:S(2)}, u32[]{:S(2)}) collective-permute-start(f32[5,4,1,128]{3,2,1,0:T(1,128)S(1)} %get-tuple-element.11), channel_id=1, source_target_pairs={{0,1},{1,2},{2,3},{3,4},{4,5},{5,6},{6,7},{7,8},{8,9},{9,10},{10,1... | collective-permute-start | bytes 30728 | tf_op jit(solution)/shard_map/ppermute | solution.py:37
  6.2 34.4 %collective-permute-start = (f32[5,1,128,128]{3,2,1,0:T(8,128)}, f32[5,1,128,128]{3,2,1,0:T(8,128)}, u32[]{:S(2)}, u32[]{:S(2)}) collective-permute-start(f32[5,1,128,128]{3,2,1,0:T(8,128)} %get-tuple-element.15), channel_id=1, source_target_pairs={{0,32},{32,64},{64,96},{96,128},{128,160},{160,192},{192,224},{224... | collective-permute-start | bytes 983048 | tf_op jit(solution)/shard_map/ppermute | solution.py:37
  7.3 33.3 %collective-permute-start.1 = (f32[5,1,128,128]{3,2,1,0:T(8,128)S(1)}, f32[5,1,128,128]{3,2,1,0:T(8,128)}, u32[]{:S(2)}, u32[]{:S(2)}) collective-permute-start(f32[5,1,128,128]{3,2,1,0:T(8,128)S(1)} %get-tuple-element.16), channel_id=1, source_target_pairs={{32,0},{64,32},{96,64},{128,96},{160,128},{192,160},{224,192},{0,2... | collective-permute-start | bytes 983048 | tf_op jit(solution)/shard_map/ppermute | solution.py:38
  10.4 9.0 %all-to-all-start = ((f32[8,5,4,128]{3,2,1,0:T(4,128)}), f32[8,5,4,128]{3,2,1,0:T(4,128)S(1)}, u32[]{:S(2)}, u32[]{:S(2)}) async-start(f32[8,5,4,128]{3,2,1,0:T(4,128)} %broadcast_in_dim.58), calls=%async_computation | async-start | bytes 163840 | tf_op jit(solution)/shard_map/all_to_all | solution.py:186
  13.8 1.4 %copy-start.8 = (s32[128]{0:T(128)S(1)}, s32[128]{0:T(128)}, u32[]{:S(2)}) copy-start(s32[128]{0:T(128)} %param.13) | copy-start | bytes 1540
  13.8 1.6 %copy-start.4 = (s32[1,4,4]{2,1,0:T(4,128)S(1)}, s32[1,4,4]{2,1,0:T(4,128)}, u32[]{:S(2)}) copy-start(s32[1,4,4]{2,1,0:T(4,128)} %param.15) | copy-start | bytes 196
  13.8 1.6 %copy-start.5 = (s32[1,4,4]{2,1,0:T(4,128)S(1)}, s32[1,4,4]{2,1,0:T(4,128)}, u32[]{:S(2)}) copy-start(s32[1,4,4]{2,1,0:T(4,128)} %param.14) | copy-start | bytes 196
  13.8 1.6 %copy-start.6 = (s32[1,4,4]{2,1,0:T(4,128)S(1)}, s32[1,4,4]{2,1,0:T(4,128)}, u32[]{:S(2)}) copy-start(s32[1,4,4]{2,1,0:T(4,128)} %param.16) | copy-start | bytes 196
  13.8 1.6 %copy-start.7 = (f32[16]{0:T(128)S(1)}, f32[16]{0:T(128)}, u32[]{:S(2)}) copy-start(f32[16]{0:T(128)} %param.17) | copy-start | bytes 196
  13.9 2.0 %copy-start.2 = (f32[3,5,5]{2,0,1:T(4,128)S(1)}, f32[3,5,5]{2,0,1:T(4,128)}, u32[]{:S(2)}) copy-start(f32[3,5,5]{2,0,1:T(4,128)} %param.11) | copy-start | bytes 904
  24.4 27.0 %all-to-all-start.1 = ((f32[32,5,4,128]{3,2,1,0:T(4,128)}), f32[32,5,4,128]{3,2,1,0:T(4,128)S(1)}, u32[]{:S(2)}, u32[]{:S(2)}) async-start(f32[32,5,4,128]{3,2,1,0:T(4,128)} %copy.28), calls=%async_computation.1 | async-start | bytes 655360 | tf_op jit(solution)/shard_map/all_to_all | solution.py:207
  63.0 4.5 %copy-start.1 = (f32[5,4,128,128]{3,2,1,0:T(8,128)S(1)}, f32[5,4,128,128]{3,2,1,0:T(8,128)}, u32[]{:S(2)}) copy-start(f32[5,4,128,128]{3,2,1,0:T(8,128)} %shard_map.91) | copy-start | bytes 3932164
  65.2 6.1 %collective-permute-start.7 = (f32[5,4,1,128]{3,2,1,0:T(1,128)S(1)}, f32[5,4,1,128]{3,2,1,0:T(1,128)S(1)}, u32[]{:S(2)}, u32[]{:S(2)}) collective-permute-start(f32[5,4,1,128]{3,2,1,0:T(1,128)S(1)} %get-tuple-element.5), channel_id=1, source_target_pairs={{0,1},{1,2},{2,3},{3,4},{4,5},{5,6},{6,7},{7,8},{8,9},{9,10},{10,1... | collective-permute-start | bytes 30728 | tf_op jit(solution)/shard_map/ppermute | solution.py:37
  67.5 11.9 %collective-permute-start.4 = (f32[5,1,128,128]{3,2,1,0:T(8,128)S(1)}, f32[5,1,128,128]{3,2,1,0:T(8,128)S(1)}, u32[]{:S(2)}, u32[]{:S(2)}) collective-permute-start(f32[5,1,128,128]{3,2,1,0:T(8,128)S(1)} %get-tuple-element.9), channel_id=1, source_target_pairs={{0,32},{32,64},{64,96},{96,128},{128,160},{160,192},{192,224},{224... | collective-permute-start | bytes 983048 | tf_op jit(solution)/shard_map/ppermute | solution.py:37
  68.1 11.3 %collective-permute-start.5 = (f32[5,1,128,128]{3,2,1,0:T(8,128)S(1)}, f32[5,1,128,128]{3,2,1,0:T(8,128)S(1)}, u32[]{:S(2)}, u32[]{:S(2)}) collective-permute-start(f32[5,1,128,128]{3,2,1,0:T(8,128)S(1)} %get-tuple-element.10), channel_id=1, source_target_pairs={{32,0},{64,32},{96,64},{128,96},{160,128},{192,160},{224,192},{0,2... | collective-permute-start | bytes 983048 | tf_op jit(solution)/shard_map/ppermute | solution.py:38
  71.1 3.4 %collective-permute-start.6 = (f32[5,4,1,128]{3,2,1,0:T(1,128)S(1)}, f32[5,4,1,128]{3,2,1,0:T(1,128)S(1)}, u32[]{:S(2)}, u32[]{:S(2)}) collective-permute-start(f32[5,4,1,128]{3,2,1,0:T(1,128)S(1)} %get-tuple-element.6), channel_id=1, source_target_pairs={{1,0},{2,1},{3,2},{4,3},{5,4},{6,5},{7,6},{8,7},{9,8},{10,9},{11,1... | collective-permute-start | bytes 30728 | tf_op jit(solution)/shard_map/ppermute | solution.py:38

commit v3 on v2

--- a/solution.py
+++ b/solution.py
@@ -97,8 +97,9 @@
     lax.fori_loop(0, c_ref.shape[2] // 8, chunk, 0)
 
 
-def sweep(current, previous, rate_cells, inlet_column, jacobians):
-    parts = halo_parts(current)
+def sweep(current, previous, rate_cells, inlet_column, jacobians, parts=None):
+    if parts is None:
+        parts = halo_parts(current)
     circ_low, circ_high, span_low, span_high = parts
     padded = jnp.concatenate([circ_low, current, circ_high], axis=1)
     span_up = jnp.concatenate([current[:, :, 1:], span_high], axis=2)
@@ -208,8 +209,18 @@
     inlet_plane = jnp.sum(received, axis=0)
 
     inlet_column = inlet_plane[..., None]
-    mid, _ = sweep(q_old, q_old, pseudo_rate, inlet_column, flux_jacobians)
-    new, _ = sweep(mid, q_old, pseudo_rate, inlet_column, flux_jacobians)
+    mid_bulk, _ = sweep(q_old, q_old, pseudo_rate, jnp.zeros_like(inlet_column), flux_jacobians)
+    bulk_parts = halo_parts(mid_bulk)
+    correction = pseudo_rate[None, :, :, :1] * (
+        0.5 * contract(flux_jacobians[2], inlet_column) + viscosity * inlet_column
+    )
+    at_inlet = lax.broadcasted_iota(jnp.int32, q_old.shape, 3) == 0
+    mid = jnp.where(at_inlet, mid_bulk + correction, mid_bulk)
+    mid_parts = [
+        jnp.where(lax.broadcasted_iota(jnp.int32, bulk.shape, 3) == 0, bulk + extra, bulk)
+        for bulk, extra in zip(bulk_parts, halo_parts(correction))
+    ]
+    new, _ = sweep(mid, q_old, pseudo_rate, inlet_column, flux_jacobians, mid_parts)
     return new
 
 

time: 90.4 us -> 100 us (1.11)
  the two profiles are of different devices: /device:TPU:1 before, /device:TPU:24 now
where the time goes in v3:
time: 100 us; the launch traced here: 99.7 us
  starting transfers between devices  39.6 us (40%)
  other arithmetic  20.2 us (20%)
  Pallas kernels  18.1 us (18%)
  local copies, waits for them, and re-layouts  15.6 us (16%)
  waiting for transfers between devices  4.67 us (5%)
  matrix products  1.25 us (1%)
    ppermute x6, starting transfers between devices, halo_parts(): high = lax.ppermute(lax.slice_in_dim(block, 0, 1, axis=dim), axis, backward)  22.6 us
    pallas_call x2, Pallas kernels, sweep(): pl.pallas_call(stencil_kernel, grid=(rows,), in_specs=[pl.BlockSpec(memor...  18.1 us
    all_to_all x1, starting transfers between devices, body(): received = lax.all_to_all(contributions, 'span', 0, 0, tiled=True)  8.53 us
    all_to_all x1, starting transfers between devices, body(): gathered = lax.all_to_all(copies, 'circ', 0, 0, tiled=True)  6.7 us
    concatenate x2, other arithmetic, sweep(): span_up = jnp.concatenate([current[:, :, 1:], span_high], axis=2)  5.63 us
    concatenate x2, other arithmetic, sweep(): padded = jnp.concatenate([circ_low, current, circ_high], axis=1)  3.93 us
    slice x6, local copies, waits for them, and re-layouts, halo_parts(): lax.slice_in_dim(block, block.shape[dim] - 1, None, axis=dim)  3.77 us
    ppermute x6, waiting for transfers between devices, halo_parts(): lax.ppermute(lax.slice_in_dim(block, block.shape[dim] - 1, None, axis=dim...  3.35 us
  transfers between devices with their start and end apart: 14, of which 2 were waited for; matrix products, arithmetic and copies ran while one was open for 33% of the time, Pallas kernels for 9%

profile of v3, /device:TPU:24, one launch (start us, length us, event | category | flops | bytes accessed | tf_op | source)
XLA Modules:
  0.0 99.7 jit_solution(16201359630490575597)
XLA Ops:
  0.0 1.2 %fusion.8 = (f32[5,1,128,128]{3,2,1,0:T(8,128)S(1)}, f32[5,1,128,128]{3,2,1,0:T(8,128)S(1)}) fusion(f32[5,4,128,128]{3,2,1,0:T(8,128)} %prev_ref.3), kind=kLoop, calls=%fused_computation.52 | loop fusion | bytes 1310720 | tf_op jit(solution)/shard_map/slice | solution.py:37
  1.2 3.0 %collective-permute-start.1 = (f32[5,1,128,128]{3,2,1,0:T(8,128)S(1)}, f32[5,1,128,128]{3,2,1,0:T(8,128)}, u32[]{:S(2)}, u32[]{:S(2)}) collective-permute-start(f32[5,1,128,128]{3,2,1,0:T(8,128)S(1)} %get-tuple-element.21), channel_id=1, source_target_pairs={{32,0},{64,32},{96,64},{128,96},{160,128},{192,160},{224,192},{0,2... | collective-permute-start | bytes 983048 | tf_op jit(solution)/shard_map/ppermute | solution.py:38
  4.9 5.4 %collective-permute-start.2 = (f32[5,4,1,128]{3,2,1,0:T(1,128)}, f32[5,4,1,128]{3,2,1,0:T(1,128)}, u32[]{:S(2)}, u32[]{:S(2)}) collective-permute-start(f32[5,4,1,128]{3,2,1,0:T(1,128)} %get-tuple-element.17), channel_id=1, source_target_pairs={{1,0},{2,1},{3,2},{4,3},{5,4},{6,5},{7,6},{8,7},{9,8},{10,9},{11,1... | collective-permute-start | bytes 30728 | tf_op jit(solution)/shard_map/ppermute | solution.py:38
  10.9 6.7 %all-to-all-start = ((f32[8,5,4,128]{3,2,1,0:T(4,128)}), f32[8,5,4,128]{3,2,1,0:T(4,128)}, u32[]{:S(2)}, u32[]{:S(2)}) async-start(f32[8,5,4,128]{3,2,1,0:T(4,128)} %broadcast_in_dim.61), calls=%async_computation | async-start | bytes 163840 | tf_op jit(solution)/shard_map/all_to_all | solution.py:187
  17.6 1.4 %fusion.7 = (f32[5,4,127,128]{3,2,1,0:T(8,128)S(1)}, f32[5,4,127,128]{3,2,1,0:T(8,128)}) fusion(f32[5,4,128,128]{3,2,1,0:T(8,128)S(1)} %copy-done), kind=kLoop, calls=%fused_computation.51 | loop fusion | bytes 5201920 | tf_op jit(solution)/shard_map/slice | solution.py:106
  26.5 2.5 %pad_maximum_fusion.2.su_ref = f32[5,4,128,128]{3,2,1,0:T(8,128)} fusion(f32[5,4,1,128]{3,2,1,0:T(1,128)S(1)} %broadcast_multiply_fusion.1, f32[5,4,127,128]{3,2,1,0:T(8,128)} %get-tuple-element.19), kind=kLoop, calls=%fused_computation.3 | loop fusion | flops 327680 | bytes 2621440 | tf_op jit(solution)/shard_map/concatenate | solution.py:105
  31.9 1.2 %fusion = f32[5,4,32,32,4]{3,2,4,1,0:T(8,128)S(1)} fusion(f32[32,4,4,1,1]{0,2,1,4,3:T(4,128)S(1)} %copy.70, f32[5,4,4,32,1]{3,2,1,0,4:T(4,128)S(1)} %reshape.201), kind=kOutput, calls=%fused_computation.12 | convolution fusion | flops 3932160 | bytes 339968 | tf_op jit(solution)/shard_map/ogk,ftkp->oftgp/dot_general | solution.py:205
  34.3 8.5 %all-to-all-start.1 = ((f32[32,5,4,128]{3,2,1,0:T(4,128)}), f32[32,5,4,128]{3,2,1,0:T(4,128)S(1)}, u32[]{:S(2)}, u32[]{:S(2)}) async-start(f32[32,5,4,128]{3,2,1,0:T(4,128)} %copy.57), calls=%async_computation.1 | async-start | bytes 655360 | tf_op jit(solution)/shard_map/all_to_all | solution.py:208
  42.9 2.5 %pad_maximum_fusion.c_ref.cu_ref.cd_ref = f32[5,6,128,128]{3,2,1,0:T(8,128)} fusion(f32[5,1,128,128]{3,2,1,0:T(8,128)} %collective-permute-done.1, f32[5,4,128,128]{3,2,1,0:T(8,128)S(1)} %copy-done, f32[5,1,128,128]{3,2,1,0:T(8,128)} %collective-permute-done), kind=kLoop, calls=%fused_computation | loop fusion | flops 983040 | bytes 3932160 | tf_op jit(solution)/shard_map/concatenate | solution.py:104
  45.4 1.3 %broadcast_in_dim.59.inlet_ref = f32[5,4,128,1]{3,2,1,0:T(8,128)} broadcast(f32[]{:T(128)} %constant.17.clone.1), dimensions={} | broadcast | bytes 10244 | tf_op jit(solution)/shard_map/broadcast_in_dim | solution.py:212
  46.6 9.0 %shard_map.91 = f32[5,4,128,128]{3,2,1,0:T(8,128)} custom-call(f32[75]{0:T(128)} %reshape.197.j_ref, f32[5,6,128,128]{3,2,1,0:T(8,128)} %pad_maximum_fusion.c_ref.cu_ref.cd_ref, f32[5,6,128,128]{3,2,1,0:T(8,128)} %pad_maximum_fusion.c_ref.cu_ref.cd_ref, f32[5,6,128,128]{3,2,1,0:T(8,128)} %pad_maximum_fusion.c_ref.cu_ref.cd_ref, ...), custom_call_target="tpu_custom_call" | custom-call | tf_op jit(solution)/shard_map/pallas_call | solution.py:110
  56.9 1.5 %collective-permute-start.4 = (f32[5,1,128,128]{3,2,1,0:T(8,128)S(1)}, f32[5,1,128,128]{3,2,1,0:T(8,128)}, u32[]{:S(2)}, u32[]{:S(2)}) collective-permute-start(f32[5,1,128,128]{3,2,1,0:T(8,128)S(1)} %get-tuple-element.14), channel_id=1, source_target_pairs={{0,32},{32,64},{64,96},{96,128},{128,160},{160,192},{192,224},{224... | collective-permute-start | bytes 983048 | tf_op jit(solution)/shard_map/ppermute | solution.py:37
  58.5 2.7 %collective-permute-start.6 = (f32[5,1,128,128]{3,2,1,0:T(8,128)S(1)}, f32[5,1,128,128]{3,2,1,0:T(8,128)}, u32[]{:S(2)}, u32[]{:S(2)}) collective-permute-start(f32[5,1,128,128]{3,2,1,0:T(8,128)S(1)} %get-tuple-element.15), channel_id=1, source_target_pairs={{32,0},{64,32},{96,64},{128,96},{160,128},{192,160},{224,192},{0,2... | collective-permute-start | bytes 983048 | tf_op jit(solution)/shard_map/ppermute | solution.py:38
  61.8 5.4 %collective-permute-start.8 = (f32[5,4,1,128]{3,2,1,0:T(1,128)}, f32[5,4,1,128]{3,2,1,0:T(1,128)}, u32[]{:S(2)}, u32[]{:S(2)}) collective-permute-start(f32[5,4,1,128]{3,2,1,0:T(1,128)} %get-tuple-element.11), channel_id=1, source_target_pairs={{1,0},{2,1},{3,2},{4,3},{5,4},{6,5},{7,6},{8,7},{9,8},{10,9},{11,1... | collective-permute-start | bytes 30728 | tf_op jit(solution)/shard_map/ppermute | solution.py:38
  69.9 1.4 %fusion.4 = (f32[5,4,127,128]{3,2,1,0:T(8,128)S(1)}, f32[5,4,127,128]{3,2,1,0:T(8,128)}) fusion(f32[5,4,128,128]{3,2,1,0:T(8,128)S(1)} %add_select_fusion), kind=kLoop, calls=%fused_computation.48 | loop fusion | bytes 5201920 | tf_op jit(solution)/shard_map/slice | solution.py:106
  71.3 1.5 %copy.68.inlet_ref = f32[5,4,128,1]{3,2,1,0:T(8,128)} copy(f32[5,4,128,1]{2,1,0,3:T(4,128)S(1)} %bitcast.35) | data formatting | bytes 20480 | tf_op jit(solution)/shard_map/reduce_sum | solution.py:209
  72.8 3.3 %collective-permute-done.11 = f32[5,4,1,1]{0,1,3,2:T(4,128)S(1)} collective-permute-done((f32[5,4,1,1]{0,1,3,2:T(4,128)S(1)}, f32[5,4,1,1]{0,1,3,2:T(4,128)S(1)}, u32[]{:S(2)}, u32[]{:S(2)}) %collective-permute-start.11) | collective-permute-done | bytes 112 | tf_op jit(solution)/shard_map/ppermute | solution.py:37
  76.1 2.0 %collective-permute-start.9 = (f32[5,4,1,1]{0,1,3,2:T(4,128)S(1)}, f32[5,4,1,1]{0,1,3,2:T(4,128)S(1)}, u32[]{:S(2)}, u32[]{:S(2)}) collective-permute-start(f32[5,4,1,1]{0,1,3,2:T(4,128)S(1)} %get-tuple-element.23), channel_id=1, source_target_pairs={{1,0},{2,1},{3,2},{4,3},{5,4},{6,5},{7,6},{8,7},{9,8},{10,9},{11,1... | collective-permute-start | bytes 248 | tf_op jit(solution)/shard_map/ppermute | solution.py:38
  78.1 1.3 %collective-permute-done.9 = f32[5,4,1,1]{0,1,3,2:T(4,128)S(1)} collective-permute-done((f32[5,4,1,1]{0,1,3,2:T(4,128)S(1)}, f32[5,4,1,1]{0,1,3,2:T(4,128)S(1)}, u32[]{:S(2)}, u32[]{:S(2)}) %collective-permute-start.9) | collective-permute-done | bytes 112 | tf_op jit(solution)/shard_map/ppermute | solution.py:38
  79.6 4.1 %collective-permute-start.7 = (f32[5,1,128,1]{0,1,3,2:T(1,128)S(1)}, f32[5,1,128,1]{0,1,3,2:T(1,128)S(1)}, u32[]{:S(2)}, u32[]{:S(2)}) collective-permute-start(f32[5,1,128,1]{0,1,3,2:T(1,128)S(1)} %get-tuple-element.25), channel_id=1, source_target_pairs={{32,0},{64,32},{96,64},{128,96},{160,128},{192,160},{224,192},{0,2... | collective-permute-start | bytes 7688 | tf_op jit(solution)/shard_map/ppermute | solution.py:38
  84.6 3.1 %pad_maximum_fusion.4 = (f32[5,4,128,128]{3,2,1,0:T(8,128)}, f32[5,4,128,128]{3,2,1,0:T(8,128)}) fusion(f32[5,4,1,128]{3,2,1,0:T(1,128)S(1)} %get-tuple-element.32, f32[5,4,127,128]{3,2,1,0:T(8,128)} %get-tuple-element.13, f32[5,4,127,128]{3,2,1,0:T(8,128)S(1)} %get-tuple-element.12, f32[5,4,1,128]{3,2,1,0:T(1,128)S(1)} %get-tuple-element.31), kind=kLoop, calls=%fused_computation.5 | loop fusion | flops 655360 | bytes 5242880 | tf_op jit(solution)/shard_map/concatenate | solution.py:105
  87.9 1.3 %add_select_fusion.2 = (f32[5,1,128,128]{3,2,1,0:T(8,128)S(1)}, f32[5,1,128,128]{3,2,1,0:T(8,128)S(1)}) fusion(f32[5,1,128,128]{3,2,1,0:T(8,128)} %collective-permute-done.4, f32[5,128]{1,0:T(8,128)S(1)} %bitcast.36, pred[128]{0:T(512)(128)(4,1)S(1)} %copy-done.6, f32[5,1,128,128]{3,2,1,0:T(8,128)} %collective-permute-done.6, f32[5,128]{1,0:T(8,128)S(1)} %bitcast.37), kind=kLoop, calls=%fused_computation.8 | loop fusion | flops 327680 | bytes 1315968 | tf_op jit(solution)/shard_map/jit(_where)/select_n | solution.py:220
  89.2 1.4 %pad_maximum_fusion.1.c_ref.cu_ref.cd_ref = f32[5,6,128,128]{3,2,1,0:T(8,128)} fusion(f32[5,1,128,128]{3,2,1,0:T(8,128)S(1)} %get-tuple-element.34, f32[5,4,128,128]{3,2,1,0:T(8,128)S(1)} %add_select_fusion, f32[5,1,128,128]{3,2,1,0:T(8,128)S(1)} %get-tuple-element.33), kind=kLoop, calls=%fused_computation.1 | loop fusion | flops 983040 | bytes 3932160 | tf_op jit(solution)/shard_map/concatenate | solution.py:104
  90.6 9.0 %shard_map.92 = f32[5,4,128,128]{3,2,1,0:T(8,128)} custom-call(f32[75]{0:T(128)} %reshape.197.j_ref, f32[5,6,128,128]{3,2,1,0:T(8,128)} %pad_maximum_fusion.1.c_ref.cu_ref.cd_ref, f32[5,6,128,128]{3,2,1,0:T(8,128)} %pad_maximum_fusion.1.c_ref.cu_ref.cd_ref, f32[5,6,128,128]{3,2,1,0:T(8,128)} %pad_maximum_fusion.1.c_ref.cu_ref.cd_ref, ...), custom_call_target="tpu_custom_call" | custom-call | tf_op jit(solution)/shard_map/pallas_call | solution.py:110
  (88 shorter events, 18.5 us)
Async XLA Ops:
  0.0 4.3 %copy-start = (f32[5,4,128,128]{3,2,1,0:T(8,128)S(1)}, f32[5,4,128,128]{3,2,1,0:T(8,128)}, u32[]{:S(2)}) copy-start(f32[5,4,128,128]{3,2,1,0:T(8,128)} %prev_ref.3) | copy-start | bytes 3932164
  0.0 10.3 %copy-start.5 = (f32[5,4,128]{2,1,0:T(4,128)S(1)}, f32[5,4,128]{2,1,0:T(4,128)}, u32[]{:S(2)}) copy-start(f32[5,4,128]{2,1,0:T(4,128)} %param.12) | copy-start | bytes 30724
  1.2 41.6 %collective-permute-start.1 = (f32[5,1,128,128]{3,2,1,0:T(8,128)S(1)}, f32[5,1,128,128]{3,2,1,0:T(8,128)}, u32[]{:S(2)}, u32[]{:S(2)}) collective-permute-start(f32[5,1,128,128]{3,2,1,0:T(8,128)S(1)} %get-tuple-element.21), channel_id=1, source_target_pairs={{32,0},{64,32},{96,64},{128,96},{160,128},{192,160},{224,192},{0,2... | collective-permute-start | bytes 983048 | tf_op jit(solution)/shard_map/ppermute | solution.py:38
  4.2 38.6 %collective-permute-start = (f32[5,1,128,128]{3,2,1,0:T(8,128)S(1)}, f32[5,1,128,128]{3,2,1,0:T(8,128)}, u32[]{:S(2)}, u32[]{:S(2)}) collective-permute-start(f32[5,1,128,128]{3,2,1,0:T(8,128)S(1)} %get-tuple-element.20), channel_id=1, source_target_pairs={{0,32},{32,64},{64,96},{96,128},{128,160},{160,192},{192,224},{224... | collective-permute-start | bytes 983048 | tf_op jit(solution)/shard_map/ppermute | solution.py:37
  4.9 20.9 %collective-permute-start.2 = (f32[5,4,1,128]{3,2,1,0:T(1,128)}, f32[5,4,1,128]{3,2,1,0:T(1,128)}, u32[]{:S(2)}, u32[]{:S(2)}) collective-permute-start(f32[5,4,1,128]{3,2,1,0:T(1,128)} %get-tuple-element.17), channel_id=1, source_target_pairs={{1,0},{2,1},{3,2},{4,3},{5,4},{6,5},{7,6},{8,7},{9,8},{10,9},{11,1... | collective-permute-start | bytes 30728 | tf_op jit(solution)/shard_map/ppermute | solution.py:38
  10.3 18.7 %collective-permute-start.3 = (f32[5,4,1,128]{3,2,1,0:T(1,128)}, f32[5,4,1,128]{3,2,1,0:T(1,128)}, u32[]{:S(2)}, u32[]{:S(2)}) collective-permute-start(f32[5,4,1,128]{3,2,1,0:T(1,128)} %get-tuple-element.16), channel_id=1, source_target_pairs={{0,1},{1,2},{2,3},{3,4},{4,5},{5,6},{6,7},{7,8},{8,9},{9,10},{10,1... | collective-permute-start | bytes 30728 | tf_op jit(solution)/shard_map/ppermute | solution.py:37
  10.9 20.0 %all-to-all-start = ((f32[8,5,4,128]{3,2,1,0:T(4,128)}), f32[8,5,4,128]{3,2,1,0:T(4,128)}, u32[]{:S(2)}, u32[]{:S(2)}) async-start(f32[8,5,4,128]{3,2,1,0:T(4,128)} %broadcast_in_dim.61), calls=%async_computation | async-start | bytes 163840 | tf_op jit(solution)/shard_map/all_to_all | solution.py:187
  34.3 32.8 %all-to-all-start.1 = ((f32[32,5,4,128]{3,2,1,0:T(4,128)}), f32[32,5,4,128]{3,2,1,0:T(4,128)S(1)}, u32[]{:S(2)}, u32[]{:S(2)}) async-start(f32[32,5,4,128]{3,2,1,0:T(4,128)} %copy.57), calls=%async_computation.1 | async-start | bytes 655360 | tf_op jit(solution)/shard_map/all_to_all | solution.py:208
  55.6 5.5 %copy-start.1 = (f32[5,4,128,128]{3,2,1,0:T(8,128)S(1)}, f32[5,4,128,128]{3,2,1,0:T(8,128)}, u32[]{:S(2)}) copy-start(f32[5,4,128,128]{3,2,1,0:T(8,128)} %shard_map.91) | copy-start | bytes 3932164
  55.6 12.3 %copy-start.7 = (f32[5]{0:T(128)S(1)}, f32[5]{0:T(128)}, u32[]{:S(2)}) copy-start(f32[5]{0:T(128)} %get-tuple-element.5) | copy-start | bytes 64
  55.7 12.3 %copy-start.8 = (f32[5]{0:T(128)S(1)}, f32[5]{0:T(128)}, u32[]{:S(2)}) copy-start(f32[5]{0:T(128)} %get-tuple-element.6) | copy-start | bytes 64
  55.7 12.3 %copy-start.9 = (f32[5]{0:T(128)S(1)}, f32[5]{0:T(128)}, u32[]{:S(2)}) copy-start(f32[5]{0:T(128)} %get-tuple-element.7) | copy-start | bytes 64
  55.7 12.3 %copy-start.10 = (f32[5]{0:T(128)S(1)}, f32[5]{0:T(128)}, u32[]{:S(2)}) copy-start(f32[5]{0:T(128)} %get-tuple-element.8) | copy-start | bytes 64
  55.7 12.3 %copy-start.11 = (f32[5]{0:T(128)S(1)}, f32[5]{0:T(128)}, u32[]{:S(2)}) copy-start(f32[5]{0:T(128)} %get-tuple-element.9) | copy-start | bytes 64
  55.7 12.4 %copy-start.3 = (f32[4,128]{0,1:T(8,128)S(1)}, f32[4,128]{0,1:T(8,128)}, u32[]{:S(2)}) copy-start(f32[4,128]{0,1:T(8,128)} %copy.53) | copy-start | bytes 6148
  56.9 12.6 %copy-start.6 = (pred[128]{0:T(512)(128)(4,1)S(1)}, pred[128]{0:T(512)(128)(4,1)}, u32[]{:S(2)}) copy-start(pred[128]{0:T(512)(128)(4,1)} %iota_compare_fusion.2) | copy-start | bytes 388
  56.9 30.9 %collective-permute-start.4 = (f32[5,1,128,128]{3,2,1,0:T(8,128)S(1)}, f32[5,1,128,128]{3,2,1,0:T(8,128)}, u32[]{:S(2)}, u32[]{:S(2)}) collective-permute-start(f32[5,1,128,128]{3,2,1,0:T(8,128)S(1)} %get-tuple-element.14), channel_id=1, source_target_pairs={{0,32},{32,64},{64,96},{96,128},{128,160},{160,192},{192,224},{224... | collective-permute-start | bytes 983048 | tf_op jit(solution)/shard_map/ppermute | solution.py:37
  58.5 29.4 %collective-permute-start.6 = (f32[5,1,128,128]{3,2,1,0:T(8,128)S(1)}, f32[5,1,128,128]{3,2,1,0:T(8,128)}, u32[]{:S(2)}, u32[]{:S(2)}) collective-permute-start(f32[5,1,128,128]{3,2,1,0:T(8,128)S(1)} %get-tuple-element.15), channel_id=1, source_target_pairs={{32,0},{64,32},{96,64},{128,96},{160,128},{192,160},{224,192},{0,2... | collective-permute-start | bytes 983048 | tf_op jit(solution)/shard_map/ppermute | solution.py:38
  61.8 17.9 %collective-permute-start.10 = (f32[5,4,1,128]{3,2,1,0:T(1,128)S(1)}, f32[5,4,1,128]{3,2,1,0:T(1,128)}, u32[]{:S(2)}, u32[]{:S(2)}) collective-permute-start(f32[5,4,1,128]{3,2,1,0:T(1,128)S(1)} %get-tuple-element.10), channel_id=1, source_target_pairs={{0,1},{1,2},{2,3},{3,4},{4,5},{5,6},{6,7},{7,8},{8,9},{9,10},{10,1... | collective-permute-start | bytes 30728 | tf_op jit(solution)/shard_map/ppermute | solution.py:37
  61.8 22.0 %collective-permute-start.8 = (f32[5,4,1,128]{3,2,1,0:T(1,128)}, f32[5,4,1,128]{3,2,1,0:T(1,128)}, u32[]{:S(2)}, u32[]{:S(2)}) collective-permute-start(f32[5,4,1,128]{3,2,1,0:T(1,128)} %get-tuple-element.11), channel_id=1, source_target_pairs={{1,0},{2,1},{3,2},{4,3},{5,4},{6,5},{7,6},{8,7},{9,8},{10,9},{11,1... | collective-permute-start | bytes 30728 | tf_op jit(solution)/shard_map/ppermute | solution.py:38
  69.2 6.9 %collective-permute-start.11 = (f32[5,4,1,1]{0,1,3,2:T(4,128)S(1)}, f32[5,4,1,1]{0,1,3,2:T(4,128)S(1)}, u32[]{:S(2)}, u32[]{:S(2)}) collective-permute-start(f32[5,4,1,1]{0,1,3,2:T(4,128)S(1)} %get-tuple-element.22), channel_id=1, source_target_pairs={{0,1},{1,2},{2,3},{3,4},{4,5},{5,6},{6,7},{7,8},{8,9},{9,10},{10,1... | collective-permute-start | bytes 248 | tf_op jit(solution)/shard_map/ppermute | solution.py:37
  76.1 3.3 %collective-permute-start.9 = (f32[5,4,1,1]{0,1,3,2:T(4,128)S(1)}, f32[5,4,1,1]{0,1,3,2:T(4,128)S(1)}, u32[]{:S(2)}, u32[]{:S(2)}) collective-permute-start(f32[5,4,1,1]{0,1,3,2:T(4,128)S(1)} %get-tuple-element.23), channel_id=1, source_target_pairs={{1,0},{2,1},{3,2},{4,3},{5,4},{6,5},{7,6},{8,7},{9,8},{10,9},{11,1... | collective-permute-start | bytes 248 | tf_op jit(solution)/shard_map/ppermute | solution.py:38
  79.4 8.3 %collective-permute-start.5 = (f32[5,1,128,1]{0,1,3,2:T(1,128)S(1)}, f32[5,1,128,1]{0,1,3,2:T(1,128)S(1)}, u32[]{:S(2)}, u32[]{:S(2)}) collective-permute-start(f32[5,1,128,1]{0,1,3,2:T(1,128)S(1)} %get-tuple-element.24), channel_id=1, source_target_pairs={{0,32},{32,64},{64,96},{96,128},{128,160},{160,192},{192,224},{224... | collective-permute-start | bytes 7688 | tf_op jit(solution)/shard_map/ppermute | solution.py:37
  79.6 8.2 %collective-permute-start.7 = (f32[5,1,128,1]{0,1,3,2:T(1,128)S(1)}, f32[5,1,128,1]{0,1,3,2:T(1,128)S(1)}, u32[]{:S(2)}, u32[]{:S(2)}) collective-permute-start(f32[5,1,128,1]{0,1,3,2:T(1,128)S(1)} %get-tuple-element.25), channel_id=1, source_target_pairs={{32,0},{64,32},{96,64},{128,96},{160,128},{192,160},{224,192},{0,2... | collective-permute-start | bytes 7688 | tf_op jit(solution)/shard_map/ppermute | solution.py:38
  (2 other events, 4.7 us)

commit v4 on v2

--- a/solution.py
+++ b/solution.py
@@ -97,8 +97,9 @@
     lax.fori_loop(0, c_ref.shape[2] // 8, chunk, 0)
 
 
-def sweep(current, previous, rate_cells, inlet_column, jacobians):
-    parts = halo_parts(current)
+def sweep(current, previous, rate_cells, inlet_column, jacobians, parts=None):
+    if parts is None:
+        parts = halo_parts(current)
     circ_low, circ_high, span_low, span_high = parts
     padded = jnp.concatenate([circ_low, current, circ_high], axis=1)
     span_up = jnp.concatenate([current[:, :, 1:], span_high], axis=2)
@@ -208,8 +209,20 @@
     inlet_plane = jnp.sum(received, axis=0)
 
     inlet_column = inlet_plane[..., None]
-    mid, _ = sweep(q_old, q_old, pseudo_rate, inlet_column, flux_jacobians)
-    new, _ = sweep(mid, q_old, pseudo_rate, inlet_column, flux_jacobians)
+    contributions, q_for_halo = lax.optimization_barrier((contributions, q_old))
+    mid, _ = sweep(q_old, q_old, pseudo_rate, inlet_column, flux_jacobians, halo_parts(q_for_halo))
+    mid_parts = halo_parts(mid)
+    zero_parts = [jnp.zeros_like(p) for p in mid_parts]
+    new, _ = sweep(mid, q_old, pseudo_rate, inlet_column, flux_jacobians, zero_parts)
+    circ_low, circ_high, span_low, span_high = mid_parts
+    eye = jnp.eye(NF, dtype=q_old.dtype)
+    from_low = lambda d: 0.5 * flux_jacobians[d] + viscosity * eye
+    from_high = lambda d: viscosity * eye - 0.5 * flux_jacobians[d]
+    rate = pseudo_rate[None]
+    new = new.at[:, :1].add(rate[:, :1] * contract(from_low(0), circ_low))
+    new = new.at[:, -1:].add(rate[:, -1:] * contract(from_high(0), circ_high))
+    new = new.at[:, :, :1].add(rate[:, :, :1] * contract(from_low(1), span_low))
+    new = new.at[:, :, -1:].add(rate[:, :, -1:] * contract(from_high(1), span_high))
     return new
 
 

time: 90.4 us -> 96.8 us (1.071)
  the two profiles are of different devices: /device:TPU:1 before, /device:TPU:6 now
where the time goes in v4:
time: 96.8 us; the launch traced here: 95.9 us
  starting transfers between devices  30.1 us (31%)
  local copies, waits for them, and re-layouts  21.5 us (22%)
  Pallas kernels  18.1 us (19%)
  other arithmetic  14.5 us (15%)
  waiting for transfers between devices  9.28 us (10%)
  matrix products  2.31 us (2%)
    pallas_call x2, Pallas kernels, sweep(): pl.pallas_call(stencil_kernel, grid=(rows,), in_specs=[pl.BlockSpec(memor...  18.1 us
    ppermute x4, starting transfers between devices, halo_parts(): high = lax.ppermute(lax.slice_in_dim(block, 0, 1, axis=dim), axis, backward)  12.1 us
    all_to_all x1, starting transfers between devices, body(): received = lax.all_to_all(contributions, 'span', 0, 0, tiled=True)  7.06 us
    all_to_all x1, starting transfers between devices, body(): gathered = lax.all_to_all(copies, 'circ', 0, 0, tiled=True)  5.79 us
    ppermute x4, starting transfers between devices, halo_parts(): lax.ppermute(lax.slice_in_dim(block, block.shape[dim] - 1, None, axis=dim...  5.15 us
    ppermute x4, waiting for transfers between devices, halo_parts(): lax.ppermute(lax.slice_in_dim(block, block.shape[dim] - 1, None, axis=dim...  5.05 us
    ppermute x4, waiting for transfers between devices, halo_parts(): high = lax.ppermute(lax.slice_in_dim(block, 0, 1, axis=dim), axis, backward)  4.21 us
    slice x2, local copies, waits for them, and re-layouts, sweep(): span_down = jnp.concatenate([span_low, current[:, :, :-1]], axis=2)  3.45 us
  transfers between devices with their start and end apart: 10, of which 2 were waited for; matrix products, arithmetic and copies ran while one was open for 24% of the time, Pallas kernels for 9%

profile of v4, /device:TPU:6, one launch (start us, length us, event | category | flops | bytes accessed | tf_op | source)
XLA Modules:
  0.0 95.9 jit_solution(1314867618882059062)
XLA Ops:
  0.0 1.3 %broadcast_in_dim.61 = f32[8,5,4,128]{3,2,1,0:T(4,128)} broadcast(f32[5,4,128]{2,1,0:T(4,128)} %param.20), dimensions={1,2,3} | broadcast | bytes 92160 | tf_op jit(solution)/shard_map/broadcast_in_dim | solution.py:186
  1.3 5.8 %all-to-all-start = ((f32[8,5,4,128]{3,2,1,0:T(4,128)}), f32[8,5,4,128]{3,2,1,0:T(4,128)S(1)}, u32[]{:S(2)}, u32[]{:S(2)}) async-start(f32[8,5,4,128]{3,2,1,0:T(4,128)} %broadcast_in_dim.61), calls=%async_computation | async-start | bytes 163840 | tf_op jit(solution)/shard_map/all_to_all | solution.py:187
  12.7 3.2 %fusion.11 = (f32[5,4,127,128]{3,2,1,0:T(8,128)}, f32[5,4,127,128]{3,2,1,0:T(8,128)S(1)}) fusion(f32[5,4,128,128]{3,2,1,0:T(8,128)} %prev_ref.3), kind=kLoop, calls=%fused_computation.76 | loop fusion | bytes 5201920 | tf_op jit(solution)/shard_map/slice | solution.py:106
  16.4 2.3 %fusion.2 = f32[5,4,32,32,4]{3,2,4,1,0:T(8,128)} fusion(f32[32,4,4,1,1]{0,2,1,4,3:T(4,128)S(1)} %copy.42, f32[5,4,4,32,1]{3,2,1,0,4:T(4,128)S(1)} %reshape.508), kind=kOutput, calls=%fused_computation.21 | convolution fusion | flops 3932160 | bytes 339968 | tf_op jit(solution)/shard_map/ogk,ftkp->oftgp/dot_general | solution.py:205
  19.6 2.4 %copy.36 = f32[32,5,4,128]{3,2,1,0:T(4,128)} copy(f32[32,5,4,128]{0,3,2,1:T(8,128)} %bitcast.63) | data formatting | bytes 655360 | tf_op jit(solution)/shard_map/reshape | solution.py:207
  22.1 7.1 %collective-permute-start.2 = (f32[5,4,1,128]{3,2,1,0:T(1,128)S(1)}, f32[5,4,1,128]{3,2,1,0:T(1,128)S(1)}, u32[]{:S(2)}, u32[]{:S(2)}) collective-permute-start(f32[5,4,1,128]{3,2,1,0:T(1,128)S(1)} %get-tuple-element.82), channel_id=1, source_target_pairs={{1,0},{2,1},{3,2},{4,3},{5,4},{6,5},{7,6},{8,7},{9,8},{10,9},{11,1... | collective-permute-start | bytes 30728 | tf_op jit(solution)/shard_map/ppermute | solution.py:38
  29.1 7.1 %all-to-all-start.1 = ((f32[32,5,4,128]{3,2,1,0:T(4,128)}), f32[32,5,4,128]{3,2,1,0:T(4,128)S(1)}, u32[]{:S(2)}, u32[]{:S(2)}) async-start(f32[32,5,4,128]{3,2,1,0:T(4,128)} %copy.36), calls=%async_computation.1 | async-start | bytes 655360 | tf_op jit(solution)/shard_map/all_to_all | solution.py:208
  37.1 1.2 %collective-permute-start.1 = (f32[5,1,128,128]{3,2,1,0:T(8,128)S(1)}, f32[5,1,128,128]{3,2,1,0:T(8,128)S(1)}, u32[]{:S(2)}, u32[]{:S(2)}) collective-permute-start(f32[5,1,128,128]{3,2,1,0:T(8,128)S(1)} %get-tuple-element.86), channel_id=1, source_target_pairs={{32,0},{64,32},{96,64},{128,96},{160,128},{192,160},{224,192},{0,2... | collective-permute-start | bytes 983048 | tf_op jit(solution)/shard_map/ppermute | solution.py:38
  38.4 2.5 %pad_maximum_fusion.3.sd_ref = f32[5,4,128,128]{3,2,1,0:T(8,128)} fusion(f32[5,4,127,128]{3,2,1,0:T(8,128)} %get-tuple-element.83, f32[5,4,1,128]{3,2,1,0:T(1,128)S(1)} %broadcast_multiply_fusion.1), kind=kLoop, calls=%fused_computation.3 | loop fusion | flops 327680 | bytes 2621440 | tf_op jit(solution)/shard_map/concatenate | solution.py:106
  42.1 5.0 %collective-permute-done = f32[5,1,128,128]{3,2,1,0:T(8,128)S(1)} collective-permute-done((f32[5,1,128,128]{3,2,1,0:T(8,128)}, f32[5,1,128,128]{3,2,1,0:T(8,128)S(1)}, u32[]{:S(2)}, u32[]{:S(2)}) %collective-permute-start) | collective-permute-done | bytes 327712 | tf_op jit(solution)/shard_map/ppermute | solution.py:37
  47.1 4.2 %collective-permute-done.1 = f32[5,1,128,128]{3,2,1,0:T(8,128)S(1)} collective-permute-done((f32[5,1,128,128]{3,2,1,0:T(8,128)S(1)}, f32[5,1,128,128]{3,2,1,0:T(8,128)S(1)}, u32[]{:S(2)}, u32[]{:S(2)}) %collective-permute-start.1) | collective-permute-done | bytes 327712 | tf_op jit(solution)/shard_map/ppermute | solution.py:38
  51.3 1.4 %pad_maximum_fusion.c_ref.cu_ref.cd_ref = f32[5,6,128,128]{3,2,1,0:T(8,128)} fusion(f32[5,1,128,128]{3,2,1,0:T(8,128)S(1)} %collective-permute-done.1, f32[5,4,128,128]{3,2,1,0:T(8,128)S(1)} %copy-done, f32[5,1,128,128]{3,2,1,0:T(8,128)S(1)} %collective-permute-done), kind=kLoop, calls=%fused_computation | loop fusion | flops 983040 | bytes 3932160 | tf_op jit(solution)/shard_map/concatenate | solution.py:104
  52.8 1.5 %copy.37.inlet_ref = f32[5,4,128,1]{3,2,1,0:T(8,128)} copy(f32[5,4,128,1]{2,1,0,3:T(4,128)S(1)} %bitcast.67) | data formatting | bytes 20480 | tf_op jit(solution)/shard_map/broadcast_in_dim | solution.py:211
  54.3 9.0 %shard_map.91 = f32[5,4,128,128]{3,2,1,0:T(8,128)} custom-call(f32[75]{0:T(128)} %reshape.504.j_ref, f32[5,6,128,128]{3,2,1,0:T(8,128)} %pad_maximum_fusion.c_ref.cu_ref.cd_ref, f32[5,6,128,128]{3,2,1,0:T(8,128)} %pad_maximum_fusion.c_ref.cu_ref.cd_ref, f32[5,6,128,128]{3,2,1,0:T(8,128)} %pad_maximum_fusion.c_ref.cu_ref.cd_ref, ...), custom_call_target="tpu_custom_call" | custom-call | tf_op jit(solution)/shard_map/pallas_call | solution.py:110
  65.9 3.8 %collective-permute-start.7 = (f32[5,4,1,128]{3,2,1,0:T(1,128)S(1)}, f32[5,4,1,128]{3,2,1,0:T(1,128)S(1)}, u32[]{:S(2)}, u32[]{:S(2)}) collective-permute-start(f32[5,4,1,128]{3,2,1,0:T(1,128)S(1)} %get-tuple-element.75), channel_id=1, source_target_pairs={{1,0},{2,1},{3,2},{4,3},{5,4},{6,5},{7,6},{8,7},{9,8},{10,9},{11,1... | collective-permute-start | bytes 30728 | tf_op jit(solution)/shard_map/ppermute | solution.py:38
  69.7 4.1 %collective-permute-start.4 = (f32[5,1,128,128]{3,2,1,0:T(8,128)S(1)}, f32[5,1,128,128]{3,2,1,0:T(8,128)S(1)}, u32[]{:S(2)}, u32[]{:S(2)}) collective-permute-start(f32[5,1,128,128]{3,2,1,0:T(8,128)S(1)} %get-tuple-element.78), channel_id=1, source_target_pairs={{0,32},{32,64},{64,96},{96,128},{128,160},{160,192},{192,224},{224... | collective-permute-start | bytes 983048 | tf_op jit(solution)/shard_map/ppermute | solution.py:37
  73.9 1.5 %pad_maximum_fusion.1.c_ref.cu_ref.cd_ref = f32[5,6,128,128]{3,2,1,0:T(8,128)} fusion(f32[5,1,128,128]{3,2,1,0:T(8,128)S(1)} %broadcast.606, f32[5,4,128,128]{3,2,1,0:T(8,128)S(1)} %copy-done.1), kind=kLoop, calls=%fused_computation.1 | loop fusion | flops 983040 | bytes 3604480 | tf_op jit(solution)/shard_map/concatenate | solution.py:104
  75.4 1.2 %concatenate.31.sd_ref = f32[5,4,128,128]{3,2,1,0:T(8,128)} pad(f32[5,4,127,128]{3,2,1,0:T(8,128)S(1)} %get-tuple-element.79, f32[]{:T(128)} %constant.136.clone.1), padding=0_0x0_0x1_0x0_0 | pad | bytes 2611204 | tf_op jit(solution)/shard_map/concatenate | solution.py:106
  76.6 1.2 %concatenate.30.su_ref = f32[5,4,128,128]{3,2,1,0:T(8,128)} pad(f32[5,4,127,128]{3,2,1,0:T(8,128)S(1)} %get-tuple-element.80, f32[]{:T(128)} %constant.136.clone.1), padding=0_0x0_0x0_1x0_0 | pad | bytes 2611204 | tf_op jit(solution)/shard_map/concatenate | solution.py:105
  77.8 9.0 %shard_map.92 = f32[5,4,128,128]{3,2,1,0:T(8,128)} custom-call(f32[75]{0:T(128)} %reshape.504.j_ref, f32[5,6,128,128]{3,2,1,0:T(8,128)} %pad_maximum_fusion.1.c_ref.cu_ref.cd_ref, f32[5,6,128,128]{3,2,1,0:T(8,128)} %pad_maximum_fusion.1.c_ref.cu_ref.cd_ref, f32[5,6,128,128]{3,2,1,0:T(8,128)} %pad_maximum_fusion.1.c_ref.cu_ref.cd_ref, ...), custom_call_target="tpu_custom_call" | custom-call | tf_op jit(solution)/shard_map/pallas_call | solution.py:110
  86.9 1.9 %fusion.1 = f32[5,4,128,128]{3,2,1,0:T(8,128)} fusion(f32[5,4,128,128]{3,2,1,0:T(8,128)} %shard_map.92, f32[128,128]{1,0:T(8,128)S(1)} %get-tuple-element.93, f32[5]{0:T(128)S(1)} %get-tuple-element.71, f32[128,128]{1,0:T(8,128)S(1)} %get-tuple-element.94, f32[5]{0:T(128)S(1)} %get-tuple-element.72, f32[128,128]{1,0:T(8,128)S(1)} %get-tuple-element.95, ...), kind=kLoop, calls=%fused_computation.7 | loop fusion | flops 901120 | bytes 1048676 | tf_op jit(solution)/shard_map/scatter-add | solution.py:222
  88.9 1.9 %fusion = f32[5,4,128,128]{3,2,1,0:T(8,128)} fusion(f32[5,4,128,128]{3,2,1,0:T(8,128)} %fusion.1, f32[128,128]{1,0:T(8,128)S(1)} %get-tuple-element.88, f32[5]{0:T(128)S(1)} %get-tuple-element.66, f32[128,128]{1,0:T(8,128)S(1)} %get-tuple-element.89, f32[5]{0:T(128)S(1)} %get-tuple-element.67, f32[128,128]{1,0:T(8,128)S(1)} %get-tuple-element.90, ...), kind=kLoop, calls=%fused_computation.5 | loop fusion | flops 901120 | bytes 1048676 | tf_op jit(solution)/shard_map/scatter-add | solution.py:223
  91.8 1.6 %scatter-add.16 = f32[5,4,128,128]{3,2,1,0:T(8,128)} dynamic-update-slice(f32[5,4,128,128]{3,2,1,0:T(8,128)} %fusion, f32[5,4,1,128]{3,2,1,0:T(1,128)S(1)} %slice_add_fusion.3, s32[]{:T(128)} %constant.140.clone.1, s32[]{:T(128)} %constant.140.clone.1, s32[]{:T(128)} %constant.140.clone.1, s32[]{:T(128)} %constant.140.clone.1) | dynamic-update-slice | bytes 20484 | tf_op jit(solution)/shard_map/scatter-add | solution.py:224
  94.4 1.6 %scatter-add.19 = f32[5,4,128,128]{3,2,1,0:T(8,128)} dynamic-update-slice(f32[5,4,128,128]{3,2,1,0:T(8,128)} %scatter-add.16, f32[5,4,1,128]{3,2,1,0:T(1,128)S(1)} %slice_add_fusion.2, s32[]{:T(128)} %constant.140.clone.1, s32[]{:T(128)} %constant.140.clone.1, s32[]{:T(128)} %constant.147.clone.1, s32[]{:T(128)} %constant.140.clone.1) | dynamic-update-slice | bytes 20484 | tf_op jit(solution)/shard_map/scatter-add | solution.py:225
  (57 shorter events, 13.7 us)
Async XLA Ops:
  1.3 14.9 %all-to-all-start = ((f32[8,5,4,128]{3,2,1,0:T(4,128)}), f32[8,5,4,128]{3,2,1,0:T(4,128)S(1)}, u32[]{:S(2)}, u32[]{:S(2)}) async-start(f32[8,5,4,128]{3,2,1,0:T(4,128)} %broadcast_in_dim.61), calls=%async_computation | async-start | bytes 163840 | tf_op jit(solution)/shard_map/all_to_all | solution.py:187
  12.7 3.2 %copy-start.2 = (s32[128]{0:T(128)S(1)}, s32[128]{0:T(128)}, u32[]{:S(2)}) copy-start(s32[128]{0:T(128)} %param.21) | copy-start | bytes 1540
  15.9 2.9 %copy-start = (f32[5,4,128,128]{3,2,1,0:T(8,128)S(1)}, f32[5,4,128,128]{3,2,1,0:T(8,128)}, u32[]{:S(2)}) copy-start(f32[5,4,128,128]{3,2,1,0:T(8,128)} %prev_ref.3) | copy-start | bytes 3932164
  18.8 19.6 %collective-permute-start.3 = (f32[5,4,1,128]{3,2,1,0:T(1,128)S(1)}, f32[5,4,1,128]{3,2,1,0:T(1,128)S(1)}, u32[]{:S(2)}, u32[]{:S(2)}) collective-permute-start(f32[5,4,1,128]{3,2,1,0:T(1,128)S(1)} %get-tuple-element.81), channel_id=1, source_target_pairs={{0,1},{1,2},{2,3},{3,4},{4,5},{5,6},{6,7},{7,8},{8,9},{9,10},{10,1... | collective-permute-start | bytes 30728 | tf_op jit(solution)/shard_map/ppermute | solution.py:37
  22.1 16.3 %collective-permute-start.2 = (f32[5,4,1,128]{3,2,1,0:T(1,128)S(1)}, f32[5,4,1,128]{3,2,1,0:T(1,128)S(1)}, u32[]{:S(2)}, u32[]{:S(2)}) collective-permute-start(f32[5,4,1,128]{3,2,1,0:T(1,128)S(1)} %get-tuple-element.82), channel_id=1, source_target_pairs={{1,0},{2,1},{3,2},{4,3},{5,4},{6,5},{7,6},{8,7},{9,8},{10,9},{11,1... | collective-permute-start | bytes 30728 | tf_op jit(solution)/shard_map/ppermute | solution.py:38
  29.1 23.6 %all-to-all-start.1 = ((f32[32,5,4,128]{3,2,1,0:T(4,128)}), f32[32,5,4,128]{3,2,1,0:T(4,128)S(1)}, u32[]{:S(2)}, u32[]{:S(2)}) async-start(f32[32,5,4,128]{3,2,1,0:T(4,128)} %copy.36), calls=%async_computation.1 | async-start | bytes 655360 | tf_op jit(solution)/shard_map/all_to_all | solution.py:208
  36.2 10.9 %collective-permute-start = (f32[5,1,128,128]{3,2,1,0:T(8,128)}, f32[5,1,128,128]{3,2,1,0:T(8,128)S(1)}, u32[]{:S(2)}, u32[]{:S(2)}) collective-permute-start(f32[5,1,128,128]{3,2,1,0:T(8,128)} %get-tuple-element.85), channel_id=1, source_target_pairs={{0,32},{32,64},{64,96},{96,128},{128,160},{160,192},{192,224},{224... | collective-permute-start | bytes 983048 | tf_op jit(solution)/shard_map/ppermute | solution.py:37
  37.1 14.1 %collective-permute-start.1 = (f32[5,1,128,128]{3,2,1,0:T(8,128)S(1)}, f32[5,1,128,128]{3,2,1,0:T(8,128)S(1)}, u32[]{:S(2)}, u32[]{:S(2)}) collective-permute-start(f32[5,1,128,128]{3,2,1,0:T(8,128)S(1)} %get-tuple-element.86), channel_id=1, source_target_pairs={{32,0},{64,32},{96,64},{128,96},{160,128},{192,160},{224,192},{0,2... | collective-permute-start | bytes 983048 | tf_op jit(solution)/shard_map/ppermute | solution.py:38
  63.4 2.2 %copy-start.1 = (f32[5,4,128,128]{3,2,1,0:T(8,128)S(1)}, f32[5,4,128,128]{3,2,1,0:T(8,128)}, u32[]{:S(2)}) copy-start(f32[5,4,128,128]{3,2,1,0:T(8,128)} %shard_map.91) | copy-start | bytes 3932164
  65.9 21.0 %collective-permute-start.7 = (f32[5,4,1,128]{3,2,1,0:T(1,128)S(1)}, f32[5,4,1,128]{3,2,1,0:T(1,128)S(1)}, u32[]{:S(2)}, u32[]{:S(2)}) collective-permute-start(f32[5,4,1,128]{3,2,1,0:T(1,128)S(1)} %get-tuple-element.75), channel_id=1, source_target_pairs={{1,0},{2,1},{3,2},{4,3},{5,4},{6,5},{7,6},{8,7},{9,8},{10,9},{11,1... | collective-permute-start | bytes 30728 | tf_op jit(solution)/shard_map/ppermute | solution.py:38
  69.7 17.1 %collective-permute-start.6 = (f32[5,4,1,128]{3,2,1,0:T(1,128)S(1)}, f32[5,4,1,128]{3,2,1,0:T(1,128)S(1)}, u32[]{:S(2)}, u32[]{:S(2)}) collective-permute-start(f32[5,4,1,128]{3,2,1,0:T(1,128)S(1)} %get-tuple-element.76), channel_id=1, source_target_pairs={{0,1},{1,2},{2,3},{3,4},{4,5},{5,6},{6,7},{7,8},{8,9},{9,10},{10,1... | collective-permute-start | bytes 30728 | tf_op jit(solution)/shard_map/ppermute | solution.py:37
  69.7 19.2 %collective-permute-start.5 = (f32[5,1,128,128]{3,2,1,0:T(8,128)S(1)}, f32[5,1,128,128]{3,2,1,0:T(8,128)S(1)}, u32[]{:S(2)}, u32[]{:S(2)}) collective-permute-start(f32[5,1,128,128]{3,2,1,0:T(8,128)S(1)} %get-tuple-element.77), channel_id=1, source_target_pairs={{32,0},{64,32},{96,64},{128,96},{160,128},{192,160},{224,192},{0,2... | collective-permute-start | bytes 983048 | tf_op jit(solution)/shard_map/ppermute | solution.py:38
  69.7 17.2 %collective-permute-start.4 = (f32[5,1,128,128]{3,2,1,0:T(8,128)S(1)}, f32[5,1,128,128]{3,2,1,0:T(8,128)S(1)}, u32[]{:S(2)}, u32[]{:S(2)}) collective-permute-start(f32[5,1,128,128]{3,2,1,0:T(8,128)S(1)} %get-tuple-element.78), channel_id=1, source_target_pairs={{0,32},{32,64},{64,96},{96,128},{128,160},{160,192},{192,224},{224... | collective-permute-start | bytes 983048 | tf_op jit(solution)/shard_map/ppermute | solution.py:37

commit v5 on v4

--- a/solution.py
+++ b/solution.py
@@ -14,20 +14,6 @@
 viscosity = 0.1
 
 
-def with_halo(block, sides, width):
-    for axis, dim in sides:
-        count = lax.axis_size(axis)
-        forward = [(i, i + 1) for i in range(count - 1)]
-        forward.append((count - 1, 0))
-        backward = [(target, source) for source, target in forward]
-        low = lax.ppermute(
-            lax.slice_in_dim(block, block.shape[dim] - width, None, axis=dim), axis, forward
-        )
-        high = lax.ppermute(lax.slice_in_dim(block, 0, width, axis=dim), axis, backward)
-        block = jnp.concatenate([low, block, high], axis=dim)
-    return block
-
-
 def halo_parts(block):
     parts = []
     for axis, dim in (("circ", 1), ("span", 2)):
@@ -42,16 +28,6 @@
     parts[2] = parts[2] * (span_index != 0).astype(block.dtype)
     parts[3] = parts[3] * (span_index != span_last).astype(block.dtype)
     return parts
-
-
-def lateral_of(block, parts):
-    circ_low, circ_high, span_low, span_high = parts
-    return (
-        jnp.concatenate([block[:, 1:], circ_high], axis=1),
-        jnp.concatenate([circ_low, block[:, :-1]], axis=1),
-        jnp.concatenate([block[:, :, 1:], span_high], axis=2),
-        jnp.concatenate([span_low, block[:, :, :-1]], axis=2),
-    )
 
 
 def stencil_kernel(j_ref, c_ref, cu_ref, cd_ref, su_ref, sd_ref, prev_ref, rate_ref, inlet_ref, out_ref):
@@ -135,47 +111,6 @@
     return total
 
 
-def update(current, previous, rate_cells, neighbours, jacobians):
-    circ_up, circ_down, span_up, span_down, axial_up, axial_down = neighbours
-    convection = contract(jacobians[0], circ_up - circ_down)
-    convection = convection + contract(jacobians[1], span_up - span_down)
-    convection = convection + contract(jacobians[2], axial_up - axial_down)
-    laplacian = (
-        circ_up + circ_down + (span_up + span_down) + (axial_up + axial_down) - 6.0 * current
-    )
-    residual = inv_step * (current - previous) + 0.5 * convection - viscosity * laplacian
-    return current - rate_cells[None] * residual
-
-
-def lateral(padded):
-    return (
-        padded[:, 2:, 1:-1],
-        padded[:, :-2, 1:-1],
-        padded[:, 1:-1, 2:],
-        padded[:, 1:-1, :-2],
-    )
-
-
-def advance(padded, current, previous, rate_cells, jacobians):
-    zero_column = jnp.zeros_like(current[..., :1])
-    axial_up = jnp.concatenate([current[..., 1:], zero_column], axis=-1)
-    axial_down = jnp.concatenate([zero_column, current[..., :-1]], axis=-1)
-    neighbours = lateral(padded) + (axial_up, axial_down)
-    return update(current, previous, rate_cells, neighbours, jacobians)
-
-
-def wall_zero(field_array, width):
-    span_index = lax.axis_index("span")
-    span_count = lax.axis_size("span")
-    length = field_array.shape[2]
-    position = jnp.arange(length, dtype=jnp.int32)
-    at_hub = jnp.logical_and(span_index == 0, position < width)
-    at_tip = jnp.logical_and(span_index == span_count - 1, position >= length - width)
-    keeping = jnp.logical_not(jnp.logical_or(at_hub, at_tip)).astype(field_array.dtype)
-    keeping = keeping.reshape(1, 1, length, 1)
-    return field_array * keeping
-
-
 def body(
     q_old, pseudo_rate, flux_jacobians, rotor_face, offsets, owners, slots, weight_idx, weight_table
 ):
@@ -210,7 +145,8 @@
 
     inlet_column = inlet_plane[..., None]
     contributions, q_for_halo = lax.optimization_barrier((contributions, q_old))
-    mid, _ = sweep(q_old, q_old, pseudo_rate, inlet_column, flux_jacobians, halo_parts(q_for_halo))
+    old_parts = halo_parts(q_for_halo)
+    mid, _ = sweep(q_old, q_old, pseudo_rate, inlet_column, flux_jacobians, old_parts)
     mid_parts = halo_parts(mid)
     zero_parts = [jnp.zeros_like(p) for p in mid_parts]
     new, _ = sweep(mid, q_old, pseudo_rate, inlet_column, flux_jacobians, zero_parts)
@@ -219,11 +155,24 @@
     from_low = lambda d: 0.5 * flux_jacobians[d] + viscosity * eye
     from_high = lambda d: viscosity * eye - 0.5 * flux_jacobians[d]
     rate = pseudo_rate[None]
-    new = new.at[:, :1].add(rate[:, :1] * contract(from_low(0), circ_low))
-    new = new.at[:, -1:].add(rate[:, -1:] * contract(from_high(0), circ_high))
-    new = new.at[:, :, :1].add(rate[:, :, :1] * contract(from_low(1), span_low))
-    new = new.at[:, :, -1:].add(rate[:, :, -1:] * contract(from_high(1), span_high))
-    return new
+    rows, span = q_old.shape[1], q_old.shape[2]
+    circ_terms = jnp.concatenate(
+        [
+            rate[:, :1] * contract(from_low(0), circ_low),
+            jnp.zeros((NF, rows - 2) + q_old.shape[2:], q_old.dtype),
+            rate[:, -1:] * contract(from_high(0), circ_high),
+        ],
+        axis=1,
+    )
+    span_terms = jnp.concatenate(
+        [
+            rate[:, :, :1] * contract(from_low(1), span_low),
+            jnp.zeros((NF, rows, span - 2, q_old.shape[3]), q_old.dtype),
+            rate[:, :, -1:] * contract(from_high(1), span_high),
+        ],
+        axis=2,
+    )
+    return new + circ_terms + span_terms
 
 
 def solution(mesh):

time: 96.8 us -> 91.8 us (0.948)
  the two profiles are of different devices: /device:TPU:6 before, /device:TPU:16 now
where the time goes in v5:
time: 91.8 us; the launch traced here: 91.1 us
  starting transfers between devices  33.5 us (36%)
  local copies, waits for them, and re-layouts  19.1 us (21%)
  Pallas kernels  18.1 us (20%)
  other arithmetic  10.6 us (12%)
  waiting for transfers between devices  7.25 us (8%)
  matrix products  2.31 us (3%)
    pallas_call x2, Pallas kernels, sweep(): pl.pallas_call(stencil_kernel, grid=(rows,), in_specs=[pl.BlockSpec(memor...  18.1 us
    ppermute x4, starting transfers between devices, halo_parts(): high = lax.ppermute(lax.slice_in_dim(block, 0, 1, axis=dim), axis, backward)  17 us
    all_to_all x1, starting transfers between devices, body(): received = lax.all_to_all(contributions, 'span', 0, 0, tiled=True)  9.19 us
    ppermute x4, waiting for transfers between devices, halo_parts(): lax.ppermute(lax.slice_in_dim(block, block.shape[dim] - 1, None, axis=dim...  7.23 us
    all_to_all x1, starting transfers between devices, body(): gathered = lax.all_to_all(copies, 'circ', 0, 0, tiled=True)  5.02 us
    slice x2, local copies, waits for them, and re-layouts, sweep(): span_down = jnp.concatenate([span_low, current[:, :, :-1]], axis=2)  3.45 us
    slice x4, local copies, waits for them, and re-layouts, halo_parts(): lax.slice_in_dim(block, block.shape[dim] - 1, None, axis=dim)  2.98 us
    concatenate x2, other arithmetic, sweep(): padded = jnp.concatenate([circ_low, current, circ_high], axis=1)  2.97 us
  transfers between devices with their start and end apart: 10, of which 1 were waited for; matrix products, arithmetic and copies ran while one was open for 24% of the time, Pallas kernels for 10%

profile of v5, /device:TPU:16, one launch (start us, length us, event | category | flops | bytes accessed | tf_op | source)
XLA Modules:
  0.0 91.1 jit_solution(2838316314869673255)
XLA Ops:
  0.0 1.3 %broadcast_in_dim.67 = f32[8,5,4,128]{3,2,1,0:T(4,128)} broadcast(f32[5,4,128]{2,1,0:T(4,128)} %param.12), dimensions={1,2,3} | broadcast | bytes 92160 | tf_op jit(solution)/shard_map/broadcast_in_dim | solution.py:121
  1.3 5.0 %all-to-all-start = ((f32[8,5,4,128]{3,2,1,0:T(4,128)}), f32[8,5,4,128]{3,2,1,0:T(4,128)S(1)}, u32[]{:S(2)}, u32[]{:S(2)}) async-start(f32[8,5,4,128]{3,2,1,0:T(4,128)} %broadcast_in_dim.67), calls=%async_computation | async-start | bytes 163840 | tf_op jit(solution)/shard_map/all_to_all | solution.py:122
  11.6 3.2 %fusion.10 = (f32[5,4,127,128]{3,2,1,0:T(8,128)}, f32[5,4,127,128]{3,2,1,0:T(8,128)S(1)}) fusion(f32[5,4,128,128]{3,2,1,0:T(8,128)} %prev_ref.3), kind=kLoop, calls=%fused_computation.76 | loop fusion | bytes 5201920 | tf_op jit(solution)/shard_map/slice | solution.py:82
  15.7 2.3 %fusion.1 = f32[5,4,32,32,4]{3,2,4,1,0:T(8,128)} fusion(f32[32,4,4,1,1]{0,2,1,4,3:T(4,128)S(1)} %copy.42, f32[5,4,4,32,1]{3,2,1,0,4:T(4,128)S(1)} %reshape.371), kind=kOutput, calls=%fused_computation.21 | convolution fusion | flops 3932160 | bytes 339968 | tf_op jit(solution)/shard_map/ogk,ftkp->oftgp/dot_general | solution.py:140
  18.9 2.4 %copy.36 = f32[32,5,4,128]{3,2,1,0:T(4,128)} copy(f32[32,5,4,128]{0,3,2,1:T(8,128)} %bitcast.63) | data formatting | bytes 655360 | tf_op jit(solution)/shard_map/reshape | solution.py:142
  21.4 5.3 %collective-permute-start.2 = (f32[5,4,1,128]{3,2,1,0:T(1,128)S(1)}, f32[5,4,1,128]{3,2,1,0:T(1,128)S(1)}, u32[]{:S(2)}, u32[]{:S(2)}) collective-permute-start(f32[5,4,1,128]{3,2,1,0:T(1,128)S(1)} %get-tuple-element.34), channel_id=1, source_target_pairs={{1,0},{2,1},{3,2},{4,3},{5,4},{6,5},{7,6},{8,7},{9,8},{10,9},{11,1... | collective-permute-start | bytes 30728 | tf_op jit(solution)/shard_map/ppermute | solution.py:24
  26.7 9.2 %all-to-all-start.1 = ((f32[32,5,4,128]{3,2,1,0:T(4,128)}), f32[32,5,4,128]{3,2,1,0:T(4,128)S(1)}, u32[]{:S(2)}, u32[]{:S(2)}) async-start(f32[32,5,4,128]{3,2,1,0:T(4,128)} %copy.36), calls=%async_computation.1 | async-start | bytes 655360 | tf_op jit(solution)/shard_map/all_to_all | solution.py:143
  35.9 2.1 %collective-permute-start = (f32[5,1,128,128]{3,2,1,0:T(8,128)}, f32[5,1,128,128]{3,2,1,0:T(8,128)S(1)}, u32[]{:S(2)}, u32[]{:S(2)}) collective-permute-start(f32[5,1,128,128]{3,2,1,0:T(8,128)} %get-tuple-element.37), channel_id=1, source_target_pairs={{0,32},{32,64},{64,96},{96,128},{128,160},{160,192},{192,224},{224... | collective-permute-start | bytes 983048 | tf_op jit(solution)/shard_map/ppermute | solution.py:23
  38.0 2.2 %collective-permute-start.1 = (f32[5,1,128,128]{3,2,1,0:T(8,128)S(1)}, f32[5,1,128,128]{3,2,1,0:T(8,128)S(1)}, u32[]{:S(2)}, u32[]{:S(2)}) collective-permute-start(f32[5,1,128,128]{3,2,1,0:T(8,128)S(1)} %get-tuple-element.38), channel_id=1, source_target_pairs={{32,0},{64,32},{96,64},{128,96},{160,128},{192,160},{224,192},{0,2... | collective-permute-start | bytes 983048 | tf_op jit(solution)/shard_map/ppermute | solution.py:24
  40.2 2.5 %pad_maximum_fusion.3.sd_ref = f32[5,4,128,128]{3,2,1,0:T(8,128)} fusion(f32[5,4,127,128]{3,2,1,0:T(8,128)} %get-tuple-element.35, f32[5,4,1,128]{3,2,1,0:T(1,128)S(1)} %broadcast_multiply_fusion.1), kind=kLoop, calls=%fused_computation.3 | loop fusion | flops 327680 | bytes 2621440 | tf_op jit(solution)/shard_map/concatenate | solution.py:82
  42.8 1.2 %pad_maximum_fusion.2.su_ref = f32[5,4,128,128]{3,2,1,0:T(8,128)} fusion(f32[5,4,1,128]{3,2,1,0:T(1,128)S(1)} %broadcast_multiply_fusion.3, f32[5,4,127,128]{3,2,1,0:T(8,128)S(1)} %get-tuple-element.36), kind=kLoop, calls=%fused_computation.2 | loop fusion | flops 327680 | bytes 2621440 | tf_op jit(solution)/shard_map/concatenate | solution.py:81
  43.9 7.2 %collective-permute-done = f32[5,1,128,128]{3,2,1,0:T(8,128)S(1)} collective-permute-done((f32[5,1,128,128]{3,2,1,0:T(8,128)}, f32[5,1,128,128]{3,2,1,0:T(8,128)S(1)}, u32[]{:S(2)}, u32[]{:S(2)}) %collective-permute-start) | collective-permute-done | bytes 327712 | tf_op jit(solution)/shard_map/ppermute | solution.py:23
  51.2 1.4 %pad_maximum_fusion.c_ref.cu_ref.cd_ref = f32[5,6,128,128]{3,2,1,0:T(8,128)} fusion(f32[5,1,128,128]{3,2,1,0:T(8,128)S(1)} %collective-permute-done.1, f32[5,4,128,128]{3,2,1,0:T(8,128)S(1)} %copy-done, f32[5,1,128,128]{3,2,1,0:T(8,128)S(1)} %collective-permute-done), kind=kLoop, calls=%fused_computation | loop fusion | flops 983040 | bytes 3932160 | tf_op jit(solution)/shard_map/concatenate | solution.py:80
  52.7 1.5 %copy.37.inlet_ref = f32[5,4,128,1]{3,2,1,0:T(8,128)} copy(f32[5,4,128,1]{2,1,0,3:T(4,128)S(1)} %bitcast.67) | data formatting | bytes 20480 | tf_op jit(solution)/shard_map/broadcast_in_dim | solution.py:146
  54.2 9.0 %shard_map.91 = f32[5,4,128,128]{3,2,1,0:T(8,128)} custom-call(f32[75]{0:T(128)} %reshape.367.j_ref, f32[5,6,128,128]{3,2,1,0:T(8,128)} %pad_maximum_fusion.c_ref.cu_ref.cd_ref, f32[5,6,128,128]{3,2,1,0:T(8,128)} %pad_maximum_fusion.c_ref.cu_ref.cd_ref, f32[5,6,128,128]{3,2,1,0:T(8,128)} %pad_maximum_fusion.c_ref.cu_ref.cd_ref, ...), custom_call_target="tpu_custom_call" | custom-call | tf_op jit(solution)/shard_map/pallas_call | solution.py:86
  63.2 1.0 %fusion.6 = (f32[5,4,1,128]{3,2,1,0:T(1,128)S(1)}, f32[5,4,1,128]{3,2,1,0:T(1,128)S(1)}) fusion(f32[5,4,128,128]{3,2,1,0:T(8,128)} %shard_map.91), kind=kLoop, calls=%fused_computation.72 | loop fusion | bytes 40960 | tf_op jit(solution)/shard_map/slice | solution.py:23
  64.3 1.1 %fusion.7 = (f32[5,1,128,128]{3,2,1,0:T(8,128)S(1)}, f32[5,1,128,128]{3,2,1,0:T(8,128)S(1)}) fusion(f32[5,4,128,128]{3,2,1,0:T(8,128)} %shard_map.91), kind=kLoop, calls=%fused_computation.73 | loop fusion | bytes 1310720 | tf_op jit(solution)/shard_map/slice | solution.py:23
  65.8 5.3 %collective-permute-start.7 = (f32[5,4,1,128]{3,2,1,0:T(1,128)S(1)}, f32[5,4,1,128]{3,2,1,0:T(1,128)S(1)}, u32[]{:S(2)}, u32[]{:S(2)}) collective-permute-start(f32[5,4,1,128]{3,2,1,0:T(1,128)S(1)} %get-tuple-element.28), channel_id=1, source_target_pairs={{1,0},{2,1},{3,2},{4,3},{5,4},{6,5},{7,6},{8,7},{9,8},{10,9},{11,1... | collective-permute-start | bytes 30728 | tf_op jit(solution)/shard_map/ppermute | solution.py:24
  71.1 4.1 %collective-permute-start.5 = (f32[5,1,128,128]{3,2,1,0:T(8,128)S(1)}, f32[5,1,128,128]{3,2,1,0:T(8,128)S(1)}, u32[]{:S(2)}, u32[]{:S(2)}) collective-permute-start(f32[5,1,128,128]{3,2,1,0:T(8,128)S(1)} %get-tuple-element.30), channel_id=1, source_target_pairs={{32,0},{64,32},{96,64},{128,96},{160,128},{192,160},{224,192},{0,2... | collective-permute-start | bytes 983048 | tf_op jit(solution)/shard_map/ppermute | solution.py:24
  75.3 1.5 %pad_maximum_fusion.1.c_ref.cu_ref.cd_ref = f32[5,6,128,128]{3,2,1,0:T(8,128)} fusion(f32[5,1,128,128]{3,2,1,0:T(8,128)S(1)} %broadcast.530, f32[5,4,128,128]{3,2,1,0:T(8,128)S(1)} %copy-done.1), kind=kLoop, calls=%fused_computation.1 | loop fusion | flops 983040 | bytes 3604480 | tf_op jit(solution)/shard_map/concatenate | solution.py:80
  76.9 1.2 %concatenate.29.sd_ref = f32[5,4,128,128]{3,2,1,0:T(8,128)} pad(f32[5,4,127,128]{3,2,1,0:T(8,128)S(1)} %get-tuple-element.31, f32[]{:T(128)} %constant.15.clone.1), padding=0_0x0_0x1_0x0_0 | pad | bytes 2611204 | tf_op jit(solution)/shard_map/concatenate | solution.py:82
  78.0 1.2 %concatenate.28.su_ref = f32[5,4,128,128]{3,2,1,0:T(8,128)} pad(f32[5,4,127,128]{3,2,1,0:T(8,128)S(1)} %get-tuple-element.32, f32[]{:T(128)} %constant.15.clone.1), padding=0_0x0_0x0_1x0_0 | pad | bytes 2611204 | tf_op jit(solution)/shard_map/concatenate | solution.py:81
  79.2 9.0 %shard_map.92 = f32[5,4,128,128]{3,2,1,0:T(8,128)} custom-call(f32[75]{0:T(128)} %reshape.367.j_ref, f32[5,6,128,128]{3,2,1,0:T(8,128)} %pad_maximum_fusion.1.c_ref.cu_ref.cd_ref, f32[5,6,128,128]{3,2,1,0:T(8,128)} %pad_maximum_fusion.1.c_ref.cu_ref.cd_ref, f32[5,6,128,128]{3,2,1,0:T(8,128)} %pad_maximum_fusion.1.c_ref.cu_ref.cd_ref, ...), custom_call_target="tpu_custom_call" | custom-call | tf_op jit(solution)/shard_map/pallas_call | solution.py:86
  89.8 1.3 %fusion = f32[5,4,128,128]{3,2,1,0:T(8,128)} fusion(f32[5,4,128,128]{3,2,1,0:T(8,128)S(1)} %copy-done.2, f32[5,1,128,128]{3,2,1,0:T(8,128)S(1)} %add_multiply_fusion, f32[5,1,128,128]{3,2,1,0:T(8,128)S(1)} %add_multiply_fusion.1, f32[5,4,1,128]{3,2,1,0:T(1,128)S(1)} %add_multiply_fusion.2, f32[5,4,1,128]{3,2,1,0:T(1,128)S(1)} %add_multiply_fusion.3, ...), kind=kLoop, calls=%fused_computation.5 | loop fusion | flops 1966080 | bytes 3297808 | tf_op jit(solution)/shard_map/add | solution.py:175
  (61 shorter events, 9.0 us)
Async XLA Ops:
  1.3 14.2 %all-to-all-start = ((f32[8,5,4,128]{3,2,1,0:T(4,128)}), f32[8,5,4,128]{3,2,1,0:T(4,128)S(1)}, u32[]{:S(2)}, u32[]{:S(2)}) async-start(f32[8,5,4,128]{3,2,1,0:T(4,128)} %broadcast_in_dim.67), calls=%async_computation | async-start | bytes 163840 | tf_op jit(solution)/shard_map/all_to_all | solution.py:122
  11.6 3.2 %copy-start.3 = (s32[128]{0:T(128)S(1)}, s32[128]{0:T(128)}, u32[]{:S(2)}) copy-start(s32[128]{0:T(128)} %param.13) | copy-start | bytes 1540
  14.8 3.2 %copy-start = (f32[5,4,128,128]{3,2,1,0:T(8,128)S(1)}, f32[5,4,128,128]{3,2,1,0:T(8,128)}, u32[]{:S(2)}) copy-start(f32[5,4,128,128]{3,2,1,0:T(8,128)} %prev_ref.3) | copy-start | bytes 3932164
  18.0 22.2 %collective-permute-start.3 = (f32[5,4,1,128]{3,2,1,0:T(1,128)S(1)}, f32[5,4,1,128]{3,2,1,0:T(1,128)S(1)}, u32[]{:S(2)}, u32[]{:S(2)}) collective-permute-start(f32[5,4,1,128]{3,2,1,0:T(1,128)S(1)} %get-tuple-element.33), channel_id=1, source_target_pairs={{0,1},{1,2},{2,3},{3,4},{4,5},{5,6},{6,7},{7,8},{8,9},{9,10},{10,1... | collective-permute-start | bytes 30728 | tf_op jit(solution)/shard_map/ppermute | solution.py:23
  21.4 18.9 %collective-permute-start.2 = (f32[5,4,1,128]{3,2,1,0:T(1,128)S(1)}, f32[5,4,1,128]{3,2,1,0:T(1,128)S(1)}, u32[]{:S(2)}, u32[]{:S(2)}) collective-permute-start(f32[5,4,1,128]{3,2,1,0:T(1,128)S(1)} %get-tuple-element.34), channel_id=1, source_target_pairs={{1,0},{2,1},{3,2},{4,3},{5,4},{6,5},{7,6},{8,7},{9,8},{10,9},{11,1... | collective-permute-start | bytes 30728 | tf_op jit(solution)/shard_map/ppermute | solution.py:24
  26.7 25.9 %all-to-all-start.1 = ((f32[32,5,4,128]{3,2,1,0:T(4,128)}), f32[32,5,4,128]{3,2,1,0:T(4,128)S(1)}, u32[]{:S(2)}, u32[]{:S(2)}) async-start(f32[32,5,4,128]{3,2,1,0:T(4,128)} %copy.36), calls=%async_computation.1 | async-start | bytes 655360 | tf_op jit(solution)/shard_map/all_to_all | solution.py:143
  35.9 15.3 %collective-permute-start = (f32[5,1,128,128]{3,2,1,0:T(8,128)}, f32[5,1,128,128]{3,2,1,0:T(8,128)S(1)}, u32[]{:S(2)}, u32[]{:S(2)}) collective-permute-start(f32[5,1,128,128]{3,2,1,0:T(8,128)} %get-tuple-element.37), channel_id=1, source_target_pairs={{0,32},{32,64},{64,96},{96,128},{128,160},{160,192},{192,224},{224... | collective-permute-start | bytes 983048 | tf_op jit(solution)/shard_map/ppermute | solution.py:23
  38.0 13.2 %collective-permute-start.1 = (f32[5,1,128,128]{3,2,1,0:T(8,128)S(1)}, f32[5,1,128,128]{3,2,1,0:T(8,128)S(1)}, u32[]{:S(2)}, u32[]{:S(2)}) collective-permute-start(f32[5,1,128,128]{3,2,1,0:T(8,128)S(1)} %get-tuple-element.38), channel_id=1, source_target_pairs={{32,0},{64,32},{96,64},{128,96},{160,128},{192,160},{224,192},{0,2... | collective-permute-start | bytes 983048 | tf_op jit(solution)/shard_map/ppermute | solution.py:24
  63.2 2.2 %copy-start.1 = (f32[5,4,128,128]{3,2,1,0:T(8,128)S(1)}, f32[5,4,128,128]{3,2,1,0:T(8,128)}, u32[]{:S(2)}) copy-start(f32[5,4,128,128]{3,2,1,0:T(8,128)} %shard_map.91) | copy-start | bytes 3932164
  65.7 22.5 %collective-permute-start.6 = (f32[5,4,1,128]{3,2,1,0:T(1,128)S(1)}, f32[5,4,1,128]{3,2,1,0:T(1,128)S(1)}, u32[]{:S(2)}, u32[]{:S(2)}) collective-permute-start(f32[5,4,1,128]{3,2,1,0:T(1,128)S(1)} %get-tuple-element.27), channel_id=1, source_target_pairs={{0,1},{1,2},{2,3},{3,4},{4,5},{5,6},{6,7},{7,8},{8,9},{9,10},{10,1... | collective-permute-start | bytes 30728 | tf_op jit(solution)/shard_map/ppermute | solution.py:23
  65.8 22.6 %collective-permute-start.7 = (f32[5,4,1,128]{3,2,1,0:T(1,128)S(1)}, f32[5,4,1,128]{3,2,1,0:T(1,128)S(1)}, u32[]{:S(2)}, u32[]{:S(2)}) collective-permute-start(f32[5,4,1,128]{3,2,1,0:T(1,128)S(1)} %get-tuple-element.28), channel_id=1, source_target_pairs={{1,0},{2,1},{3,2},{4,3},{5,4},{6,5},{7,6},{8,7},{9,8},{10,9},{11,1... | collective-permute-start | bytes 30728 | tf_op jit(solution)/shard_map/ppermute | solution.py:24
  71.1 17.4 %collective-permute-start.4 = (f32[5,1,128,128]{3,2,1,0:T(8,128)S(1)}, f32[5,1,128,128]{3,2,1,0:T(8,128)S(1)}, u32[]{:S(2)}, u32[]{:S(2)}) collective-permute-start(f32[5,1,128,128]{3,2,1,0:T(8,128)S(1)} %get-tuple-element.29), channel_id=1, source_target_pairs={{0,32},{32,64},{64,96},{96,128},{128,160},{160,192},{192,224},{224... | collective-permute-start | bytes 983048 | tf_op jit(solution)/shard_map/ppermute | solution.py:23
  71.1 17.6 %collective-permute-start.5 = (f32[5,1,128,128]{3,2,1,0:T(8,128)S(1)}, f32[5,1,128,128]{3,2,1,0:T(8,128)S(1)}, u32[]{:S(2)}, u32[]{:S(2)}) collective-permute-start(f32[5,1,128,128]{3,2,1,0:T(8,128)S(1)} %get-tuple-element.30), channel_id=1, source_target_pairs={{32,0},{64,32},{96,64},{128,96},{160,128},{192,160},{224,192},{0,2... | collective-permute-start | bytes 983048 | tf_op jit(solution)/shard_map/ppermute | solution.py:24
  88.5 1.3 %copy-start.2 = (f32[5,4,128,128]{3,2,1,0:T(8,128)S(1)}, f32[5,4,128,128]{3,2,1,0:T(8,128)}, u32[]{:S(2)}) copy-start(f32[5,4,128,128]{3,2,1,0:T(8,128)} %shard_map.92) | copy-start | bytes 3932164

commit v6 on v5

--- a/solution.py
+++ b/solution.py
@@ -28,6 +28,12 @@
     parts[2] = parts[2] * (span_index != 0).astype(block.dtype)
     parts[3] = parts[3] * (span_index != span_last).astype(block.dtype)
     return parts
+
+
+def halo_shapes(block):
+    nf, rows, span, axial = block.shape
+    shapes = [(nf, 1, span, axial)] * 2 + [(nf, rows, 1, axial)] * 2
+    return [jnp.zeros(shape, block.dtype) for shape in shapes]
 
 
 def stencil_kernel(j_ref, c_ref, cu_ref, cd_ref, su_ref, sd_ref, prev_ref, rate_ref, inlet_ref, out_ref):
@@ -144,22 +150,27 @@
     inlet_plane = jnp.sum(received, axis=0)
 
     inlet_column = inlet_plane[..., None]
-    contributions, q_for_halo = lax.optimization_barrier((contributions, q_old))
-    old_parts = halo_parts(q_for_halo)
-    mid, _ = sweep(q_old, q_old, pseudo_rate, inlet_column, flux_jacobians, old_parts)
-    mid_parts = halo_parts(mid)
-    zero_parts = [jnp.zeros_like(p) for p in mid_parts]
+    zero_parts = halo_shapes(q_old)
+    mid, _ = sweep(q_old, q_old, pseudo_rate, inlet_column, flux_jacobians, zero_parts)
+    mid, q_for_halo = lax.optimization_barrier((mid, q_old))
+    mid = mid + boundary_terms(halo_parts(q_for_halo), pseudo_rate, flux_jacobians)
     new, _ = sweep(mid, q_old, pseudo_rate, inlet_column, flux_jacobians, zero_parts)
-    circ_low, circ_high, span_low, span_high = mid_parts
-    eye = jnp.eye(NF, dtype=q_old.dtype)
-    from_low = lambda d: 0.5 * flux_jacobians[d] + viscosity * eye
-    from_high = lambda d: viscosity * eye - 0.5 * flux_jacobians[d]
-    rate = pseudo_rate[None]
-    rows, span = q_old.shape[1], q_old.shape[2]
+    new, mid_for_halo = lax.optimization_barrier((new, mid))
+    return new + boundary_terms(halo_parts(mid_for_halo), pseudo_rate, flux_jacobians)
+
+
+def boundary_terms(parts, rate_cells, jacobians):
+    circ_low, circ_high, span_low, span_high = parts
+    nf, _, span, axial = circ_low.shape
+    rows = span_low.shape[1]
+    eye = jnp.eye(nf, dtype=circ_low.dtype)
+    from_low = lambda d: 0.5 * jacobians[d] + viscosity * eye
+    from_high = lambda d: viscosity * eye - 0.5 * jacobians[d]
+    rate = rate_cells[None]
     circ_terms = jnp.concatenate(
         [
             rate[:, :1] * contract(from_low(0), circ_low),
-            jnp.zeros((NF, rows - 2) + q_old.shape[2:], q_old.dtype),
+            jnp.zeros((nf, rows - 2, span, axial), circ_low.dtype),
             rate[:, -1:] * contract(from_high(0), circ_high),
         ],
         axis=1,
@@ -167,12 +178,12 @@
     span_terms = jnp.concatenate(
         [
             rate[:, :, :1] * contract(from_low(1), span_low),
-            jnp.zeros((NF, rows, span - 2, q_old.shape[3]), q_old.dtype),
+            jnp.zeros((nf, rows, span - 2, axial), circ_low.dtype),
             rate[:, :, -1:] * contract(from_high(1), span_high),
         ],
         axis=2,
     )
-    return new + circ_terms + span_terms
+    return circ_terms + span_terms
 
 
 def solution(mesh):

time: 91.8 us -> 102 us (1.11)
  the two profiles are of different devices: /device:TPU:16 before, /device:TPU:6 now
where the time goes in v6:
time: 102 us; the launch traced here: 101 us
  starting transfers between devices  32 us (31%)
  waiting for transfers between devices  24.8 us (24%)
  Pallas kernels  18.2 us (18%)
  local copies, waits for them, and re-layouts  15.8 us (15%)
  other arithmetic  7.7 us (8%)
  matrix products  2.31 us (2%)
    pallas_call x2, Pallas kernels, sweep(): pl.pallas_call(stencil_kernel, grid=(rows,), in_specs=[pl.BlockSpec(memor...  18.2 us
    ppermute x4, starting transfers between devices, halo_parts(): high = lax.ppermute(lax.slice_in_dim(block, 0, 1, axis=dim), axis, backward)  13.8 us
    all_to_all x1, starting transfers between devices, body(): received = lax.all_to_all(contributions, 'span', 0, 0, tiled=True)  11.2 us
    all_to_all x1, waiting for transfers between devices, body(): received = lax.all_to_all(contributions, 'span', 0, 0, tiled=True)  10.4 us
    ppermute x4, waiting for transfers between devices, halo_parts(): lax.ppermute(lax.slice_in_dim(block, block.shape[dim] - 1, None, axis=dim...  9.5 us
    all_to_all x1, starting transfers between devices, body(): gathered = lax.all_to_all(copies, 'circ', 0, 0, tiled=True)  5.79 us
    ppermute x4, waiting for transfers between devices, halo_parts(): high = lax.ppermute(lax.slice_in_dim(block, 0, 1, axis=dim), axis, backward)  4.86 us
    concatenate x2, other arithmetic, sweep(): padded = jnp.concatenate([circ_low, current, circ_high], axis=1)  2.98 us
  transfers between devices with their start and end apart: 10, of which 5 were waited for; matrix products, arithmetic and copies ran while one was open for 11% of the time, Pallas kernels for 0%

profile of v6, /device:TPU:6, one launch (start us, length us, event | category | flops | bytes accessed | tf_op | source)
XLA Modules:
  0.0 101.2 jit_solution(12820584427353139549)
XLA Ops:
  0.0 1.3 %broadcast_in_dim.62 = f32[8,5,4,128]{3,2,1,0:T(4,128)} broadcast(f32[5,4,128]{2,1,0:T(4,128)} %param.12), dimensions={1,2,3} | broadcast | bytes 92160 | tf_op jit(solution)/shard_map/broadcast_in_dim | solution.py:127
  1.3 5.8 %all-to-all-start = ((f32[8,5,4,128]{3,2,1,0:T(4,128)}), f32[8,5,4,128]{3,2,1,0:T(4,128)S(1)}, u32[]{:S(2)}, u32[]{:S(2)}) async-start(f32[8,5,4,128]{3,2,1,0:T(4,128)} %broadcast_in_dim.62), calls=%async_computation | async-start | bytes 163840 | tf_op jit(solution)/shard_map/all_to_all | solution.py:128
  9.7 2.1 %fusion.12 = (f32[5,4,127,128]{3,2,1,0:T(8,128)S(1)}, f32[5,4,127,128]{3,2,1,0:T(8,128)S(1)}) fusion(f32[5,4,128,128]{3,2,1,0:T(8,128)} %prev_ref.3), kind=kLoop, calls=%fused_computation.93 | loop fusion | bytes 5201920 | tf_op jit(solution)/shard_map/slice | solution.py:88
  12.7 2.3 %fusion.2 = f32[5,4,32,32,4]{3,2,4,1,0:T(8,128)} fusion(f32[32,4,4,1,1]{0,2,1,4,3:T(4,128)S(1)} %copy.42, f32[5,4,4,32,1]{3,2,1,0,4:T(4,128)S(1)} %reshape.571), kind=kOutput, calls=%fused_computation.35 | convolution fusion | flops 3932160 | bytes 339968 | tf_op jit(solution)/shard_map/ogk,ftkp->oftgp/dot_general | solution.py:146
  15.0 2.4 %copy.36 = f32[32,5,4,128]{3,2,1,0:T(4,128)} copy(f32[32,5,4,128]{0,3,2,1:T(8,128)} %bitcast.93) | data formatting | bytes 655360 | tf_op jit(solution)/shard_map/reshape | solution.py:148
  17.4 11.2 %all-to-all-start.1 = ((f32[32,5,4,128]{3,2,1,0:T(4,128)}), f32[32,5,4,128]{3,2,1,0:T(4,128)S(1)}, u32[]{:S(2)}, u32[]{:S(2)}) async-start(f32[32,5,4,128]{3,2,1,0:T(4,128)} %copy.36), calls=%async_computation.1 | async-start | bytes 655360 | tf_op jit(solution)/shard_map/all_to_all | solution.py:149
  29.7 1.2 %concatenate.32.sd_ref = f32[5,4,128,128]{3,2,1,0:T(8,128)} pad(f32[5,4,127,128]{3,2,1,0:T(8,128)S(1)} %get-tuple-element.43, f32[]{:T(128)} %constant.15.clone.1), padding=0_0x0_0x1_0x0_0 | pad | bytes 2611204 | tf_op jit(solution)/shard_map/concatenate | solution.py:88
  32.7 1.5 %pad_maximum_fusion.1.c_ref.cu_ref.cd_ref = f32[5,6,128,128]{3,2,1,0:T(8,128)} fusion(f32[5,1,128,128]{3,2,1,0:T(8,128)S(1)} %broadcast.912, f32[5,4,128,128]{3,2,1,0:T(8,128)S(1)} %copy-done), kind=kLoop, calls=%fused_computation.1 | loop fusion | flops 983040 | bytes 3604480 | tf_op jit(solution)/shard_map/concatenate | solution.py:86
  34.2 10.4 %all-to-all-done.1 = f32[32,5,4,128]{3,2,1,0:T(4,128)S(1)} async-done(((f32[32,5,4,128]{3,2,1,0:T(4,128)}), f32[32,5,4,128]{3,2,1,0:T(4,128)S(1)}, u32[]{:S(2)}, u32[]{:S(2)}) %all-to-all-start.1) | async-done | bytes 327712 | tf_op jit(solution)/shard_map/all_to_all | solution.py:149
  44.7 1.5 %copy.37.inlet_ref = f32[5,4,128,1]{3,2,1,0:T(8,128)} copy(f32[5,4,128,1]{2,1,0,3:T(4,128)S(1)} %bitcast.97) | data formatting | bytes 20480 | tf_op jit(solution)/shard_map/broadcast_in_dim | solution.py:152
  46.2 9.1 %shard_map.91 = f32[5,4,128,128]{3,2,1,0:T(8,128)} custom-call(f32[75]{0:T(128)} %reshape.567.j_ref, f32[5,6,128,128]{3,2,1,0:T(8,128)} %pad_maximum_fusion.1.c_ref.cu_ref.cd_ref, f32[5,6,128,128]{3,2,1,0:T(8,128)} %pad_maximum_fusion.1.c_ref.cu_ref.cd_ref, f32[5,6,128,128]{3,2,1,0:T(8,128)} %pad_maximum_fusion.1.c_ref.cu_ref.cd_ref, ...), custom_call_target="tpu_custom_call" | custom-call | tf_op jit(solution)/shard_map/pallas_call | solution.py:92
  55.5 5.4 %collective-permute-start.3 = (f32[5,4,1,128]{3,2,1,0:T(1,128)S(1)}, f32[5,4,1,128]{3,2,1,0:T(1,128)S(1)}, u32[]{:S(2)}, u32[]{:S(2)}) collective-permute-start(f32[5,4,1,128]{3,2,1,0:T(1,128)S(1)} %get-tuple-element.40), channel_id=1, source_target_pairs={{1,0},{2,1},{3,2},{4,3},{5,4},{6,5},{7,6},{8,7},{9,8},{10,9},{11,1... | collective-permute-start | bytes 30728 | tf_op jit(solution)/shard_map/ppermute | solution.py:24
  61.8 1.2 %collective-permute-start.1 = (f32[5,1,128,128]{3,2,1,0:T(8,128)S(1)}, f32[5,1,128,128]{3,2,1,0:T(8,128)S(1)}, u32[]{:S(2)}, u32[]{:S(2)}) collective-permute-start(f32[5,1,128,128]{3,2,1,0:T(8,128)S(1)} %get-tuple-element.42), channel_id=1, source_target_pairs={{32,0},{64,32},{96,64},{128,96},{160,128},{192,160},{224,192},{0,2... | collective-permute-start | bytes 983048 | tf_op jit(solution)/shard_map/ppermute | solution.py:24
  63.3 4.7 %collective-permute-done = f32[5,1,128,128]{3,2,1,0:T(8,128)S(1)} collective-permute-done((f32[5,1,128,128]{3,2,1,0:T(8,128)S(1)}, f32[5,1,128,128]{3,2,1,0:T(8,128)S(1)}, u32[]{:S(2)}, u32[]{:S(2)}) %collective-permute-start) | collective-permute-done | bytes 327712 | tf_op jit(solution)/shard_map/ppermute | solution.py:23
  68.3 2.7 %collective-permute-done.1 = f32[5,1,128,128]{3,2,1,0:T(8,128)S(1)} collective-permute-done((f32[5,1,128,128]{3,2,1,0:T(8,128)S(1)}, f32[5,1,128,128]{3,2,1,0:T(8,128)S(1)}, u32[]{:S(2)}, u32[]{:S(2)}) %collective-permute-start.1) | collective-permute-done | bytes 327712 | tf_op jit(solution)/shard_map/ppermute | solution.py:24
  71.5 1.5 %pad_maximum_fusion.c_ref.cu_ref.cd_ref = f32[5,6,128,128]{3,2,1,0:T(8,128)} fusion(f32[5,1,128,128]{3,2,1,0:T(8,128)S(1)} %broadcast.912, f32[5,4,128,128]{3,2,1,0:T(8,128)S(1)} %fusion), kind=kLoop, calls=%fused_computation | loop fusion | flops 983040 | bytes 3604480 | tf_op jit(solution)/shard_map/concatenate | solution.py:86
  73.2 1.2 %concatenate.37.sd_ref = f32[5,4,128,128]{3,2,1,0:T(8,128)} pad(f32[5,4,127,128]{3,2,1,0:T(8,128)S(1)} %get-tuple-element.37, f32[]{:T(128)} %constant.15.clone.1), padding=0_0x0_0x1_0x0_0 | pad | bytes 2611204 | tf_op jit(solution)/shard_map/concatenate | solution.py:88
  74.4 1.2 %concatenate.36.su_ref = f32[5,4,128,128]{3,2,1,0:T(8,128)} pad(f32[5,4,127,128]{3,2,1,0:T(8,128)S(1)} %get-tuple-element.38, f32[]{:T(128)} %constant.15.clone.1), padding=0_0x0_0x0_1x0_0 | pad | bytes 2611204 | tf_op jit(solution)/shard_map/concatenate | solution.py:87
  75.6 9.0 %shard_map.92 = f32[5,4,128,128]{3,2,1,0:T(8,128)} custom-call(f32[75]{0:T(128)} %reshape.567.j_ref, f32[5,6,128,128]{3,2,1,0:T(8,128)} %pad_maximum_fusion.c_ref.cu_ref.cd_ref, f32[5,6,128,128]{3,2,1,0:T(8,128)} %pad_maximum_fusion.c_ref.cu_ref.cd_ref, f32[5,6,128,128]{3,2,1,0:T(8,128)} %pad_maximum_fusion.c_ref.cu_ref.cd_ref, ...), custom_call_target="tpu_custom_call" | custom-call | tf_op jit(solution)/shard_map/pallas_call | solution.py:92
  84.8 5.4 %collective-permute-start.7 = (f32[5,4,1,128]{3,2,1,0:T(1,128)S(1)}, f32[5,4,1,128]{3,2,1,0:T(1,128)S(1)}, u32[]{:S(2)}, u32[]{:S(2)}) collective-permute-start(f32[5,4,1,128]{3,2,1,0:T(1,128)S(1)} %get-tuple-element.34), channel_id=1, source_target_pairs={{1,0},{2,1},{3,2},{4,3},{5,4},{6,5},{7,6},{8,7},{9,8},{10,9},{11,1... | collective-permute-start | bytes 30728 | tf_op jit(solution)/shard_map/ppermute | solution.py:24
  90.5 1.8 %collective-permute-start.5 = (f32[5,1,128,128]{3,2,1,0:T(8,128)S(1)}, f32[5,1,128,128]{3,2,1,0:T(8,128)S(1)}, u32[]{:S(2)}, u32[]{:S(2)}) collective-permute-start(f32[5,1,128,128]{3,2,1,0:T(8,128)S(1)} %get-tuple-element.36), channel_id=1, source_target_pairs={{32,0},{64,32},{96,64},{128,96},{160,128},{192,160},{224,192},{0,2... | collective-permute-start | bytes 983048 | tf_op jit(solution)/shard_map/ppermute | solution.py:24
  92.5 4.7 %collective-permute-done.4 = f32[5,1,128,128]{3,2,1,0:T(8,128)S(1)} collective-permute-done((f32[5,1,128,128]{3,2,1,0:T(8,128)S(1)}, f32[5,1,128,128]{3,2,1,0:T(8,128)S(1)}, u32[]{:S(2)}, u32[]{:S(2)}) %collective-permute-start.4) | collective-permute-done | bytes 327712 | tf_op jit(solution)/shard_map/ppermute | solution.py:23
  97.5 2.1 %collective-permute-done.5 = f32[5,1,128,128]{3,2,1,0:T(8,128)S(1)} collective-permute-done((f32[5,1,128,128]{3,2,1,0:T(8,128)S(1)}, f32[5,1,128,128]{3,2,1,0:T(8,128)S(1)}, u32[]{:S(2)}, u32[]{:S(2)}) %collective-permute-start.5) | collective-permute-done | bytes 327712 | tf_op jit(solution)/shard_map/ppermute | solution.py:24
  99.9 1.3 %fusion.1 = f32[5,4,128,128]{3,2,1,0:T(8,128)} fusion(f32[5,4,128,128]{3,2,1,0:T(8,128)S(1)} %copy-done.2, f32[5,1,128,128]{3,2,1,0:T(8,128)S(1)} %add_multiply_fusion, f32[5,1,128,128]{3,2,1,0:T(8,128)S(1)} %add_multiply_fusion.1, f32[5,4,1,128]{3,2,1,0:T(1,128)S(1)} %add_multiply_fusion.4, f32[5,4,1,128]{3,2,1,0:T(1,128)S(1)} %add_multiply_fusion.5, ...), kind=kLoop, calls=%fused_computation.7 | loop fusion | flops 1966080 | bytes 3297808 | tf_op jit(solution)/shard_map/add | solution.py:159
  (74 shorter events, 9.7 us)
Async XLA Ops:
  1.3 11.2 %all-to-all-start = ((f32[8,5,4,128]{3,2,1,0:T(4,128)}), f32[8,5,4,128]{3,2,1,0:T(4,128)S(1)}, u32[]{:S(2)}, u32[]{:S(2)}) async-start(f32[8,5,4,128]{3,2,1,0:T(4,128)} %broadcast_in_dim.62), calls=%async_computation | async-start | bytes 163840 | tf_op jit(solution)/shard_map/all_to_all | solution.py:128
  9.7 2.1 %copy-start.5 = (s32[128]{0:T(128)S(1)}, s32[128]{0:T(128)}, u32[]{:S(2)}) copy-start(s32[128]{0:T(128)} %param.13) | copy-start | bytes 1540
  17.4 27.2 %all-to-all-start.1 = ((f32[32,5,4,128]{3,2,1,0:T(4,128)}), f32[32,5,4,128]{3,2,1,0:T(4,128)S(1)}, u32[]{:S(2)}, u32[]{:S(2)}) async-start(f32[32,5,4,128]{3,2,1,0:T(4,128)} %copy.36), calls=%async_computation.1 | async-start | bytes 655360 | tf_op jit(solution)/shard_map/all_to_all | solution.py:149
  30.9 1.8 %copy-start = (f32[5,4,128,128]{3,2,1,0:T(8,128)S(1)}, f32[5,4,128,128]{3,2,1,0:T(8,128)}, u32[]{:S(2)}) copy-start(f32[5,4,128,128]{3,2,1,0:T(8,128)} %prev_ref.3) | copy-start | bytes 3932164
  32.7 1.5 %copy-start.4 = (f32[4,128,128]{2,1,0:T(8,128)S(1)}, f32[4,128,128]{2,1,0:T(8,128)}, u32[]{:S(2)}) copy-start(f32[4,128,128]{2,1,0:T(8,128)} %rate_ref.3) | copy-start | bytes 786436
  46.2 9.2 %copy-start.1 = (f32[5,4,128,128]{3,2,1,0:T(8,128)S(1)}, f32[5,4,128,128]{3,2,1,0:T(8,128)}, u32[]{:S(2)}) copy-start(f32[5,4,128,128]{3,2,1,0:T(8,128)} %prev_ref.3) | copy-start | bytes 3932164
  55.4 7.6 %collective-permute-start.2 = (f32[5,4,1,128]{3,2,1,0:T(1,128)S(1)}, f32[5,4,1,128]{3,2,1,0:T(1,128)S(1)}, u32[]{:S(2)}, u32[]{:S(2)}) collective-permute-start(f32[5,4,1,128]{3,2,1,0:T(1,128)S(1)} %get-tuple-element.39), channel_id=1, source_target_pairs={{0,1},{1,2},{2,3},{3,4},{4,5},{5,6},{6,7},{7,8},{8,9},{9,10},{10,1... | collective-permute-start | bytes 30728 | tf_op jit(solution)/shard_map/ppermute | solution.py:23
  55.5 7.6 %collective-permute-start.3 = (f32[5,4,1,128]{3,2,1,0:T(1,128)S(1)}, f32[5,4,1,128]{3,2,1,0:T(1,128)S(1)}, u32[]{:S(2)}, u32[]{:S(2)}) collective-permute-start(f32[5,4,1,128]{3,2,1,0:T(1,128)S(1)} %get-tuple-element.40), channel_id=1, source_target_pairs={{1,0},{2,1},{3,2},{4,3},{5,4},{6,5},{7,6},{8,7},{9,8},{10,9},{11,1... | collective-permute-start | bytes 30728 | tf_op jit(solution)/shard_map/ppermute | solution.py:24
  61.0 7.1 %collective-permute-start = (f32[5,1,128,128]{3,2,1,0:T(8,128)S(1)}, f32[5,1,128,128]{3,2,1,0:T(8,128)S(1)}, u32[]{:S(2)}, u32[]{:S(2)}) collective-permute-start(f32[5,1,128,128]{3,2,1,0:T(8,128)S(1)} %get-tuple-element.41), channel_id=1, source_target_pairs={{0,32},{32,64},{64,96},{96,128},{128,160},{160,192},{192,224},{224... | collective-permute-start | bytes 983048 | tf_op jit(solution)/shard_map/ppermute | solution.py:23
  61.8 9.2 %collective-permute-start.1 = (f32[5,1,128,128]{3,2,1,0:T(8,128)S(1)}, f32[5,1,128,128]{3,2,1,0:T(8,128)S(1)}, u32[]{:S(2)}, u32[]{:S(2)}) collective-permute-start(f32[5,1,128,128]{3,2,1,0:T(8,128)S(1)} %get-tuple-element.42), channel_id=1, source_target_pairs={{32,0},{64,32},{96,64},{128,96},{160,128},{192,160},{224,192},{0,2... | collective-permute-start | bytes 983048 | tf_op jit(solution)/shard_map/ppermute | solution.py:24
  63.3 8.0 %copy-start.3 = (f32[5,4,128,128]{3,2,1,0:T(8,128)S(1)}, f32[5,4,128,128]{3,2,1,0:T(8,128)}, u32[]{:S(2)}) copy-start(f32[5,4,128,128]{3,2,1,0:T(8,128)} %shard_map.91) | copy-start | bytes 3932164
  84.6 7.6 %collective-permute-start.6 = (f32[5,4,1,128]{3,2,1,0:T(1,128)S(1)}, f32[5,4,1,128]{3,2,1,0:T(1,128)S(1)}, u32[]{:S(2)}, u32[]{:S(2)}) collective-permute-start(f32[5,4,1,128]{3,2,1,0:T(1,128)S(1)} %get-tuple-element.33), channel_id=1, source_target_pairs={{0,1},{1,2},{2,3},{3,4},{4,5},{5,6},{6,7},{7,8},{8,9},{9,10},{10,1... | collective-permute-start | bytes 30728 | tf_op jit(solution)/shard_map/ppermute | solution.py:23
  84.8 7.6 %collective-permute-start.7 = (f32[5,4,1,128]{3,2,1,0:T(1,128)S(1)}, f32[5,4,1,128]{3,2,1,0:T(1,128)S(1)}, u32[]{:S(2)}, u32[]{:S(2)}) collective-permute-start(f32[5,4,1,128]{3,2,1,0:T(1,128)S(1)} %get-tuple-element.34), channel_id=1, source_target_pairs={{1,0},{2,1},{3,2},{4,3},{5,4},{6,5},{7,6},{8,7},{9,8},{10,9},{11,1... | collective-permute-start | bytes 30728 | tf_op jit(solution)/shard_map/ppermute | solution.py:24
  90.2 7.1 %collective-permute-start.4 = (f32[5,1,128,128]{3,2,1,0:T(8,128)S(1)}, f32[5,1,128,128]{3,2,1,0:T(8,128)S(1)}, u32[]{:S(2)}, u32[]{:S(2)}) collective-permute-start(f32[5,1,128,128]{3,2,1,0:T(8,128)S(1)} %get-tuple-element.35), channel_id=1, source_target_pairs={{0,32},{32,64},{64,96},{96,128},{128,160},{160,192},{192,224},{224... | collective-permute-start | bytes 983048 | tf_op jit(solution)/shard_map/ppermute | solution.py:23
  90.5 9.2 %collective-permute-start.5 = (f32[5,1,128,128]{3,2,1,0:T(8,128)S(1)}, f32[5,1,128,128]{3,2,1,0:T(8,128)S(1)}, u32[]{:S(2)}, u32[]{:S(2)}) collective-permute-start(f32[5,1,128,128]{3,2,1,0:T(8,128)S(1)} %get-tuple-element.36), channel_id=1, source_target_pairs={{32,0},{64,32},{96,64},{128,96},{160,128},{192,160},{224,192},{0,2... | collective-permute-start | bytes 983048 | tf_op jit(solution)/shard_map/ppermute | solution.py:24
  92.5 7.4 %copy-start.2 = (f32[5,4,128,128]{3,2,1,0:T(8,128)S(1)}, f32[5,4,128,128]{3,2,1,0:T(8,128)}, u32[]{:S(2)}) copy-start(f32[5,4,128,128]{3,2,1,0:T(8,128)} %shard_map.92) | copy-start | bytes 3932164

commit v7 on v2

--- a/solution.py
+++ b/solution.py
@@ -8,6 +8,7 @@
 NF = 5
 KP_DEV = 4
 PW = 32
+CAP = 2
 
 
 inv_step = 0.5
@@ -195,17 +196,32 @@
     panels = rotated.reshape(NF, rows_local, KP_DEV, PW)
     table_ids = jnp.arange(weight_table.shape[0], dtype=jnp.int32)
     weights = jnp.sum(jnp.where(weight_idx[..., None] == table_ids, weight_table, 0.0), axis=-1)
-    targets = owners[0] * KP_DEV + slots[0]
-    local_weights = weights[0]
-    panel_ids = jnp.arange(KP_DEV * span_count, dtype=jnp.int32)
-    mixing = jnp.sum(
-        jnp.where(targets[None] == panel_ids[:, None, None], local_weights[None], 0.0), axis=-1
-    ).reshape(span_count, KP_DEV, KP_DEV)
-    contributions = jnp.einsum(
-        "ogk,ftkp->oftgp", mixing, panels, precision=lax.Precision.HIGHEST
-    ).reshape(span_count, NF, rows_local, KP_DEV * PW)
-    received = lax.all_to_all(contributions, "span", 0, 0, tiled=True)
-    inlet_plane = jnp.sum(received, axis=0)
+    owner_of = owners[0].reshape(-1)
+    slot_of = slots[0].reshape(-1)
+    weight_of = weights[0].reshape(-1)
+    entries = owner_of.shape[0]
+    panel_of = jnp.arange(entries, dtype=jnp.int32) // owners.shape[-1]
+    earlier = jnp.tril(jnp.ones((entries, entries), dtype=bool), -1)
+    position = jnp.sum(earlier & (owner_of[:, None] == owner_of[None, :]), axis=1)
+    chosen = (owner_of[None, None] == jnp.arange(span_count, dtype=jnp.int32)[:, None, None]) & (
+        position[None, None] == jnp.arange(CAP, dtype=jnp.int32)[None, :, None]
+    )
+    picked = jnp.where(chosen, weight_of, 0.0)
+    selection = jnp.sum(
+        picked[..., None] * (panel_of[:, None] == jnp.arange(KP_DEV, dtype=jnp.int32)), axis=2
+    )
+    data = jnp.einsum("opk,ftkq->opftq", selection, panels, precision=lax.Precision.HIGHEST)
+    code = jnp.sum(jnp.where(chosen, slot_of + 1, 0), axis=2).astype(jnp.float32) - 1.0
+    payload = jnp.concatenate(
+        [data.reshape(span_count, CAP, -1), code[..., None]], axis=-1
+    )
+    received = lax.all_to_all(payload, "span", 0, 0, tiled=True)
+    values = received[..., :-1].reshape(span_count * CAP, NF, rows_local, 1, PW)
+    codes = received[..., -1].reshape(span_count * CAP, 1, 1, 1, 1)
+    slot_ids = jnp.arange(KP_DEV, dtype=jnp.float32).reshape(1, 1, 1, KP_DEV, 1)
+    inlet_plane = jnp.sum(jnp.where(codes == slot_ids, values, 0.0), axis=0).reshape(
+        NF, rows_local, KP_DEV * PW
+    )
 
     inlet_column = inlet_plane[..., None]
     mid, _ = sweep(q_old, q_old, pseudo_rate, inlet_column, flux_jacobians)

time: 90.4 us -> 85.9 us (0.950)
  the two profiles are of different devices: /device:TPU:1 before, /device:TPU:6 now
where the time goes in v7:
time: 85.9 us; the launch traced here: 85.2 us
  starting transfers between devices  30 us (35%)
  Pallas kernels  18.1 us (21%)
  local copies, waits for them, and re-layouts  13.4 us (16%)
  other arithmetic  11.6 us (14%)
  waiting for transfers between devices  11.4 us (13%)
    pallas_call x2, Pallas kernels, sweep(): pl.pallas_call(stencil_kernel, grid=(rows,), in_specs=[pl.BlockSpec(memor...  18.1 us
    ppermute x4, starting transfers between devices, halo_parts(): high = lax.ppermute(lax.slice_in_dim(block, 0, 1, axis=dim), axis, backward)  14 us
    all_to_all x1, waiting for transfers between devices, body(): received = lax.all_to_all(payload, 'span', 0, 0, tiled=True)  7.01 us
    all_to_all x1, starting transfers between devices, body(): received = lax.all_to_all(payload, 'span', 0, 0, tiled=True)  6.22 us
    all_to_all x1, starting transfers between devices, body(): gathered = lax.all_to_all(copies, 'circ', 0, 0, tiled=True)  5.79 us
    ppermute x4, waiting for transfers between devices, halo_parts(): high = lax.ppermute(lax.slice_in_dim(block, 0, 1, axis=dim), axis, backward)  4.16 us
    concatenate x2, other arithmetic, sweep(): padded = jnp.concatenate([circ_low, current, circ_high], axis=1)  4.09 us
    ppermute x4, starting transfers between devices, halo_parts(): lax.ppermute(lax.slice_in_dim(block, block.shape[dim] - 1, None, axis=dim...  4.06 us
  transfers between devices with their start and end apart: 10, of which 4 were waited for; matrix products, arithmetic and copies ran while one was open for 18% of the time, Pallas kernels for 0%

profile of v7, /device:TPU:6, one launch (start us, length us, event | category | flops | bytes accessed | tf_op | source)
XLA Modules:
  0.0 85.2 jit_solution(14910244048706393753)
XLA Ops:
  0.0 1.4 %broadcast_in_dim.94 = f32[8,5,4,128]{3,2,1,0:T(4,128)} broadcast(f32[5,4,128]{2,1,0:T(4,128)} %param.12), dimensions={1,2,3} | broadcast | bytes 92160 | tf_op jit(solution)/shard_map/broadcast_in_dim | solution.py:186
  1.5 5.8 %all-to-all-start = ((f32[8,5,4,128]{3,2,1,0:T(4,128)}), f32[8,5,4,128]{3,2,1,0:T(4,128)S(1)}, u32[]{:S(2)}, u32[]{:S(2)}) async-start(f32[8,5,4,128]{3,2,1,0:T(4,128)} %broadcast_in_dim.94), calls=%async_computation | async-start | bytes 163840 | tf_op jit(solution)/shard_map/all_to_all | solution.py:187
  7.2 0.9 %fusion.7 = (f32[5,4,1,128]{3,2,1,0:T(1,128)S(1)}, f32[5,4,1,128]{3,2,1,0:T(1,128)S(1)}) fusion(f32[5,4,128,128]{3,2,1,0:T(8,128)} %prev_ref.3), kind=kLoop, calls=%fused_computation.47 | loop fusion | bytes 40960 | tf_op jit(solution)/shard_map/slice | solution.py:38
  8.2 7.1 %collective-permute-start.2 = (f32[5,4,1,128]{3,2,1,0:T(1,128)S(1)}, f32[5,4,1,128]{3,2,1,0:T(1,128)S(1)}, u32[]{:S(2)}, u32[]{:S(2)}) collective-permute-start(f32[5,4,1,128]{3,2,1,0:T(1,128)S(1)} %get-tuple-element.12), channel_id=1, source_target_pairs={{1,0},{2,1},{3,2},{4,3},{5,4},{6,5},{7,6},{8,7},{9,8},{10,9},{11,1... | collective-permute-start | bytes 30728 | tf_op jit(solution)/shard_map/ppermute | solution.py:39
  15.3 1.1 %fusion.9 = (f32[5,1,128,128]{3,2,1,0:T(8,128)S(1)}, f32[5,1,128,128]{3,2,1,0:T(8,128)S(1)}) fusion(f32[5,4,128,128]{3,2,1,0:T(8,128)} %prev_ref.3), kind=kLoop, calls=%fused_computation.49 | loop fusion | bytes 1310720 | tf_op jit(solution)/shard_map/slice | solution.py:38
  17.4 1.2 %collective-permute-start.1 = (f32[5,1,128,128]{3,2,1,0:T(8,128)S(1)}, f32[5,1,128,128]{3,2,1,0:T(8,128)}, u32[]{:S(2)}, u32[]{:S(2)}) collective-permute-start(f32[5,1,128,128]{3,2,1,0:T(8,128)S(1)} %get-tuple-element.16), channel_id=1, source_target_pairs={{32,0},{64,32},{96,64},{128,96},{160,128},{192,160},{224,192},{0,2... | collective-permute-start | bytes 983048 | tf_op jit(solution)/shard_map/ppermute | solution.py:39
  18.7 1.3 %fusion.8 = (f32[5,4,127,128]{3,2,1,0:T(8,128)S(1)}, f32[5,4,127,128]{3,2,1,0:T(8,128)}) fusion(f32[5,4,128,128]{3,2,1,0:T(8,128)S(1)} %copy-done), kind=kLoop, calls=%fused_computation.48 | loop fusion | bytes 5201920 | tf_op jit(solution)/shard_map/slice | solution.py:106
  23.7 6.2 %all-to-all-start.1 = ((f32[32,2,641]{2,1,0:T(2,128)}), f32[32,2,641]{2,1,0:T(2,128)S(1)}, u32[]{:S(2)}, u32[]{:S(2)}) async-start(f32[32,2,641]{2,1,0:T(2,128)} %copy.43), calls=%async_computation.1 | async-start | bytes 393216 | tf_op jit(solution)/shard_map/all_to_all | solution.py:218
  29.9 2.5 %pad_maximum_fusion.2.su_ref = f32[5,4,128,128]{3,2,1,0:T(8,128)} fusion(f32[5,4,1,128]{3,2,1,0:T(1,128)S(1)} %broadcast_multiply_fusion.3, f32[5,4,127,128]{3,2,1,0:T(8,128)} %get-tuple-element.14), kind=kLoop, calls=%fused_computation.2 | loop fusion | flops 327680 | bytes 2621440 | tf_op jit(solution)/shard_map/concatenate | solution.py:105
  32.5 1.2 %pad_maximum_fusion.3.sd_ref = f32[5,4,128,128]{3,2,1,0:T(8,128)} fusion(f32[5,4,127,128]{3,2,1,0:T(8,128)S(1)} %get-tuple-element.13, f32[5,4,1,128]{3,2,1,0:T(1,128)S(1)} %broadcast_multiply_fusion.1), kind=kLoop, calls=%fused_computation.3 | loop fusion | flops 327680 | bytes 2621440 | tf_op jit(solution)/shard_map/concatenate | solution.py:106
  33.6 2.6 %pad_maximum_fusion.c_ref.cu_ref.cd_ref = f32[5,6,128,128]{3,2,1,0:T(8,128)} fusion(f32[5,1,128,128]{3,2,1,0:T(8,128)} %collective-permute-done.1, f32[5,4,128,128]{3,2,1,0:T(8,128)S(1)} %copy-done, f32[5,1,128,128]{3,2,1,0:T(8,128)} %collective-permute-done), kind=kLoop, calls=%fused_computation | loop fusion | flops 983040 | bytes 3932160 | tf_op jit(solution)/shard_map/concatenate | solution.py:104
  36.2 7.0 %all-to-all-done.1 = f32[32,2,641]{2,1,0:T(2,128)S(1)} async-done(((f32[32,2,641]{2,1,0:T(2,128)}), f32[32,2,641]{2,1,0:T(2,128)S(1)}, u32[]{:S(2)}, u32[]{:S(2)}) %all-to-all-start.1) | async-done | bytes 164128 | tf_op jit(solution)/shard_map/all_to_all | solution.py:218
  44.6 2.4 %broadcast_in_dim_reshape.14.inlet_ref = f32[5,4,128,1]{3,2,1,0:T(8,128)} reshape(f32[5,4,4,32]{3,2,1,0:T(4,128)S(1)} %select_reduce_fusion) | data formatting | bytes 20480 | tf_op jit(solution)/shard_map/broadcast_in_dim;reshape | solution.py:226
  47.0 9.0 %shard_map.91 = f32[5,4,128,128]{3,2,1,0:T(8,128)} custom-call(f32[75]{0:T(128)} %reshape.222.j_ref, f32[5,6,128,128]{3,2,1,0:T(8,128)} %pad_maximum_fusion.c_ref.cu_ref.cd_ref, f32[5,6,128,128]{3,2,1,0:T(8,128)} %pad_maximum_fusion.c_ref.cu_ref.cd_ref, f32[5,6,128,128]{3,2,1,0:T(8,128)} %pad_maximum_fusion.c_ref.cu_ref.cd_ref, ...), custom_call_target="tpu_custom_call" | custom-call | tf_op jit(solution)/shard_map/pallas_call | solution.py:110
  56.1 0.9 %fusion.4 = (f32[5,4,1,128]{3,2,1,0:T(1,128)S(1)}, f32[5,4,1,128]{3,2,1,0:T(1,128)S(1)}) fusion(f32[5,4,128,128]{3,2,1,0:T(8,128)} %shard_map.91), kind=kLoop, calls=%fused_computation.44 | loop fusion | bytes 40960 | tf_op jit(solution)/shard_map/slice | solution.py:38
  57.0 2.2 %fusion.5 = (f32[5,4,127,128]{3,2,1,0:T(8,128)S(1)}, f32[5,4,127,128]{3,2,1,0:T(8,128)S(1)}) fusion(f32[5,4,128,128]{3,2,1,0:T(8,128)} %shard_map.91), kind=kLoop, calls=%fused_computation.45 | loop fusion | bytes 5201920 | tf_op jit(solution)/shard_map/slice | solution.py:106
  59.4 3.0 %collective-permute-start.4 = (f32[5,1,128,128]{3,2,1,0:T(8,128)S(1)}, f32[5,1,128,128]{3,2,1,0:T(8,128)S(1)}, u32[]{:S(2)}, u32[]{:S(2)}) collective-permute-start(f32[5,1,128,128]{3,2,1,0:T(8,128)S(1)} %get-tuple-element.9), channel_id=1, source_target_pairs={{0,32},{32,64},{64,96},{96,128},{128,160},{160,192},{192,224},{224... | collective-permute-start | bytes 983048 | tf_op jit(solution)/shard_map/ppermute | solution.py:38
  62.4 5.7 %collective-permute-start.6 = (f32[5,4,1,128]{3,2,1,0:T(1,128)S(1)}, f32[5,4,1,128]{3,2,1,0:T(1,128)S(1)}, u32[]{:S(2)}, u32[]{:S(2)}) collective-permute-start(f32[5,4,1,128]{3,2,1,0:T(1,128)S(1)} %get-tuple-element.6), channel_id=1, source_target_pairs={{1,0},{2,1},{3,2},{4,3},{5,4},{6,5},{7,6},{8,7},{9,8},{10,9},{11,1... | collective-permute-start | bytes 30728 | tf_op jit(solution)/shard_map/ppermute | solution.py:39
  68.1 1.4 %collective-permute-done.6 = f32[5,4,1,128]{3,2,1,0:T(1,128)S(1)} collective-permute-done((f32[5,4,1,128]{3,2,1,0:T(1,128)S(1)}, f32[5,4,1,128]{3,2,1,0:T(1,128)S(1)}, u32[]{:S(2)}, u32[]{:S(2)}) %collective-permute-start.6) | collective-permute-done | bytes 10272 | tf_op jit(solution)/shard_map/ppermute | solution.py:39
  69.5 1.2 %pad_maximum_fusion.5.sd_ref = f32[5,4,128,128]{3,2,1,0:T(8,128)} fusion(f32[5,4,127,128]{3,2,1,0:T(8,128)S(1)} %get-tuple-element.7, f32[5,4,1,128]{3,2,1,0:T(1,128)S(1)} %broadcast_multiply_fusion), kind=kLoop, calls=%fused_computation.5 | loop fusion | flops 327680 | bytes 2621440 | tf_op jit(solution)/shard_map/concatenate | solution.py:106
  70.7 1.2 %pad_maximum_fusion.4.su_ref = f32[5,4,128,128]{3,2,1,0:T(8,128)} fusion(f32[5,4,1,128]{3,2,1,0:T(1,128)S(1)} %broadcast_multiply_fusion.2, f32[5,4,127,128]{3,2,1,0:T(8,128)S(1)} %get-tuple-element.8), kind=kLoop, calls=%fused_computation.4 | loop fusion | flops 327680 | bytes 2621440 | tf_op jit(solution)/shard_map/concatenate | solution.py:105
  71.9 2.8 %collective-permute-done.5 = f32[5,1,128,128]{3,2,1,0:T(8,128)S(1)} collective-permute-done((f32[5,1,128,128]{3,2,1,0:T(8,128)S(1)}, f32[5,1,128,128]{3,2,1,0:T(8,128)S(1)}, u32[]{:S(2)}, u32[]{:S(2)}) %collective-permute-start.5) | collective-permute-done | bytes 327712 | tf_op jit(solution)/shard_map/ppermute | solution.py:39
  74.7 1.5 %pad_maximum_fusion.1.c_ref.cu_ref.cd_ref = f32[5,6,128,128]{3,2,1,0:T(8,128)} fusion(f32[5,1,128,128]{3,2,1,0:T(8,128)S(1)} %collective-permute-done.5, f32[5,4,128,128]{3,2,1,0:T(8,128)S(1)} %copy-done.1, f32[5,1,128,128]{3,2,1,0:T(8,128)S(1)} %collective-permute-done.4), kind=kLoop, calls=%fused_computation.1 | loop fusion | flops 983040 | bytes 3932160 | tf_op jit(solution)/shard_map/concatenate | solution.py:104
  76.2 9.0 %shard_map.92 = f32[5,4,128,128]{3,2,1,0:T(8,128)} custom-call(f32[75]{0:T(128)} %reshape.222.j_ref, f32[5,6,128,128]{3,2,1,0:T(8,128)} %pad_maximum_fusion.1.c_ref.cu_ref.cd_ref, f32[5,6,128,128]{3,2,1,0:T(8,128)} %pad_maximum_fusion.1.c_ref.cu_ref.cd_ref, f32[5,6,128,128]{3,2,1,0:T(8,128)} %pad_maximum_fusion.1.c_ref.cu_ref.cd_ref, ...), custom_call_target="tpu_custom_call" | custom-call | tf_op jit(solution)/shard_map/pallas_call | solution.py:110
  (69 shorter events, 6.1 us)
Async XLA Ops:
  0.0 18.6 %copy-start = (f32[5,4,128,128]{3,2,1,0:T(8,128)S(1)}, f32[5,4,128,128]{3,2,1,0:T(8,128)}, u32[]{:S(2)}) copy-start(f32[5,4,128,128]{3,2,1,0:T(8,128)} %prev_ref.3) | copy-start | bytes 3932164
  1.5 20.7 %all-to-all-start = ((f32[8,5,4,128]{3,2,1,0:T(4,128)}), f32[8,5,4,128]{3,2,1,0:T(4,128)S(1)}, u32[]{:S(2)}, u32[]{:S(2)}) async-start(f32[8,5,4,128]{3,2,1,0:T(4,128)} %broadcast_in_dim.94), calls=%async_computation | async-start | bytes 163840 | tf_op jit(solution)/shard_map/all_to_all | solution.py:187
  8.2 13.7 %collective-permute-start.2 = (f32[5,4,1,128]{3,2,1,0:T(1,128)S(1)}, f32[5,4,1,128]{3,2,1,0:T(1,128)S(1)}, u32[]{:S(2)}, u32[]{:S(2)}) collective-permute-start(f32[5,4,1,128]{3,2,1,0:T(1,128)S(1)} %get-tuple-element.12), channel_id=1, source_target_pairs={{1,0},{2,1},{3,2},{4,3},{5,4},{6,5},{7,6},{8,7},{9,8},{10,9},{11,1... | collective-permute-start | bytes 30728 | tf_op jit(solution)/shard_map/ppermute | solution.py:39
  15.3 6.8 %collective-permute-start.3 = (f32[5,4,1,128]{3,2,1,0:T(1,128)S(1)}, f32[5,4,1,128]{3,2,1,0:T(1,128)S(1)}, u32[]{:S(2)}, u32[]{:S(2)}) collective-permute-start(f32[5,4,1,128]{3,2,1,0:T(1,128)S(1)} %get-tuple-element.11), channel_id=1, source_target_pairs={{0,1},{1,2},{2,3},{3,4},{4,5},{5,6},{6,7},{7,8},{8,9},{9,10},{10,1... | collective-permute-start | bytes 30728 | tf_op jit(solution)/shard_map/ppermute | solution.py:38
  16.5 17.2 %collective-permute-start = (f32[5,1,128,128]{3,2,1,0:T(8,128)S(1)}, f32[5,1,128,128]{3,2,1,0:T(8,128)}, u32[]{:S(2)}, u32[]{:S(2)}) collective-permute-start(f32[5,1,128,128]{3,2,1,0:T(8,128)S(1)} %get-tuple-element.15), channel_id=1, source_target_pairs={{0,32},{32,64},{64,96},{96,128},{128,160},{160,192},{192,224},{224... | collective-permute-start | bytes 983048 | tf_op jit(solution)/shard_map/ppermute | solution.py:38
  17.4 16.2 %collective-permute-start.1 = (f32[5,1,128,128]{3,2,1,0:T(8,128)S(1)}, f32[5,1,128,128]{3,2,1,0:T(8,128)}, u32[]{:S(2)}, u32[]{:S(2)}) collective-permute-start(f32[5,1,128,128]{3,2,1,0:T(8,128)S(1)} %get-tuple-element.16), channel_id=1, source_target_pairs={{32,0},{64,32},{96,64},{128,96},{160,128},{192,160},{224,192},{0,2... | collective-permute-start | bytes 983048 | tf_op jit(solution)/shard_map/ppermute | solution.py:39
  18.6 1.4 %copy-start.3 = (s32[1,4,4]{2,1,0:T(4,128)S(1)}, s32[1,4,4]{2,1,0:T(4,128)}, u32[]{:S(2)}) copy-start(s32[1,4,4]{2,1,0:T(4,128)} %param.14) | copy-start | bytes 196
  18.6 1.7 %copy-start.4 = (s32[1,4,4]{2,1,0:T(4,128)S(1)}, s32[1,4,4]{2,1,0:T(4,128)}, u32[]{:S(2)}) copy-start(s32[1,4,4]{2,1,0:T(4,128)} %param.16) | copy-start | bytes 196
  18.6 1.7 %copy-start.6 = (f32[16]{0:T(128)S(1)}, f32[16]{0:T(128)}, u32[]{:S(2)}) copy-start(f32[16]{0:T(128)} %param.17) | copy-start | bytes 196
  18.6 2.0 %copy-start.5 = (s32[1,4,4]{2,1,0:T(4,128)S(1)}, s32[1,4,4]{2,1,0:T(4,128)}, u32[]{:S(2)}) copy-start(s32[1,4,4]{2,1,0:T(4,128)} %param.15) | copy-start | bytes 196
  18.6 2.3 %copy-start.7 = (s32[128]{0:T(128)S(1)}, s32[128]{0:T(128)}, u32[]{:S(2)}) copy-start(s32[128]{0:T(128)} %param.13) | copy-start | bytes 1540
  18.6 2.6 %copy-start.2 = (f32[3,5,5]{2,0,1:T(4,128)S(1)}, f32[3,5,5]{2,0,1:T(4,128)}, u32[]{:S(2)}) copy-start(f32[3,5,5]{2,0,1:T(4,128)} %param.11) | copy-start | bytes 904
  23.7 19.5 %all-to-all-start.1 = ((f32[32,2,641]{2,1,0:T(2,128)}), f32[32,2,641]{2,1,0:T(2,128)S(1)}, u32[]{:S(2)}, u32[]{:S(2)}) async-start(f32[32,2,641]{2,1,0:T(2,128)} %copy.43), calls=%async_computation.1 | async-start | bytes 393216 | tf_op jit(solution)/shard_map/all_to_all | solution.py:218
  57.0 2.3 %copy-start.1 = (f32[5,4,128,128]{3,2,1,0:T(8,128)S(1)}, f32[5,4,128,128]{3,2,1,0:T(8,128)}, u32[]{:S(2)}) copy-start(f32[5,4,128,128]{3,2,1,0:T(8,128)} %shard_map.91) | copy-start | bytes 3932164
  59.2 8.9 %collective-permute-start.7 = (f32[5,4,1,128]{3,2,1,0:T(1,128)S(1)}, f32[5,4,1,128]{3,2,1,0:T(1,128)S(1)}, u32[]{:S(2)}, u32[]{:S(2)}) collective-permute-start(f32[5,4,1,128]{3,2,1,0:T(1,128)S(1)} %get-tuple-element.5), channel_id=1, source_target_pairs={{0,1},{1,2},{2,3},{3,4},{4,5},{5,6},{6,7},{7,8},{8,9},{9,10},{10,1... | collective-permute-start | bytes 30728 | tf_op jit(solution)/shard_map/ppermute | solution.py:38
  59.4 12.5 %collective-permute-start.4 = (f32[5,1,128,128]{3,2,1,0:T(8,128)S(1)}, f32[5,1,128,128]{3,2,1,0:T(8,128)S(1)}, u32[]{:S(2)}, u32[]{:S(2)}) collective-permute-start(f32[5,1,128,128]{3,2,1,0:T(8,128)S(1)} %get-tuple-element.9), channel_id=1, source_target_pairs={{0,32},{32,64},{64,96},{96,128},{128,160},{160,192},{192,224},{224... | collective-permute-start | bytes 983048 | tf_op jit(solution)/shard_map/ppermute | solution.py:38
  62.4 12.2 %collective-permute-start.5 = (f32[5,1,128,128]{3,2,1,0:T(8,128)S(1)}, f32[5,1,128,128]{3,2,1,0:T(8,128)S(1)}, u32[]{:S(2)}, u32[]{:S(2)}) collective-permute-start(f32[5,1,128,128]{3,2,1,0:T(8,128)S(1)} %get-tuple-element.10), channel_id=1, source_target_pairs={{32,0},{64,32},{96,64},{128,96},{160,128},{192,160},{224,192},{0,2... | collective-permute-start | bytes 983048 | tf_op jit(solution)/shard_map/ppermute | solution.py:39
  62.4 7.0 %collective-permute-start.6 = (f32[5,4,1,128]{3,2,1,0:T(1,128)S(1)}, f32[5,4,1,128]{3,2,1,0:T(1,128)S(1)}, u32[]{:S(2)}, u32[]{:S(2)}) collective-permute-start(f32[5,4,1,128]{3,2,1,0:T(1,128)S(1)} %get-tuple-element.6), channel_id=1, source_target_pairs={{1,0},{2,1},{3,2},{4,3},{5,4},{6,5},{7,6},{8,7},{9,8},{10,9},{11,1... | collective-permute-start | bytes 30728 | tf_op jit(solution)/shard_map/ppermute | solution.py:39

commit v8 on v7

--- a/solution.py
+++ b/solution.py
@@ -55,7 +55,13 @@
     )
 
 
-def stencil_kernel(j_ref, c_ref, cu_ref, cd_ref, su_ref, sd_ref, prev_ref, rate_ref, inlet_ref, out_ref):
+def stencil_kernel(
+    j_ref, c_ref, cu_ref, cd_ref, su_ref, sd_ref, prev_ref, rate_ref, inlet_ref, out_ref, inlet_scr
+):
+    span, axial = inlet_scr.shape[1:]
+    for g in range(NF):
+        row = inlet_ref[0, g : g + 1, :]
+        inlet_scr[g] = jnp.transpose(jnp.broadcast_to(row, (axial, span)))
     lane = lax.broadcasted_iota(jnp.int32, (8, 128), 1)
     probe = pltpu.roll(lane, 1, 1)
     numpy_order = probe == (lane + 127) % 128
@@ -73,7 +79,7 @@
             other = pltpu.roll(cur[g], 127, 1)
             down = jnp.where(numpy_order, one, other)
             up = jnp.where(numpy_order, other, one)
-            ad.append(jnp.where(lane == 0, inlet_ref[g, 0, rows, :], down))
+            ad.append(jnp.where(lane == 0, inlet_scr[g, rows, :], down))
             au.append(jnp.where(lane == 127, 0.0, up))
         dc = [cu[g] - cd[g] for g in range(NF)]
         ds = [su[g] - sd[g] for g in range(NF)]
@@ -98,7 +104,7 @@
     lax.fori_loop(0, c_ref.shape[2] // 8, chunk, 0)
 
 
-def sweep(current, previous, rate_cells, inlet_column, jacobians):
+def sweep(current, previous, rate_cells, inlet_rows, jacobians):
     parts = halo_parts(current)
     circ_low, circ_high, span_low, span_high = parts
     padded = jnp.concatenate([circ_low, current, circ_high], axis=1)
@@ -119,11 +125,12 @@
             spec(0),
             spec(0),
             pl.BlockSpec((1, span, axial), lambda t: (t, 0, 0)),
-            pl.BlockSpec((nf, 1, span, 1), lambda t: (0, t, 0, 0)),
+            pl.BlockSpec((1, nf, span), lambda t: (t, 0, 0)),
         ],
+        scratch_shapes=[pltpu.VMEM((nf, span, axial), current.dtype)],
         out_specs=spec(0),
         out_shape=jax.ShapeDtypeStruct(current.shape, current.dtype),
-    )(jacobians.reshape(-1), padded, padded, padded, span_up, span_down, previous, rate_cells, inlet_column)
+    )(jacobians.reshape(-1), padded, padded, padded, span_up, span_down, previous, rate_cells, inlet_rows)
     return out, parts
 
 
@@ -219,13 +226,12 @@
     values = received[..., :-1].reshape(span_count * CAP, NF, rows_local, 1, PW)
     codes = received[..., -1].reshape(span_count * CAP, 1, 1, 1, 1)
     slot_ids = jnp.arange(KP_DEV, dtype=jnp.float32).reshape(1, 1, 1, KP_DEV, 1)
-    inlet_plane = jnp.sum(jnp.where(codes == slot_ids, values, 0.0), axis=0).reshape(
-        NF, rows_local, KP_DEV * PW
-    )
-
-    inlet_column = inlet_plane[..., None]
-    mid, _ = sweep(q_old, q_old, pseudo_rate, inlet_column, flux_jacobians)
-    new, _ = sweep(mid, q_old, pseudo_rate, inlet_column, flux_jacobians)
+    inlet_rows = jnp.transpose(
+        jnp.sum(jnp.where(codes == slot_ids, values, 0.0), axis=0), (1, 0, 2, 3)
+    ).reshape(rows_local, NF, KP_DEV * PW)
+
+    mid, _ = sweep(q_old, q_old, pseudo_rate, inlet_rows, flux_jacobians)
+    new, _ = sweep(mid, q_old, pseudo_rate, inlet_rows, flux_jacobians)
     return new
 
 

time: 85.9 us -> 84.3 us (0.981)
  local copies, waits for them, and re-layouts: 13.4 us -> 11.6 us
    another operation x1 -> x0, local copies, waits for them, and re-layouts: 2.42 us -> none  [body(): inlet_column = inlet_plane[..., None]]
where the time goes in v8:
time: 84.3 us; the launch traced here: 83.6 us
  starting transfers between devices  30 us (36%)
  Pallas kernels  18.3 us (22%)
  local copies, waits for them, and re-layouts  11.6 us (14%)
  other arithmetic  11.6 us (14%)
  waiting for transfers between devices  11.5 us (14%)
    pallas_call x2, Pallas kernels, sweep(): pl.pallas_call(stencil_kernel, grid=(rows,), in_specs=[pl.BlockSpec(memor...  18.3 us
    ppermute x4, starting transfers between devices, halo_parts(): high = lax.ppermute(lax.slice_in_dim(block, 0, 1, axis=dim), axis, backward)  14 us
    all_to_all x1, waiting for transfers between devices, body(): received = lax.all_to_all(payload, 'span', 0, 0, tiled=True)  7.01 us
    all_to_all x1, starting transfers between devices, body(): received = lax.all_to_all(payload, 'span', 0, 0, tiled=True)  6.2 us
    all_to_all x1, starting transfers between devices, body(): gathered = lax.all_to_all(copies, 'circ', 0, 0, tiled=True)  5.79 us
    ppermute x4, waiting for transfers between devices, halo_parts(): high = lax.ppermute(lax.slice_in_dim(block, 0, 1, axis=dim), axis, backward)  4.19 us
    concatenate x2, other arithmetic, sweep(): padded = jnp.concatenate([circ_low, current, circ_high], axis=1)  4.09 us
    ppermute x4, starting transfers between devices, halo_parts(): lax.ppermute(lax.slice_in_dim(block, block.shape[dim] - 1, None, axis=dim...  4.07 us
  transfers between devices with their start and end apart: 10, of which 4 were waited for; matrix products, arithmetic and copies ran while one was open for 18% of the time, Pallas kernels for 0%

profile of v8, /device:TPU:6, one launch (start us, length us, event | category | flops | bytes accessed | tf_op | source)
XLA Modules:
  0.0 83.6 jit_solution(726312356825563376)
XLA Ops:
  0.0 1.4 %broadcast_in_dim.94 = f32[8,5,4,128]{3,2,1,0:T(4,128)} broadcast(f32[5,4,128]{2,1,0:T(4,128)} %param.12), dimensions={1,2,3} | broadcast | bytes 92160 | tf_op jit(solution)/shard_map/broadcast_in_dim | solution.py:193
  1.5 5.8 %all-to-all-start = ((f32[8,5,4,128]{3,2,1,0:T(4,128)}), f32[8,5,4,128]{3,2,1,0:T(4,128)S(1)}, u32[]{:S(2)}, u32[]{:S(2)}) async-start(f32[8,5,4,128]{3,2,1,0:T(4,128)} %broadcast_in_dim.94), calls=%async_computation | async-start | bytes 163840 | tf_op jit(solution)/shard_map/all_to_all | solution.py:194
  7.2 0.9 %fusion.7 = (f32[5,4,1,128]{3,2,1,0:T(1,128)S(1)}, f32[5,4,1,128]{3,2,1,0:T(1,128)S(1)}) fusion(f32[5,4,128,128]{3,2,1,0:T(8,128)} %prev_ref.3), kind=kLoop, calls=%fused_computation.47 | loop fusion | bytes 40960 | tf_op jit(solution)/shard_map/slice | solution.py:38
  8.2 7.1 %collective-permute-start.2 = (f32[5,4,1,128]{3,2,1,0:T(1,128)S(1)}, f32[5,4,1,128]{3,2,1,0:T(1,128)S(1)}, u32[]{:S(2)}, u32[]{:S(2)}) collective-permute-start(f32[5,4,1,128]{3,2,1,0:T(1,128)S(1)} %get-tuple-element.12), channel_id=1, source_target_pairs={{1,0},{2,1},{3,2},{4,3},{5,4},{6,5},{7,6},{8,7},{9,8},{10,9},{11,1... | collective-permute-start | bytes 30728 | tf_op jit(solution)/shard_map/ppermute | solution.py:39
  15.3 1.1 %fusion.9 = (f32[5,1,128,128]{3,2,1,0:T(8,128)S(1)}, f32[5,1,128,128]{3,2,1,0:T(8,128)S(1)}) fusion(f32[5,4,128,128]{3,2,1,0:T(8,128)} %prev_ref.3), kind=kLoop, calls=%fused_computation.49 | loop fusion | bytes 1310720 | tf_op jit(solution)/shard_map/slice | solution.py:38
  16.5 0.9 %collective-permute-start = (f32[5,1,128,128]{3,2,1,0:T(8,128)S(1)}, f32[5,1,128,128]{3,2,1,0:T(8,128)}, u32[]{:S(2)}, u32[]{:S(2)}) collective-permute-start(f32[5,1,128,128]{3,2,1,0:T(8,128)S(1)} %get-tuple-element.15), channel_id=1, source_target_pairs={{0,32},{32,64},{64,96},{96,128},{128,160},{160,192},{192,224},{224... | collective-permute-start | bytes 983048 | tf_op jit(solution)/shard_map/ppermute | solution.py:38
  17.4 1.2 %collective-permute-start.1 = (f32[5,1,128,128]{3,2,1,0:T(8,128)S(1)}, f32[5,1,128,128]{3,2,1,0:T(8,128)}, u32[]{:S(2)}, u32[]{:S(2)}) collective-permute-start(f32[5,1,128,128]{3,2,1,0:T(8,128)S(1)} %get-tuple-element.16), channel_id=1, source_target_pairs={{32,0},{64,32},{96,64},{128,96},{160,128},{192,160},{224,192},{0,2... | collective-permute-start | bytes 983048 | tf_op jit(solution)/shard_map/ppermute | solution.py:39
  18.7 1.3 %fusion.8 = (f32[5,4,127,128]{3,2,1,0:T(8,128)S(1)}, f32[5,4,127,128]{3,2,1,0:T(8,128)}) fusion(f32[5,4,128,128]{3,2,1,0:T(8,128)S(1)} %copy-done), kind=kLoop, calls=%fused_computation.48 | loop fusion | bytes 5201920 | tf_op jit(solution)/shard_map/slice | solution.py:112
  23.7 6.2 %all-to-all-start.1 = ((f32[32,2,641]{2,1,0:T(2,128)}), f32[32,2,641]{2,1,0:T(2,128)S(1)}, u32[]{:S(2)}, u32[]{:S(2)}) async-start(f32[32,2,641]{2,1,0:T(2,128)} %copy.43), calls=%async_computation.1 | async-start | bytes 393216 | tf_op jit(solution)/shard_map/all_to_all | solution.py:225
  29.9 2.5 %pad_maximum_fusion.2.su_ref = f32[5,4,128,128]{3,2,1,0:T(8,128)} fusion(f32[5,4,1,128]{3,2,1,0:T(1,128)S(1)} %broadcast_multiply_fusion.3, f32[5,4,127,128]{3,2,1,0:T(8,128)} %get-tuple-element.14), kind=kLoop, calls=%fused_computation.2 | loop fusion | flops 327680 | bytes 2621440 | tf_op jit(solution)/shard_map/concatenate | solution.py:111
  32.4 1.2 %pad_maximum_fusion.3.sd_ref = f32[5,4,128,128]{3,2,1,0:T(8,128)} fusion(f32[5,4,127,128]{3,2,1,0:T(8,128)S(1)} %get-tuple-element.13, f32[5,4,1,128]{3,2,1,0:T(1,128)S(1)} %broadcast_multiply_fusion.1), kind=kLoop, calls=%fused_computation.3 | loop fusion | flops 327680 | bytes 2621440 | tf_op jit(solution)/shard_map/concatenate | solution.py:112
  33.6 2.6 %pad_maximum_fusion.c_ref.cu_ref.cd_ref = f32[5,6,128,128]{3,2,1,0:T(8,128)} fusion(f32[5,1,128,128]{3,2,1,0:T(8,128)} %collective-permute-done.1, f32[5,4,128,128]{3,2,1,0:T(8,128)S(1)} %copy-done, f32[5,1,128,128]{3,2,1,0:T(8,128)} %collective-permute-done), kind=kLoop, calls=%fused_computation | loop fusion | flops 983040 | bytes 3932160 | tf_op jit(solution)/shard_map/concatenate | solution.py:110
  36.2 7.0 %all-to-all-done.1 = f32[32,2,641]{2,1,0:T(2,128)S(1)} async-done(((f32[32,2,641]{2,1,0:T(2,128)}), f32[32,2,641]{2,1,0:T(2,128)S(1)}, u32[]{:S(2)}, u32[]{:S(2)}) %all-to-all-start.1) | async-done | bytes 164128 | tf_op jit(solution)/shard_map/all_to_all | solution.py:225
  45.3 9.1 %shard_map.91 = f32[5,4,128,128]{3,2,1,0:T(8,128)} custom-call(f32[75]{0:T(128)} %reshape.225.j_ref, f32[5,6,128,128]{3,2,1,0:T(8,128)} %pad_maximum_fusion.c_ref.cu_ref.cd_ref, f32[5,6,128,128]{3,2,1,0:T(8,128)} %pad_maximum_fusion.c_ref.cu_ref.cd_ref, f32[5,6,128,128]{3,2,1,0:T(8,128)} %pad_maximum_fusion.c_ref.cu_ref.cd_ref, ...), custom_call_target="tpu_custom_call" | custom-call | tf_op jit(solution)/shard_map/pallas_call | solution.py:116
  54.5 0.9 %fusion.4 = (f32[5,4,1,128]{3,2,1,0:T(1,128)S(1)}, f32[5,4,1,128]{3,2,1,0:T(1,128)S(1)}) fusion(f32[5,4,128,128]{3,2,1,0:T(8,128)} %shard_map.91), kind=kLoop, calls=%fused_computation.44 | loop fusion | bytes 40960 | tf_op jit(solution)/shard_map/slice | solution.py:38
  55.4 2.1 %fusion.5 = (f32[5,4,127,128]{3,2,1,0:T(8,128)S(1)}, f32[5,4,127,128]{3,2,1,0:T(8,128)S(1)}) fusion(f32[5,4,128,128]{3,2,1,0:T(8,128)} %shard_map.91), kind=kLoop, calls=%fused_computation.45 | loop fusion | bytes 5201920 | tf_op jit(solution)/shard_map/slice | solution.py:112
  57.7 3.0 %collective-permute-start.4 = (f32[5,1,128,128]{3,2,1,0:T(8,128)S(1)}, f32[5,1,128,128]{3,2,1,0:T(8,128)S(1)}, u32[]{:S(2)}, u32[]{:S(2)}) collective-permute-start(f32[5,1,128,128]{3,2,1,0:T(8,128)S(1)} %get-tuple-element.9), channel_id=1, source_target_pairs={{0,32},{32,64},{64,96},{96,128},{128,160},{160,192},{192,224},{224... | collective-permute-start | bytes 983048 | tf_op jit(solution)/shard_map/ppermute | solution.py:38
  60.7 5.7 %collective-permute-start.6 = (f32[5,4,1,128]{3,2,1,0:T(1,128)S(1)}, f32[5,4,1,128]{3,2,1,0:T(1,128)S(1)}, u32[]{:S(2)}, u32[]{:S(2)}) collective-permute-start(f32[5,4,1,128]{3,2,1,0:T(1,128)S(1)} %get-tuple-element.6), channel_id=1, source_target_pairs={{1,0},{2,1},{3,2},{4,3},{5,4},{6,5},{7,6},{8,7},{9,8},{10,9},{11,1... | collective-permute-start | bytes 30728 | tf_op jit(solution)/shard_map/ppermute | solution.py:39
  66.4 1.4 %collective-permute-done.6 = f32[5,4,1,128]{3,2,1,0:T(1,128)S(1)} collective-permute-done((f32[5,4,1,128]{3,2,1,0:T(1,128)S(1)}, f32[5,4,1,128]{3,2,1,0:T(1,128)S(1)}, u32[]{:S(2)}, u32[]{:S(2)}) %collective-permute-start.6) | collective-permute-done | bytes 10272 | tf_op jit(solution)/shard_map/ppermute | solution.py:39
  67.8 1.2 %pad_maximum_fusion.5.sd_ref = f32[5,4,128,128]{3,2,1,0:T(8,128)} fusion(f32[5,4,127,128]{3,2,1,0:T(8,128)S(1)} %get-tuple-element.7, f32[5,4,1,128]{3,2,1,0:T(1,128)S(1)} %broadcast_multiply_fusion), kind=kLoop, calls=%fused_computation.5 | loop fusion | flops 327680 | bytes 2621440 | tf_op jit(solution)/shard_map/concatenate | solution.py:112
  69.0 1.2 %pad_maximum_fusion.4.su_ref = f32[5,4,128,128]{3,2,1,0:T(8,128)} fusion(f32[5,4,1,128]{3,2,1,0:T(1,128)S(1)} %broadcast_multiply_fusion.2, f32[5,4,127,128]{3,2,1,0:T(8,128)S(1)} %get-tuple-element.8), kind=kLoop, calls=%fused_computation.4 | loop fusion | flops 327680 | bytes 2621440 | tf_op jit(solution)/shard_map/concatenate | solution.py:111
  70.1 2.8 %collective-permute-done.5 = f32[5,1,128,128]{3,2,1,0:T(8,128)S(1)} collective-permute-done((f32[5,1,128,128]{3,2,1,0:T(8,128)S(1)}, f32[5,1,128,128]{3,2,1,0:T(8,128)S(1)}, u32[]{:S(2)}, u32[]{:S(2)}) %collective-permute-start.5) | collective-permute-done | bytes 327712 | tf_op jit(solution)/shard_map/ppermute | solution.py:39
  73.0 1.5 %pad_maximum_fusion.1.c_ref.cu_ref.cd_ref = f32[5,6,128,128]{3,2,1,0:T(8,128)} fusion(f32[5,1,128,128]{3,2,1,0:T(8,128)S(1)} %collective-permute-done.5, f32[5,4,128,128]{3,2,1,0:T(8,128)S(1)} %copy-done.1, f32[5,1,128,128]{3,2,1,0:T(8,128)S(1)} %collective-permute-done.4), kind=kLoop, calls=%fused_computation.1 | loop fusion | flops 983040 | bytes 3932160 | tf_op jit(solution)/shard_map/concatenate | solution.py:110
  74.5 9.2 %shard_map.92 = f32[5,4,128,128]{3,2,1,0:T(8,128)} custom-call(f32[75]{0:T(128)} %reshape.225.j_ref, f32[5,6,128,128]{3,2,1,0:T(8,128)} %pad_maximum_fusion.1.c_ref.cu_ref.cd_ref, f32[5,6,128,128]{3,2,1,0:T(8,128)} %pad_maximum_fusion.1.c_ref.cu_ref.cd_ref, f32[5,6,128,128]{3,2,1,0:T(8,128)} %pad_maximum_fusion.1.c_ref.cu_ref.cd_ref, ...), custom_call_target="tpu_custom_call" | custom-call | tf_op jit(solution)/shard_map/pallas_call | solution.py:116
  (70 shorter events, 5.9 us)
Async XLA Ops:
  0.0 18.6 %copy-start = (f32[5,4,128,128]{3,2,1,0:T(8,128)S(1)}, f32[5,4,128,128]{3,2,1,0:T(8,128)}, u32[]{:S(2)}) copy-start(f32[5,4,128,128]{3,2,1,0:T(8,128)} %prev_ref.3) | copy-start | bytes 3932164
  1.5 20.7 %all-to-all-start = ((f32[8,5,4,128]{3,2,1,0:T(4,128)}), f32[8,5,4,128]{3,2,1,0:T(4,128)S(1)}, u32[]{:S(2)}, u32[]{:S(2)}) async-start(f32[8,5,4,128]{3,2,1,0:T(4,128)} %broadcast_in_dim.94), calls=%async_computation | async-start | bytes 163840 | tf_op jit(solution)/shard_map/all_to_all | solution.py:194
  8.2 13.7 %collective-permute-start.2 = (f32[5,4,1,128]{3,2,1,0:T(1,128)S(1)}, f32[5,4,1,128]{3,2,1,0:T(1,128)S(1)}, u32[]{:S(2)}, u32[]{:S(2)}) collective-permute-start(f32[5,4,1,128]{3,2,1,0:T(1,128)S(1)} %get-tuple-element.12), channel_id=1, source_target_pairs={{1,0},{2,1},{3,2},{4,3},{5,4},{6,5},{7,6},{8,7},{9,8},{10,9},{11,1... | collective-permute-start | bytes 30728 | tf_op jit(solution)/shard_map/ppermute | solution.py:39
  15.3 6.8 %collective-permute-start.3 = (f32[5,4,1,128]{3,2,1,0:T(1,128)S(1)}, f32[5,4,1,128]{3,2,1,0:T(1,128)S(1)}, u32[]{:S(2)}, u32[]{:S(2)}) collective-permute-start(f32[5,4,1,128]{3,2,1,0:T(1,128)S(1)} %get-tuple-element.11), channel_id=1, source_target_pairs={{0,1},{1,2},{2,3},{3,4},{4,5},{5,6},{6,7},{7,8},{8,9},{9,10},{10,1... | collective-permute-start | bytes 30728 | tf_op jit(solution)/shard_map/ppermute | solution.py:38
  16.5 17.1 %collective-permute-start = (f32[5,1,128,128]{3,2,1,0:T(8,128)S(1)}, f32[5,1,128,128]{3,2,1,0:T(8,128)}, u32[]{:S(2)}, u32[]{:S(2)}) collective-permute-start(f32[5,1,128,128]{3,2,1,0:T(8,128)S(1)} %get-tuple-element.15), channel_id=1, source_target_pairs={{0,32},{32,64},{64,96},{96,128},{128,160},{160,192},{192,224},{224... | collective-permute-start | bytes 983048 | tf_op jit(solution)/shard_map/ppermute | solution.py:38
  17.4 16.2 %collective-permute-start.1 = (f32[5,1,128,128]{3,2,1,0:T(8,128)S(1)}, f32[5,1,128,128]{3,2,1,0:T(8,128)}, u32[]{:S(2)}, u32[]{:S(2)}) collective-permute-start(f32[5,1,128,128]{3,2,1,0:T(8,128)S(1)} %get-tuple-element.16), channel_id=1, source_target_pairs={{32,0},{64,32},{96,64},{128,96},{160,128},{192,160},{224,192},{0,2... | collective-permute-start | bytes 983048 | tf_op jit(solution)/shard_map/ppermute | solution.py:39
  18.6 1.4 %copy-start.3 = (s32[1,4,4]{2,1,0:T(4,128)S(1)}, s32[1,4,4]{2,1,0:T(4,128)}, u32[]{:S(2)}) copy-start(s32[1,4,4]{2,1,0:T(4,128)} %param.14) | copy-start | bytes 196
  18.6 1.7 %copy-start.4 = (s32[1,4,4]{2,1,0:T(4,128)S(1)}, s32[1,4,4]{2,1,0:T(4,128)}, u32[]{:S(2)}) copy-start(s32[1,4,4]{2,1,0:T(4,128)} %param.16) | copy-start | bytes 196
  18.6 1.7 %copy-start.6 = (f32[16]{0:T(128)S(1)}, f32[16]{0:T(128)}, u32[]{:S(2)}) copy-start(f32[16]{0:T(128)} %param.17) | copy-start | bytes 196
  18.6 2.0 %copy-start.5 = (s32[1,4,4]{2,1,0:T(4,128)S(1)}, s32[1,4,4]{2,1,0:T(4,128)}, u32[]{:S(2)}) copy-start(s32[1,4,4]{2,1,0:T(4,128)} %param.15) | copy-start | bytes 196
  18.6 2.3 %copy-start.7 = (s32[128]{0:T(128)S(1)}, s32[128]{0:T(128)}, u32[]{:S(2)}) copy-start(s32[128]{0:T(128)} %param.13) | copy-start | bytes 1540
  18.6 2.6 %copy-start.2 = (f32[3,5,5]{2,0,1:T(4,128)S(1)}, f32[3,5,5]{2,0,1:T(4,128)}, u32[]{:S(2)}) copy-start(f32[3,5,5]{2,0,1:T(4,128)} %param.11) | copy-start | bytes 904
  23.7 19.5 %all-to-all-start.1 = ((f32[32,2,641]{2,1,0:T(2,128)}), f32[32,2,641]{2,1,0:T(2,128)S(1)}, u32[]{:S(2)}, u32[]{:S(2)}) async-start(f32[32,2,641]{2,1,0:T(2,128)} %copy.43), calls=%async_computation.1 | async-start | bytes 393216 | tf_op jit(solution)/shard_map/all_to_all | solution.py:225
  55.4 2.2 %copy-start.1 = (f32[5,4,128,128]{3,2,1,0:T(8,128)S(1)}, f32[5,4,128,128]{3,2,1,0:T(8,128)}, u32[]{:S(2)}) copy-start(f32[5,4,128,128]{3,2,1,0:T(8,128)} %shard_map.91) | copy-start | bytes 3932164
  57.5 8.9 %collective-permute-start.7 = (f32[5,4,1,128]{3,2,1,0:T(1,128)S(1)}, f32[5,4,1,128]{3,2,1,0:T(1,128)S(1)}, u32[]{:S(2)}, u32[]{:S(2)}) collective-permute-start(f32[5,4,1,128]{3,2,1,0:T(1,128)S(1)} %get-tuple-element.5), channel_id=1, source_target_pairs={{0,1},{1,2},{2,3},{3,4},{4,5},{5,6},{6,7},{7,8},{8,9},{9,10},{10,1... | collective-permute-start | bytes 30728 | tf_op jit(solution)/shard_map/ppermute | solution.py:38
  57.7 12.5 %collective-permute-start.4 = (f32[5,1,128,128]{3,2,1,0:T(8,128)S(1)}, f32[5,1,128,128]{3,2,1,0:T(8,128)S(1)}, u32[]{:S(2)}, u32[]{:S(2)}) collective-permute-start(f32[5,1,128,128]{3,2,1,0:T(8,128)S(1)} %get-tuple-element.9), channel_id=1, source_target_pairs={{0,32},{32,64},{64,96},{96,128},{128,160},{160,192},{192,224},{224... | collective-permute-start | bytes 983048 | tf_op jit(solution)/shard_map/ppermute | solution.py:38
  60.7 12.2 %collective-permute-start.5 = (f32[5,1,128,128]{3,2,1,0:T(8,128)S(1)}, f32[5,1,128,128]{3,2,1,0:T(8,128)S(1)}, u32[]{:S(2)}, u32[]{:S(2)}) collective-permute-start(f32[5,1,128,128]{3,2,1,0:T(8,128)S(1)} %get-tuple-element.10), channel_id=1, source_target_pairs={{32,0},{64,32},{96,64},{128,96},{160,128},{192,160},{224,192},{0,2... | collective-permute-start | bytes 983048 | tf_op jit(solution)/shard_map/ppermute | solution.py:39
  60.7 7.0 %collective-permute-start.6 = (f32[5,4,1,128]{3,2,1,0:T(1,128)S(1)}, f32[5,4,1,128]{3,2,1,0:T(1,128)S(1)}, u32[]{:S(2)}, u32[]{:S(2)}) collective-permute-start(f32[5,4,1,128]{3,2,1,0:T(1,128)S(1)} %get-tuple-element.6), channel_id=1, source_target_pairs={{1,0},{2,1},{3,2},{4,3},{5,4},{6,5},{7,6},{8,7},{9,8},{10,9},{11,1... | collective-permute-start | bytes 30728 | tf_op jit(solution)/shard_map/ppermute | solution.py:39

commit v9 on v8

--- a/solution.py
+++ b/solution.py
@@ -29,9 +29,18 @@
     return block
 
 
-def halo_parts(block):
+def halo_parts(block, span_edges=None):
     parts = []
     for axis, dim in (("circ", 1), ("span", 2)):
+        if dim == 2 and span_edges is not None:
+            count = lax.axis_size(axis)
+            forward = [(i, (i + 1) % count) for i in range(count)]
+            backward = [(target, source) for source, target in forward]
+            parts += [
+                lax.ppermute(span_edges[1], axis, forward),
+                lax.ppermute(span_edges[0], axis, backward),
+            ]
+            continue
         count = lax.axis_size(axis)
         forward = [(i, (i + 1) % count) for i in range(count)]
         backward = [(target, source) for source, target in forward]
@@ -56,7 +65,8 @@
 
 
 def stencil_kernel(
-    j_ref, c_ref, cu_ref, cd_ref, su_ref, sd_ref, prev_ref, rate_ref, inlet_ref, out_ref, inlet_scr
+    j_ref, c_ref, cu_ref, cd_ref, su_ref, sd_ref, prev_ref, rate_ref, inlet_ref,
+    out_ref, first_ref, last_ref, inlet_scr,
 ):
     span, axial = inlet_scr.shape[1:]
     for g in range(NF):
@@ -98,14 +108,26 @@
                 + 0.5 * convection
                 - viscosity * laplacian
             )
-            out_ref[f, 0, rows, :] = cur[f] - rate * residual
+            value = cur[f] - rate * residual
+            out_ref[f, 0, rows, :] = value
+
+            @pl.when(i == 0)
+            def _():
+                first_ref[f, 0, 0:1, :] = value[0:1]
+
+            @pl.when(i == chunks - 1)
+            def _():
+                last_ref[f, 0, 0:1, :] = value[7:8]
+
         return carry
 
-    lax.fori_loop(0, c_ref.shape[2] // 8, chunk, 0)
-
-
-def sweep(current, previous, rate_cells, inlet_rows, jacobians):
-    parts = halo_parts(current)
+    chunks = c_ref.shape[2] // 8
+    lax.fori_loop(0, chunks, chunk, 0)
+
+
+def sweep(current, previous, rate_cells, inlet_rows, jacobians, parts=None):
+    if parts is None:
+        parts = halo_parts(current)
     circ_low, circ_high, span_low, span_high = parts
     padded = jnp.concatenate([circ_low, current, circ_high], axis=1)
     span_up = jnp.concatenate([current[:, :, 1:], span_high], axis=2)
@@ -128,10 +150,12 @@
             pl.BlockSpec((1, nf, span), lambda t: (t, 0, 0)),
         ],
         scratch_shapes=[pltpu.VMEM((nf, span, axial), current.dtype)],
-        out_specs=spec(0),
-        out_shape=jax.ShapeDtypeStruct(current.shape, current.dtype),
+        out_specs=[spec(0)] + [pl.BlockSpec((nf, 1, 1, axial), lambda t: (0, t, 0, 0))] * 2,
+        out_shape=[jax.ShapeDtypeStruct(current.shape, current.dtype)]
+        + [jax.ShapeDtypeStruct((nf, rows, 1, axial), current.dtype)] * 2,
     )(jacobians.reshape(-1), padded, padded, padded, span_up, span_down, previous, rate_cells, inlet_rows)
-    return out, parts
+    out, first, last = out
+    return out, (first, last)
 
 
 def contract(matrix, values):
@@ -230,8 +254,9 @@
         jnp.sum(jnp.where(codes == slot_ids, values, 0.0), axis=0), (1, 0, 2, 3)
     ).reshape(rows_local, NF, KP_DEV * PW)
 
-    mid, _ = sweep(q_old, q_old, pseudo_rate, inlet_rows, flux_jacobians)
-    new, _ = sweep(mid, q_old, pseudo_rate, inlet_rows, flux_jacobians)
+    mid, mid_edges = sweep(q_old, q_old, pseudo_rate, inlet_rows, flux_jacobians)
+    mid_parts = halo_parts(mid, mid_edges)
+    new, _ = sweep(mid, q_old, pseudo_rate, inlet_rows, flux_jacobians, mid_parts)
     return new
 
 

time: 84.3 us -> 94.8 us (1.12)
  Pallas kernels: 18.3 us -> 28.7 us
  waiting for transfers between devices: 11.5 us -> 16.4 us
  starting transfers between devices: 30 us -> 25.6 us
    pallas_call x2, Pallas kernels: 18.3 us -> 28.7 us  [sweep(): pl.pallas_call(stencil_kernel, grid=(rows,), in_specs=[pl.BlockSpec(memor...]
    ppermute x4 -> x3, starting transfers between devices: 14 us -> 8.57 us  [halo_parts(): high = lax.ppermute(lax.slice_in_dim(block, 0, 1, axis=dim), axis, backward)]
    ppermute x0 -> x2, waiting for transfers between devices: none -> 3.24 us  [the longest x1 3.23 us: halo_parts(): lax.ppermute(span_edges[1], axis, forward)]
    ppermute x4 -> x3, waiting for transfers between devices: 0.29 us -> 1.92 us  [halo_parts(): lax.ppermute(lax.slice_in_dim(block, block.shape[dim] - 1, None, axis=dim...]
    concatenate x2, other arithmetic: 3.68 us -> 2.31 us  [sweep(): span_up = jnp.concatenate([current[:, :, 1:], span_high], axis=2)]
    concatenate x2, other arithmetic: 2.38 us -> 3.72 us  [sweep(): span_down = jnp.concatenate([span_low, current[:, :, :-1]], axis=2)]
    slice x4 -> x3, local copies, waits for them, and re-layouts: 3.05 us -> 2.21 us  [halo_parts(): lax.slice_in_dim(block, block.shape[dim] - 1, None, axis=dim)]
    ppermute x4 -> x3, starting transfers between devices: 4.07 us -> 4.59 us  [halo_parts(): lax.ppermute(lax.slice_in_dim(block, block.shape[dim] - 1, None, axis=dim...]
  transfers between devices with their start and end apart: 10 -> 10, of which waited for: 4 -> 4; matrix products, arithmetic and copies ran while one was open for 18% -> 19% of each run, Pallas kernels for 0% -> 0%
where the time goes in v9:
time: 94.8 us; the launch traced here: 94.3 us
  Pallas kernels  28.7 us (30%)
  starting transfers between devices  25.6 us (27%)
  waiting for transfers between devices  16.4 us (17%)
  other arithmetic  11.6 us (12%)
  local copies, waits for them, and re-layouts  11.2 us (12%)
    pallas_call x2, Pallas kernels, sweep(): pl.pallas_call(stencil_kernel, grid=(rows,), in_specs=[pl.BlockSpec(memor...  28.7 us
    ppermute x3, starting transfers between devices, halo_parts(): high = lax.ppermute(lax.slice_in_dim(block, 0, 1, axis=dim), axis, backward)  8.57 us
    all_to_all x1, starting transfers between devices, body(): received = lax.all_to_all(payload, 'span', 0, 0, tiled=True)  7.03 us
    all_to_all x1, waiting for transfers between devices, body(): received = lax.all_to_all(payload, 'span', 0, 0, tiled=True)  7.01 us
    all_to_all x1, starting transfers between devices, body(): gathered = lax.all_to_all(copies, 'circ', 0, 0, tiled=True)  4.89 us
    ppermute x3, starting transfers between devices, halo_parts(): lax.ppermute(lax.slice_in_dim(block, block.shape[dim] - 1, None, axis=dim...  4.59 us
    ppermute x3, waiting for transfers between devices, halo_parts(): high = lax.ppermute(lax.slice_in_dim(block, 0, 1, axis=dim), axis, backward)  4.26 us
    concatenate x2, other arithmetic, sweep(): padded = jnp.concatenate([circ_low, current, circ_high], axis=1)  4.11 us
  transfers between devices with their start and end apart: 10, of which 4 were waited for; matrix products, arithmetic and copies ran while one was open for 19% of the time, Pallas kernels for 0%

profile of v9, /device:TPU:6, one launch (start us, length us, event | category | flops | bytes accessed | tf_op | source)
XLA Modules:
  0.0 94.3 jit_solution(12799593258742836177)
XLA Ops:
  0.0 1.0 %fusion.6 = (f32[5,4,1,128]{3,2,1,0:T(1,128)S(1)}, f32[5,4,1,128]{3,2,1,0:T(1,128)S(1)}) fusion(f32[5,4,128,128]{3,2,1,0:T(8,128)} %prev_ref.3), kind=kLoop, calls=%fused_computation.46 | loop fusion | bytes 40960 | tf_op jit(solution)/shard_map/slice | solution.py:47
  1.1 8.0 %collective-permute-start.2 = (f32[5,4,1,128]{3,2,1,0:T(1,128)S(1)}, f32[5,4,1,128]{3,2,1,0:T(1,128)S(1)}, u32[]{:S(2)}, u32[]{:S(2)}) collective-permute-start(f32[5,4,1,128]{3,2,1,0:T(1,128)S(1)} %get-tuple-element.18), channel_id=1, source_target_pairs={{1,0},{2,1},{3,2},{4,3},{5,4},{6,5},{7,6},{8,7},{9,8},{10,9},{11,1... | collective-permute-start | bytes 30728 | tf_op jit(solution)/shard_map/ppermute | solution.py:48
  9.1 1.3 %broadcast_in_dim.94 = f32[8,5,4,128]{3,2,1,0:T(4,128)} broadcast(f32[5,4,128]{2,1,0:T(4,128)} %param.12), dimensions={1,2,3} | broadcast | bytes 92160 | tf_op jit(solution)/shard_map/broadcast_in_dim | solution.py:217
  10.5 4.9 %all-to-all-start = ((f32[8,5,4,128]{3,2,1,0:T(4,128)}), f32[8,5,4,128]{3,2,1,0:T(4,128)S(1)}, u32[]{:S(2)}, u32[]{:S(2)}) async-start(f32[8,5,4,128]{3,2,1,0:T(4,128)} %broadcast_in_dim.94), calls=%async_computation | async-start | bytes 163840 | tf_op jit(solution)/shard_map/all_to_all | solution.py:218
  15.4 1.1 %fusion.8 = (f32[5,1,128,128]{3,2,1,0:T(8,128)S(1)}, f32[5,1,128,128]{3,2,1,0:T(8,128)S(1)}) fusion(f32[5,4,128,128]{3,2,1,0:T(8,128)} %prev_ref.3), kind=kLoop, calls=%fused_computation.48 | loop fusion | bytes 1310720 | tf_op jit(solution)/shard_map/slice | solution.py:47
  16.5 1.5 %collective-permute-start = (f32[5,1,128,128]{3,2,1,0:T(8,128)S(1)}, f32[5,1,128,128]{3,2,1,0:T(8,128)}, u32[]{:S(2)}, u32[]{:S(2)}) collective-permute-start(f32[5,1,128,128]{3,2,1,0:T(8,128)S(1)} %get-tuple-element.21), channel_id=1, source_target_pairs={{0,32},{32,64},{64,96},{96,128},{128,160},{160,192},{192,224},{224... | collective-permute-start | bytes 983048 | tf_op jit(solution)/shard_map/ppermute | solution.py:47
  18.7 1.3 %fusion.7 = (f32[5,4,127,128]{3,2,1,0:T(8,128)}, f32[5,4,127,128]{3,2,1,0:T(8,128)S(1)}) fusion(f32[5,4,128,128]{3,2,1,0:T(8,128)S(1)} %copy-done), kind=kLoop, calls=%fused_computation.47 | loop fusion | bytes 5201920 | tf_op jit(solution)/shard_map/slice | solution.py:134
  22.7 0.8 copy.43
  23.5 7.0 %all-to-all-start.1 = ((f32[32,2,641]{2,1,0:T(2,128)}), f32[32,2,641]{2,1,0:T(2,128)S(1)}, u32[]{:S(2)}, u32[]{:S(2)}) async-start(f32[32,2,641]{2,1,0:T(2,128)} %copy.43), calls=%async_computation.1 | async-start | bytes 393216 | tf_op jit(solution)/shard_map/all_to_all | solution.py:249
  30.5 2.5 %pad_maximum_fusion.3.sd_ref = f32[5,4,128,128]{3,2,1,0:T(8,128)} fusion(f32[5,4,127,128]{3,2,1,0:T(8,128)} %get-tuple-element.19, f32[5,4,1,128]{3,2,1,0:T(1,128)S(1)} %broadcast_multiply_fusion.1), kind=kLoop, calls=%fused_computation.3 | loop fusion | flops 327680 | bytes 2621440 | tf_op jit(solution)/shard_map/concatenate | solution.py:134
  33.1 1.2 %pad_maximum_fusion.2.su_ref = f32[5,4,128,128]{3,2,1,0:T(8,128)} fusion(f32[5,4,1,128]{3,2,1,0:T(1,128)S(1)} %broadcast_multiply_fusion.3, f32[5,4,127,128]{3,2,1,0:T(8,128)S(1)} %get-tuple-element.20), kind=kLoop, calls=%fused_computation.2 | loop fusion | flops 327680 | bytes 2621440 | tf_op jit(solution)/shard_map/concatenate | solution.py:133
  34.2 2.6 %pad_maximum_fusion.c_ref.cu_ref.cd_ref = f32[5,6,128,128]{3,2,1,0:T(8,128)} fusion(f32[5,1,128,128]{3,2,1,0:T(8,128)} %collective-permute-done.1, f32[5,4,128,128]{3,2,1,0:T(8,128)S(1)} %copy-done, f32[5,1,128,128]{3,2,1,0:T(8,128)} %collective-permute-done), kind=kLoop, calls=%fused_computation | loop fusion | flops 983040 | bytes 3932160 | tf_op jit(solution)/shard_map/concatenate | solution.py:132
  36.8 7.0 %all-to-all-done.1 = f32[32,2,641]{2,1,0:T(2,128)S(1)} async-done(((f32[32,2,641]{2,1,0:T(2,128)}), f32[32,2,641]{2,1,0:T(2,128)S(1)}, u32[]{:S(2)}, u32[]{:S(2)}) %all-to-all-start.1) | async-done | bytes 164128 | tf_op jit(solution)/shard_map/all_to_all | solution.py:249
  45.9 14.4 %shard_map.91 = (f32[5,4,128,128]{3,2,1,0:T(8,128)}, f32[5,4,1,128]{3,2,1,0:T(1,128)}, f32[5,4,1,128]{3,2,1,0:T(1,128)}) custom-call(f32[75]{0:T(128)} %reshape.225.j_ref, f32[5,6,128,128]{3,2,1,0:T(8,128)} %pad_maximum_fusion.c_ref.cu_ref.cd_ref, f32[5,6,128,128]{3,2,1,0:T(8,128)} %pad_maximum_fusion.c_ref.cu_ref.cd_ref, ...), custom_call_target="tpu_custom_call" | custom-call | tf_op jit(solution)/shard_map/pallas_call | solution.py:138
  60.4 2.1 %fusion.4 = (f32[5,4,127,128]{3,2,1,0:T(8,128)S(1)}, f32[5,4,127,128]{3,2,1,0:T(8,128)S(1)}) fusion(f32[5,4,128,128]{3,2,1,0:T(8,128)} %get-tuple-element.9), kind=kLoop, calls=%fused_computation.44 | loop fusion | bytes 5201920 | tf_op jit(solution)/shard_map/slice | solution.py:134
  62.6 0.6 copy-done.8
  63.7 3.0 %collective-permute-start.4 = (f32[5,1,128,128]{3,2,1,0:T(8,128)S(1)}, f32[5,1,128,128]{3,2,1,0:T(8,128)S(1)}, u32[]{:S(2)}, u32[]{:S(2)}) collective-permute-start(f32[5,1,128,128]{3,2,1,0:T(8,128)S(1)} %get-tuple-element.15), channel_id=1, source_target_pairs={{0,32},{32,64},{64,96},{96,128},{128,160},{160,192},{192,224},{224... | collective-permute-start | bytes 983048 | tf_op jit(solution)/shard_map/ppermute | solution.py:47
  66.7 3.2 %collective-permute-done.7 = f32[5,4,1,128]{3,2,1,0:T(1,128)S(1)} collective-permute-done((f32[5,4,1,128]{3,2,1,0:T(1,128)S(1)}, f32[5,4,1,128]{3,2,1,0:T(1,128)S(1)}, u32[]{:S(2)}, u32[]{:S(2)}) %collective-permute-start.7) | collective-permute-done | bytes 10272 | tf_op jit(solution)/shard_map/ppermute | solution.py:40
  69.9 1.2 %pad_maximum_fusion.5.sd_ref = f32[5,4,128,128]{3,2,1,0:T(8,128)} fusion(f32[5,4,127,128]{3,2,1,0:T(8,128)S(1)} %get-tuple-element.13, f32[5,4,1,128]{3,2,1,0:T(1,128)S(1)} %broadcast_multiply_fusion), kind=kLoop, calls=%fused_computation.5 | loop fusion | flops 327680 | bytes 2621440 | tf_op jit(solution)/shard_map/concatenate | solution.py:134
  71.1 1.2 %pad_maximum_fusion.4.su_ref = f32[5,4,128,128]{3,2,1,0:T(8,128)} fusion(f32[5,4,1,128]{3,2,1,0:T(1,128)S(1)} %broadcast_multiply_fusion.2, f32[5,4,127,128]{3,2,1,0:T(8,128)S(1)} %get-tuple-element.14), kind=kLoop, calls=%fused_computation.4 | loop fusion | flops 327680 | bytes 2621440 | tf_op jit(solution)/shard_map/concatenate | solution.py:133
  72.3 1.9 %collective-permute-done.4 = f32[5,1,128,128]{3,2,1,0:T(8,128)S(1)} collective-permute-done((f32[5,1,128,128]{3,2,1,0:T(8,128)S(1)}, f32[5,1,128,128]{3,2,1,0:T(8,128)S(1)}, u32[]{:S(2)}, u32[]{:S(2)}) %collective-permute-start.4) | collective-permute-done | bytes 327712 | tf_op jit(solution)/shard_map/ppermute | solution.py:47
  74.2 4.3 %collective-permute-done.5 = f32[5,1,128,128]{3,2,1,0:T(8,128)S(1)} collective-permute-done((f32[5,1,128,128]{3,2,1,0:T(8,128)S(1)}, f32[5,1,128,128]{3,2,1,0:T(8,128)S(1)}, u32[]{:S(2)}, u32[]{:S(2)}) %collective-permute-start.5) | collective-permute-done | bytes 327712 | tf_op jit(solution)/shard_map/ppermute | solution.py:48
  78.4 1.5 %pad_maximum_fusion.1.c_ref.cu_ref.cd_ref = f32[5,6,128,128]{3,2,1,0:T(8,128)} fusion(f32[5,1,128,128]{3,2,1,0:T(8,128)S(1)} %collective-permute-done.5, f32[5,4,128,128]{3,2,1,0:T(8,128)S(1)} %copy-done.1, f32[5,1,128,128]{3,2,1,0:T(8,128)S(1)} %collective-permute-done.4), kind=kLoop, calls=%fused_computation.1 | loop fusion | flops 983040 | bytes 3932160 | tf_op jit(solution)/shard_map/concatenate | solution.py:132
  80.0 14.3 %shard_map.92 = (f32[5,4,128,128]{3,2,1,0:T(8,128)}, f32[5,4,1,128]{3,2,1,0:T(1,128)}, f32[5,4,1,128]{3,2,1,0:T(1,128)}) custom-call(f32[75]{0:T(128)} %reshape.225.j_ref, f32[5,6,128,128]{3,2,1,0:T(8,128)} %pad_maximum_fusion.1.c_ref.cu_ref.cd_ref, f32[5,6,128,128]{3,2,1,0:T(8,128)} %pad_maximum_fusion.1.c_ref.cu_ref.cd_ref, ...), custom_call_target="tpu_custom_call" | custom-call | tf_op jit(solution)/shard_map/pallas_call | solution.py:138
  (71 shorter events, 5.9 us)
Async XLA Ops:
  0.0 18.6 %copy-start = (f32[5,4,128,128]{3,2,1,0:T(8,128)S(1)}, f32[5,4,128,128]{3,2,1,0:T(8,128)}, u32[]{:S(2)}) copy-start(f32[5,4,128,128]{3,2,1,0:T(8,128)} %prev_ref.3) | copy-start | bytes 3932164
  1.1 20.9 %collective-permute-start.3 = (f32[5,4,1,128]{3,2,1,0:T(1,128)S(1)}, f32[5,4,1,128]{3,2,1,0:T(1,128)S(1)}, u32[]{:S(2)}, u32[]{:S(2)}) collective-permute-start(f32[5,4,1,128]{3,2,1,0:T(1,128)S(1)} %get-tuple-element.17), channel_id=1, source_target_pairs={{0,1},{1,2},{2,3},{3,4},{4,5},{5,6},{6,7},{7,8},{8,9},{9,10},{10,1... | collective-permute-start | bytes 30728 | tf_op jit(solution)/shard_map/ppermute | solution.py:47
  1.1 20.8 %collective-permute-start.2 = (f32[5,4,1,128]{3,2,1,0:T(1,128)S(1)}, f32[5,4,1,128]{3,2,1,0:T(1,128)S(1)}, u32[]{:S(2)}, u32[]{:S(2)}) collective-permute-start(f32[5,4,1,128]{3,2,1,0:T(1,128)S(1)} %get-tuple-element.18), channel_id=1, source_target_pairs={{1,0},{2,1},{3,2},{4,3},{5,4},{6,5},{7,6},{8,7},{9,8},{10,9},{11,1... | collective-permute-start | bytes 30728 | tf_op jit(solution)/shard_map/ppermute | solution.py:48
  10.5 11.5 %all-to-all-start = ((f32[8,5,4,128]{3,2,1,0:T(4,128)}), f32[8,5,4,128]{3,2,1,0:T(4,128)S(1)}, u32[]{:S(2)}, u32[]{:S(2)}) async-start(f32[8,5,4,128]{3,2,1,0:T(4,128)} %broadcast_in_dim.94), calls=%async_computation | async-start | bytes 163840 | tf_op jit(solution)/shard_map/all_to_all | solution.py:218
  16.5 17.7 %collective-permute-start = (f32[5,1,128,128]{3,2,1,0:T(8,128)S(1)}, f32[5,1,128,128]{3,2,1,0:T(8,128)}, u32[]{:S(2)}, u32[]{:S(2)}) collective-permute-start(f32[5,1,128,128]{3,2,1,0:T(8,128)S(1)} %get-tuple-element.21), channel_id=1, source_target_pairs={{0,32},{32,64},{64,96},{96,128},{128,160},{160,192},{192,224},{224... | collective-permute-start | bytes 983048 | tf_op jit(solution)/shard_map/ppermute | solution.py:47
  18.0 16.2 %collective-permute-start.1 = (f32[5,1,128,128]{3,2,1,0:T(8,128)S(1)}, f32[5,1,128,128]{3,2,1,0:T(8,128)}, u32[]{:S(2)}, u32[]{:S(2)}) collective-permute-start(f32[5,1,128,128]{3,2,1,0:T(8,128)S(1)} %get-tuple-element.22), channel_id=1, source_target_pairs={{32,0},{64,32},{96,64},{128,96},{160,128},{192,160},{224,192},{0,2... | collective-permute-start | bytes 983048 | tf_op jit(solution)/shard_map/ppermute | solution.py:48
  18.6 1.4 %copy-start.3 = (s32[1,4,4]{2,1,0:T(4,128)S(1)}, s32[1,4,4]{2,1,0:T(4,128)}, u32[]{:S(2)}) copy-start(s32[1,4,4]{2,1,0:T(4,128)} %param.14) | copy-start | bytes 196
  18.6 1.7 %copy-start.4 = (s32[1,4,4]{2,1,0:T(4,128)S(1)}, s32[1,4,4]{2,1,0:T(4,128)}, u32[]{:S(2)}) copy-start(s32[1,4,4]{2,1,0:T(4,128)} %param.15) | copy-start | bytes 196
  18.7 1.9 %copy-start.5 = (s32[1,4,4]{2,1,0:T(4,128)S(1)}, s32[1,4,4]{2,1,0:T(4,128)}, u32[]{:S(2)}) copy-start(s32[1,4,4]{2,1,0:T(4,128)} %param.16) | copy-start | bytes 196
  18.7 1.9 %copy-start.6 = (f32[16]{0:T(128)S(1)}, f32[16]{0:T(128)}, u32[]{:S(2)}) copy-start(f32[16]{0:T(128)} %param.17) | copy-start | bytes 196
  18.7 2.2 %copy-start.7 = (s32[128]{0:T(128)S(1)}, s32[128]{0:T(128)}, u32[]{:S(2)}) copy-start(s32[128]{0:T(128)} %param.13) | copy-start | bytes 1540
  18.7 2.5 %copy-start.2 = (f32[3,5,5]{2,0,1:T(4,128)S(1)}, f32[3,5,5]{2,0,1:T(4,128)}, u32[]{:S(2)}) copy-start(f32[3,5,5]{2,0,1:T(4,128)} %param.11) | copy-start | bytes 904
  23.5 20.3 %all-to-all-start.1 = ((f32[32,2,641]{2,1,0:T(2,128)}), f32[32,2,641]{2,1,0:T(2,128)S(1)}, u32[]{:S(2)}, u32[]{:S(2)}) async-start(f32[32,2,641]{2,1,0:T(2,128)} %copy.43), calls=%async_computation.1 | async-start | bytes 393216 | tf_op jit(solution)/shard_map/all_to_all | solution.py:249
  60.3 6.4 %collective-permute-start.6 = (f32[5,4,1,128]{3,2,1,0:T(1,128)}, f32[5,4,1,128]{3,2,1,0:T(1,128)S(1)}, u32[]{:S(2)}, u32[]{:S(2)}) collective-permute-start(f32[5,4,1,128]{3,2,1,0:T(1,128)} %get-tuple-element.10), channel_id=1, source_target_pairs={{1,0},{2,1},{3,2},{4,3},{5,4},{6,5},{7,6},{8,7},{9,8},{10,9},{11,1... | collective-permute-start | bytes 30728 | tf_op jit(solution)/shard_map/ppermute | solution.py:41
  60.4 2.1 %copy-start.1 = (f32[5,4,128,128]{3,2,1,0:T(8,128)S(1)}, f32[5,4,128,128]{3,2,1,0:T(8,128)}, u32[]{:S(2)}) copy-start(f32[5,4,128,128]{3,2,1,0:T(8,128)} %get-tuple-element.9) | copy-start | bytes 3932164
  62.5 0.7 copy-start.8
  63.2 6.7 %collective-permute-start.7 = (f32[5,4,1,128]{3,2,1,0:T(1,128)S(1)}, f32[5,4,1,128]{3,2,1,0:T(1,128)S(1)}, u32[]{:S(2)}, u32[]{:S(2)}) collective-permute-start(f32[5,4,1,128]{3,2,1,0:T(1,128)S(1)} %copy-done.8), channel_id=1, source_target_pairs={{0,1},{1,2},{2,3},{3,4},{4,5},{5,6},{6,7},{7,8},{8,9},{9,10},{10,1... | collective-permute-start | bytes 30728 | tf_op jit(solution)/shard_map/ppermute | solution.py:40
  63.7 10.5 %collective-permute-start.4 = (f32[5,1,128,128]{3,2,1,0:T(8,128)S(1)}, f32[5,1,128,128]{3,2,1,0:T(8,128)S(1)}, u32[]{:S(2)}, u32[]{:S(2)}) collective-permute-start(f32[5,1,128,128]{3,2,1,0:T(8,128)S(1)} %get-tuple-element.15), channel_id=1, source_target_pairs={{0,32},{32,64},{64,96},{96,128},{128,160},{160,192},{192,224},{224... | collective-permute-start | bytes 983048 | tf_op jit(solution)/shard_map/ppermute | solution.py:47
  66.7 11.8 %collective-permute-start.5 = (f32[5,1,128,128]{3,2,1,0:T(8,128)S(1)}, f32[5,1,128,128]{3,2,1,0:T(8,128)S(1)}, u32[]{:S(2)}, u32[]{:S(2)}) collective-permute-start(f32[5,1,128,128]{3,2,1,0:T(8,128)S(1)} %get-tuple-element.16), channel_id=1, source_target_pairs={{32,0},{64,32},{96,64},{128,96},{160,128},{192,160},{224,192},{0,2... | collective-permute-start | bytes 983048 | tf_op jit(solution)/shard_map/ppermute | solution.py:48

commit v10 on v9

--- a/solution.py
+++ b/solution.py
@@ -108,21 +108,12 @@
                 + 0.5 * convection
                 - viscosity * laplacian
             )
-            value = cur[f] - rate * residual
-            out_ref[f, 0, rows, :] = value
-
-            @pl.when(i == 0)
-            def _():
-                first_ref[f, 0, 0:1, :] = value[0:1]
-
-            @pl.when(i == chunks - 1)
-            def _():
-                last_ref[f, 0, 0:1, :] = value[7:8]
-
+            out_ref[f, 0, rows, :] = cur[f] - rate * residual
         return carry
 
-    chunks = c_ref.shape[2] // 8
-    lax.fori_loop(0, chunks, chunk, 0)
+    lax.fori_loop(0, c_ref.shape[2] // 8, chunk, 0)
+    first_ref[...] = out_ref[:, :, 0:1, :]
+    last_ref[...] = out_ref[:, :, span - 1 : span, :]
 
 
 def sweep(current, previous, rate_cells, inlet_rows, jacobians, parts=None):

time: 94.8 us -> 84.5 us (0.89)
  Pallas kernels: 28.7 us -> 18.5 us
    pallas_call x2, Pallas kernels: 28.7 us -> 18.5 us  [sweep(): pl.pallas_call(stencil_kernel, grid=(rows,), in_specs=[pl.BlockSpec(memor...]
  transfers between devices with their start and end apart: 10 -> 10, of which waited for: 4 -> 4; matrix products, arithmetic and copies ran while one was open for 19% -> 21% of each run, Pallas kernels for 0% -> 0%
where the time goes in v10:
time: 84.5 us; the launch traced here: 84.1 us
  starting transfers between devices  25.6 us (30%)
  Pallas kernels  18.5 us (22%)
  waiting for transfers between devices  16.4 us (19%)
  other arithmetic  11.6 us (14%)
  local copies, waits for them, and re-layouts  11.2 us (13%)
    pallas_call x2, Pallas kernels, sweep(): pl.pallas_call(stencil_kernel, grid=(rows,), in_specs=[pl.BlockSpec(memor...  18.5 us
    ppermute x3, starting transfers between devices, halo_parts(): high = lax.ppermute(lax.slice_in_dim(block, 0, 1, axis=dim), axis, backward)  8.57 us
    all_to_all x1, starting transfers between devices, body(): received = lax.all_to_all(payload, 'span', 0, 0, tiled=True)  7.03 us
    all_to_all x1, waiting for transfers between devices, body(): received = lax.all_to_all(payload, 'span', 0, 0, tiled=True)  7.01 us
    all_to_all x1, starting transfers between devices, body(): gathered = lax.all_to_all(copies, 'circ', 0, 0, tiled=True)  4.89 us
    ppermute x3, starting transfers between devices, halo_parts(): lax.ppermute(lax.slice_in_dim(block, block.shape[dim] - 1, None, axis=dim...  4.59 us
    ppermute x3, waiting for transfers between devices, halo_parts(): high = lax.ppermute(lax.slice_in_dim(block, 0, 1, axis=dim), axis, backward)  4.26 us
    concatenate x2, other arithmetic, sweep(): padded = jnp.concatenate([circ_low, current, circ_high], axis=1)  4.11 us
  transfers between devices with their start and end apart: 10, of which 4 were waited for; matrix products, arithmetic and copies ran while one was open for 21% of the time, Pallas kernels for 0%

profile of v10, /device:TPU:6, one launch (start us, length us, event | category | flops | bytes accessed | tf_op | source)
XLA Modules:
  0.0 84.1 jit_solution(13595878920473139135)
XLA Ops:
  0.0 1.0 %fusion.6 = (f32[5,4,1,128]{3,2,1,0:T(1,128)S(1)}, f32[5,4,1,128]{3,2,1,0:T(1,128)S(1)}) fusion(f32[5,4,128,128]{3,2,1,0:T(8,128)} %prev_ref.3), kind=kLoop, calls=%fused_computation.46 | loop fusion | bytes 40960 | tf_op jit(solution)/shard_map/slice | solution.py:47
  1.1 8.0 %collective-permute-start.2 = (f32[5,4,1,128]{3,2,1,0:T(1,128)S(1)}, f32[5,4,1,128]{3,2,1,0:T(1,128)S(1)}, u32[]{:S(2)}, u32[]{:S(2)}) collective-permute-start(f32[5,4,1,128]{3,2,1,0:T(1,128)S(1)} %get-tuple-element.18), channel_id=1, source_target_pairs={{1,0},{2,1},{3,2},{4,3},{5,4},{6,5},{7,6},{8,7},{9,8},{10,9},{11,1... | collective-permute-start | bytes 30728 | tf_op jit(solution)/shard_map/ppermute | solution.py:48
  9.1 1.3 %broadcast_in_dim.94 = f32[8,5,4,128]{3,2,1,0:T(4,128)} broadcast(f32[5,4,128]{2,1,0:T(4,128)} %param.12), dimensions={1,2,3} | broadcast | bytes 92160 | tf_op jit(solution)/shard_map/broadcast_in_dim | solution.py:208
  10.5 4.9 %all-to-all-start = ((f32[8,5,4,128]{3,2,1,0:T(4,128)}), f32[8,5,4,128]{3,2,1,0:T(4,128)S(1)}, u32[]{:S(2)}, u32[]{:S(2)}) async-start(f32[8,5,4,128]{3,2,1,0:T(4,128)} %broadcast_in_dim.94), calls=%async_computation | async-start | bytes 163840 | tf_op jit(solution)/shard_map/all_to_all | solution.py:209
  15.4 1.1 %fusion.8 = (f32[5,1,128,128]{3,2,1,0:T(8,128)S(1)}, f32[5,1,128,128]{3,2,1,0:T(8,128)S(1)}) fusion(f32[5,4,128,128]{3,2,1,0:T(8,128)} %prev_ref.3), kind=kLoop, calls=%fused_computation.48 | loop fusion | bytes 1310720 | tf_op jit(solution)/shard_map/slice | solution.py:47
  16.5 1.5 %collective-permute-start = (f32[5,1,128,128]{3,2,1,0:T(8,128)S(1)}, f32[5,1,128,128]{3,2,1,0:T(8,128)}, u32[]{:S(2)}, u32[]{:S(2)}) collective-permute-start(f32[5,1,128,128]{3,2,1,0:T(8,128)S(1)} %get-tuple-element.21), channel_id=1, source_target_pairs={{0,32},{32,64},{64,96},{96,128},{128,160},{160,192},{192,224},{224... | collective-permute-start | bytes 983048 | tf_op jit(solution)/shard_map/ppermute | solution.py:47
  18.7 1.3 %fusion.7 = (f32[5,4,127,128]{3,2,1,0:T(8,128)}, f32[5,4,127,128]{3,2,1,0:T(8,128)S(1)}) fusion(f32[5,4,128,128]{3,2,1,0:T(8,128)S(1)} %copy-done), kind=kLoop, calls=%fused_computation.47 | loop fusion | bytes 5201920 | tf_op jit(solution)/shard_map/slice | solution.py:125
  22.7 0.8 copy.43
  23.5 7.0 %all-to-all-start.1 = ((f32[32,2,641]{2,1,0:T(2,128)}), f32[32,2,641]{2,1,0:T(2,128)S(1)}, u32[]{:S(2)}, u32[]{:S(2)}) async-start(f32[32,2,641]{2,1,0:T(2,128)} %copy.43), calls=%async_computation.1 | async-start | bytes 393216 | tf_op jit(solution)/shard_map/all_to_all | solution.py:240
  30.5 2.5 %pad_maximum_fusion.3.sd_ref = f32[5,4,128,128]{3,2,1,0:T(8,128)} fusion(f32[5,4,127,128]{3,2,1,0:T(8,128)} %get-tuple-element.19, f32[5,4,1,128]{3,2,1,0:T(1,128)S(1)} %broadcast_multiply_fusion.1), kind=kLoop, calls=%fused_computation.3 | loop fusion | flops 327680 | bytes 2621440 | tf_op jit(solution)/shard_map/concatenate | solution.py:125
  33.1 1.2 %pad_maximum_fusion.2.su_ref = f32[5,4,128,128]{3,2,1,0:T(8,128)} fusion(f32[5,4,1,128]{3,2,1,0:T(1,128)S(1)} %broadcast_multiply_fusion.3, f32[5,4,127,128]{3,2,1,0:T(8,128)S(1)} %get-tuple-element.20), kind=kLoop, calls=%fused_computation.2 | loop fusion | flops 327680 | bytes 2621440 | tf_op jit(solution)/shard_map/concatenate | solution.py:124
  34.2 2.6 %pad_maximum_fusion.c_ref.cu_ref.cd_ref = f32[5,6,128,128]{3,2,1,0:T(8,128)} fusion(f32[5,1,128,128]{3,2,1,0:T(8,128)} %collective-permute-done.1, f32[5,4,128,128]{3,2,1,0:T(8,128)S(1)} %copy-done, f32[5,1,128,128]{3,2,1,0:T(8,128)} %collective-permute-done), kind=kLoop, calls=%fused_computation | loop fusion | flops 983040 | bytes 3932160 | tf_op jit(solution)/shard_map/concatenate | solution.py:123
  36.8 7.0 %all-to-all-done.1 = f32[32,2,641]{2,1,0:T(2,128)S(1)} async-done(((f32[32,2,641]{2,1,0:T(2,128)}), f32[32,2,641]{2,1,0:T(2,128)S(1)}, u32[]{:S(2)}, u32[]{:S(2)}) %all-to-all-start.1) | async-done | bytes 164128 | tf_op jit(solution)/shard_map/all_to_all | solution.py:240
  45.9 9.3 %shard_map.91 = (f32[5,4,128,128]{3,2,1,0:T(8,128)}, f32[5,4,1,128]{3,2,1,0:T(1,128)}, f32[5,4,1,128]{3,2,1,0:T(1,128)}) custom-call(f32[75]{0:T(128)} %reshape.225.j_ref, f32[5,6,128,128]{3,2,1,0:T(8,128)} %pad_maximum_fusion.c_ref.cu_ref.cd_ref, f32[5,6,128,128]{3,2,1,0:T(8,128)} %pad_maximum_fusion.c_ref.cu_ref.cd_ref, ...), custom_call_target="tpu_custom_call" | custom-call | tf_op jit(solution)/shard_map/pallas_call | solution.py:129
  55.3 2.1 %fusion.4 = (f32[5,4,127,128]{3,2,1,0:T(8,128)S(1)}, f32[5,4,127,128]{3,2,1,0:T(8,128)S(1)}) fusion(f32[5,4,128,128]{3,2,1,0:T(8,128)} %get-tuple-element.9), kind=kLoop, calls=%fused_computation.44 | loop fusion | bytes 5201920 | tf_op jit(solution)/shard_map/slice | solution.py:125
  57.5 0.6 copy-done.8
  58.6 3.0 %collective-permute-start.4 = (f32[5,1,128,128]{3,2,1,0:T(8,128)S(1)}, f32[5,1,128,128]{3,2,1,0:T(8,128)S(1)}, u32[]{:S(2)}, u32[]{:S(2)}) collective-permute-start(f32[5,1,128,128]{3,2,1,0:T(8,128)S(1)} %get-tuple-element.15), channel_id=1, source_target_pairs={{0,32},{32,64},{64,96},{96,128},{128,160},{160,192},{192,224},{224... | collective-permute-start | bytes 983048 | tf_op jit(solution)/shard_map/ppermute | solution.py:47
  61.6 3.2 %collective-permute-done.7 = f32[5,4,1,128]{3,2,1,0:T(1,128)S(1)} collective-permute-done((f32[5,4,1,128]{3,2,1,0:T(1,128)S(1)}, f32[5,4,1,128]{3,2,1,0:T(1,128)S(1)}, u32[]{:S(2)}, u32[]{:S(2)}) %collective-permute-start.7) | collective-permute-done | bytes 10272 | tf_op jit(solution)/shard_map/ppermute | solution.py:40
  64.8 1.2 %pad_maximum_fusion.5.sd_ref = f32[5,4,128,128]{3,2,1,0:T(8,128)} fusion(f32[5,4,127,128]{3,2,1,0:T(8,128)S(1)} %get-tuple-element.13, f32[5,4,1,128]{3,2,1,0:T(1,128)S(1)} %broadcast_multiply_fusion), kind=kLoop, calls=%fused_computation.5 | loop fusion | flops 327680 | bytes 2621440 | tf_op jit(solution)/shard_map/concatenate | solution.py:125
  66.0 1.2 %pad_maximum_fusion.4.su_ref = f32[5,4,128,128]{3,2,1,0:T(8,128)} fusion(f32[5,4,1,128]{3,2,1,0:T(1,128)S(1)} %broadcast_multiply_fusion.2, f32[5,4,127,128]{3,2,1,0:T(8,128)S(1)} %get-tuple-element.14), kind=kLoop, calls=%fused_computation.4 | loop fusion | flops 327680 | bytes 2621440 | tf_op jit(solution)/shard_map/concatenate | solution.py:124
  67.2 1.9 %collective-permute-done.4 = f32[5,1,128,128]{3,2,1,0:T(8,128)S(1)} collective-permute-done((f32[5,1,128,128]{3,2,1,0:T(8,128)S(1)}, f32[5,1,128,128]{3,2,1,0:T(8,128)S(1)}, u32[]{:S(2)}, u32[]{:S(2)}) %collective-permute-start.4) | collective-permute-done | bytes 327712 | tf_op jit(solution)/shard_map/ppermute | solution.py:47
  69.1 4.3 %collective-permute-done.5 = f32[5,1,128,128]{3,2,1,0:T(8,128)S(1)} collective-permute-done((f32[5,1,128,128]{3,2,1,0:T(8,128)S(1)}, f32[5,1,128,128]{3,2,1,0:T(8,128)S(1)}, u32[]{:S(2)}, u32[]{:S(2)}) %collective-permute-start.5) | collective-permute-done | bytes 327712 | tf_op jit(solution)/shard_map/ppermute | solution.py:48
  73.3 1.5 %pad_maximum_fusion.1.c_ref.cu_ref.cd_ref = f32[5,6,128,128]{3,2,1,0:T(8,128)} fusion(f32[5,1,128,128]{3,2,1,0:T(8,128)S(1)} %collective-permute-done.5, f32[5,4,128,128]{3,2,1,0:T(8,128)S(1)} %copy-done.1, f32[5,1,128,128]{3,2,1,0:T(8,128)S(1)} %collective-permute-done.4), kind=kLoop, calls=%fused_computation.1 | loop fusion | flops 983040 | bytes 3932160 | tf_op jit(solution)/shard_map/concatenate | solution.py:123
  74.9 9.2 %shard_map.92 = (f32[5,4,128,128]{3,2,1,0:T(8,128)}, f32[5,4,1,128]{3,2,1,0:T(1,128)}, f32[5,4,1,128]{3,2,1,0:T(1,128)}) custom-call(f32[75]{0:T(128)} %reshape.225.j_ref, f32[5,6,128,128]{3,2,1,0:T(8,128)} %pad_maximum_fusion.1.c_ref.cu_ref.cd_ref, f32[5,6,128,128]{3,2,1,0:T(8,128)} %pad_maximum_fusion.1.c_ref.cu_ref.cd_ref, ...), custom_call_target="tpu_custom_call" | custom-call | tf_op jit(solution)/shard_map/pallas_call | solution.py:129
  (71 shorter events, 5.9 us)
Async XLA Ops:
  0.0 18.6 %copy-start = (f32[5,4,128,128]{3,2,1,0:T(8,128)S(1)}, f32[5,4,128,128]{3,2,1,0:T(8,128)}, u32[]{:S(2)}) copy-start(f32[5,4,128,128]{3,2,1,0:T(8,128)} %prev_ref.3) | copy-start | bytes 3932164
  1.1 20.9 %collective-permute-start.3 = (f32[5,4,1,128]{3,2,1,0:T(1,128)S(1)}, f32[5,4,1,128]{3,2,1,0:T(1,128)S(1)}, u32[]{:S(2)}, u32[]{:S(2)}) collective-permute-start(f32[5,4,1,128]{3,2,1,0:T(1,128)S(1)} %get-tuple-element.17), channel_id=1, source_target_pairs={{0,1},{1,2},{2,3},{3,4},{4,5},{5,6},{6,7},{7,8},{8,9},{9,10},{10,1... | collective-permute-start | bytes 30728 | tf_op jit(solution)/shard_map/ppermute | solution.py:47
  1.1 20.8 %collective-permute-start.2 = (f32[5,4,1,128]{3,2,1,0:T(1,128)S(1)}, f32[5,4,1,128]{3,2,1,0:T(1,128)S(1)}, u32[]{:S(2)}, u32[]{:S(2)}) collective-permute-start(f32[5,4,1,128]{3,2,1,0:T(1,128)S(1)} %get-tuple-element.18), channel_id=1, source_target_pairs={{1,0},{2,1},{3,2},{4,3},{5,4},{6,5},{7,6},{8,7},{9,8},{10,9},{11,1... | collective-permute-start | bytes 30728 | tf_op jit(solution)/shard_map/ppermute | solution.py:48
  10.5 11.5 %all-to-all-start = ((f32[8,5,4,128]{3,2,1,0:T(4,128)}), f32[8,5,4,128]{3,2,1,0:T(4,128)S(1)}, u32[]{:S(2)}, u32[]{:S(2)}) async-start(f32[8,5,4,128]{3,2,1,0:T(4,128)} %broadcast_in_dim.94), calls=%async_computation | async-start | bytes 163840 | tf_op jit(solution)/shard_map/all_to_all | solution.py:209
  16.5 17.7 %collective-permute-start = (f32[5,1,128,128]{3,2,1,0:T(8,128)S(1)}, f32[5,1,128,128]{3,2,1,0:T(8,128)}, u32[]{:S(2)}, u32[]{:S(2)}) collective-permute-start(f32[5,1,128,128]{3,2,1,0:T(8,128)S(1)} %get-tuple-element.21), channel_id=1, source_target_pairs={{0,32},{32,64},{64,96},{96,128},{128,160},{160,192},{192,224},{224... | collective-permute-start | bytes 983048 | tf_op jit(solution)/shard_map/ppermute | solution.py:47
  18.0 16.2 %collective-permute-start.1 = (f32[5,1,128,128]{3,2,1,0:T(8,128)S(1)}, f32[5,1,128,128]{3,2,1,0:T(8,128)}, u32[]{:S(2)}, u32[]{:S(2)}) collective-permute-start(f32[5,1,128,128]{3,2,1,0:T(8,128)S(1)} %get-tuple-element.22), channel_id=1, source_target_pairs={{32,0},{64,32},{96,64},{128,96},{160,128},{192,160},{224,192},{0,2... | collective-permute-start | bytes 983048 | tf_op jit(solution)/shard_map/ppermute | solution.py:48
  18.6 1.4 %copy-start.3 = (s32[1,4,4]{2,1,0:T(4,128)S(1)}, s32[1,4,4]{2,1,0:T(4,128)}, u32[]{:S(2)}) copy-start(s32[1,4,4]{2,1,0:T(4,128)} %param.14) | copy-start | bytes 196
  18.6 1.7 %copy-start.4 = (s32[1,4,4]{2,1,0:T(4,128)S(1)}, s32[1,4,4]{2,1,0:T(4,128)}, u32[]{:S(2)}) copy-start(s32[1,4,4]{2,1,0:T(4,128)} %param.15) | copy-start | bytes 196
  18.7 1.9 %copy-start.5 = (s32[1,4,4]{2,1,0:T(4,128)S(1)}, s32[1,4,4]{2,1,0:T(4,128)}, u32[]{:S(2)}) copy-start(s32[1,4,4]{2,1,0:T(4,128)} %param.16) | copy-start | bytes 196
  18.7 1.9 %copy-start.6 = (f32[16]{0:T(128)S(1)}, f32[16]{0:T(128)}, u32[]{:S(2)}) copy-start(f32[16]{0:T(128)} %param.17) | copy-start | bytes 196
  18.7 2.2 %copy-start.7 = (s32[128]{0:T(128)S(1)}, s32[128]{0:T(128)}, u32[]{:S(2)}) copy-start(s32[128]{0:T(128)} %param.13) | copy-start | bytes 1540
  18.7 2.5 %copy-start.2 = (f32[3,5,5]{2,0,1:T(4,128)S(1)}, f32[3,5,5]{2,0,1:T(4,128)}, u32[]{:S(2)}) copy-start(f32[3,5,5]{2,0,1:T(4,128)} %param.11) | copy-start | bytes 904
  23.5 20.3 %all-to-all-start.1 = ((f32[32,2,641]{2,1,0:T(2,128)}), f32[32,2,641]{2,1,0:T(2,128)S(1)}, u32[]{:S(2)}, u32[]{:S(2)}) async-start(f32[32,2,641]{2,1,0:T(2,128)} %copy.43), calls=%async_computation.1 | async-start | bytes 393216 | tf_op jit(solution)/shard_map/all_to_all | solution.py:240
  55.2 6.4 %collective-permute-start.6 = (f32[5,4,1,128]{3,2,1,0:T(1,128)}, f32[5,4,1,128]{3,2,1,0:T(1,128)S(1)}, u32[]{:S(2)}, u32[]{:S(2)}) collective-permute-start(f32[5,4,1,128]{3,2,1,0:T(1,128)} %get-tuple-element.10), channel_id=1, source_target_pairs={{1,0},{2,1},{3,2},{4,3},{5,4},{6,5},{7,6},{8,7},{9,8},{10,9},{11,1... | collective-permute-start | bytes 30728 | tf_op jit(solution)/shard_map/ppermute | solution.py:41
  55.3 2.1 %copy-start.1 = (f32[5,4,128,128]{3,2,1,0:T(8,128)S(1)}, f32[5,4,128,128]{3,2,1,0:T(8,128)}, u32[]{:S(2)}) copy-start(f32[5,4,128,128]{3,2,1,0:T(8,128)} %get-tuple-element.9) | copy-start | bytes 3932164
  57.4 0.7 copy-start.8
  58.1 6.7 %collective-permute-start.7 = (f32[5,4,1,128]{3,2,1,0:T(1,128)S(1)}, f32[5,4,1,128]{3,2,1,0:T(1,128)S(1)}, u32[]{:S(2)}, u32[]{:S(2)}) collective-permute-start(f32[5,4,1,128]{3,2,1,0:T(1,128)S(1)} %copy-done.8), channel_id=1, source_target_pairs={{0,1},{1,2},{2,3},{3,4},{4,5},{5,6},{6,7},{7,8},{8,9},{9,10},{10,1... | collective-permute-start | bytes 30728 | tf_op jit(solution)/shard_map/ppermute | solution.py:40
  58.6 10.5 %collective-permute-start.4 = (f32[5,1,128,128]{3,2,1,0:T(8,128)S(1)}, f32[5,1,128,128]{3,2,1,0:T(8,128)S(1)}, u32[]{:S(2)}, u32[]{:S(2)}) collective-permute-start(f32[5,1,128,128]{3,2,1,0:T(8,128)S(1)} %get-tuple-element.15), channel_id=1, source_target_pairs={{0,32},{32,64},{64,96},{96,128},{128,160},{160,192},{192,224},{224... | collective-permute-start | bytes 983048 | tf_op jit(solution)/shard_map/ppermute | solution.py:47
  61.6 11.8 %collective-permute-start.5 = (f32[5,1,128,128]{3,2,1,0:T(8,128)S(1)}, f32[5,1,128,128]{3,2,1,0:T(8,128)S(1)}, u32[]{:S(2)}, u32[]{:S(2)}) collective-permute-start(f32[5,1,128,128]{3,2,1,0:T(8,128)S(1)} %get-tuple-element.16), channel_id=1, source_target_pairs={{32,0},{64,32},{96,64},{128,96},{160,128},{192,160},{224,192},{0,2... | collective-permute-start | bytes 983048 | tf_op jit(solution)/shard_map/ppermute | solution.py:48

commit v11 on v10

--- a/solution.py
+++ b/solution.py
@@ -29,17 +29,15 @@
     return block
 
 
-def halo_parts(block, span_edges=None):
+def halo_parts(block, edges=None):
     parts = []
     for axis, dim in (("circ", 1), ("span", 2)):
-        if dim == 2 and span_edges is not None:
+        if edges is not None:
             count = lax.axis_size(axis)
             forward = [(i, (i + 1) % count) for i in range(count)]
             backward = [(target, source) for source, target in forward]
-            parts += [
-                lax.ppermute(span_edges[1], axis, forward),
-                lax.ppermute(span_edges[0], axis, backward),
-            ]
+            first, last = edges[2:] if dim == 1 else edges[:2]
+            parts += [lax.ppermute(last, axis, forward), lax.ppermute(first, axis, backward)]
             continue
         count = lax.axis_size(axis)
         forward = [(i, (i + 1) % count) for i in range(count)]
@@ -66,7 +64,7 @@
 
 def stencil_kernel(
     j_ref, c_ref, cu_ref, cd_ref, su_ref, sd_ref, prev_ref, rate_ref, inlet_ref,
-    out_ref, first_ref, last_ref, inlet_scr,
+    out_ref, first_ref, last_ref, top_ref, bottom_ref, inlet_scr,
 ):
     span, axial = inlet_scr.shape[1:]
     for g in range(NF):
@@ -115,6 +113,14 @@
     first_ref[...] = out_ref[:, :, 0:1, :]
     last_ref[...] = out_ref[:, :, span - 1 : span, :]
 
+    @pl.when(pl.program_id(0) == 0)
+    def _():
+        top_ref[...] = out_ref[...]
+
+    @pl.when(pl.program_id(0) == pl.num_programs(0) - 1)
+    def _():
+        bottom_ref[...] = out_ref[...]
+
 
 def sweep(current, previous, rate_cells, inlet_rows, jacobians, parts=None):
     if parts is None:
@@ -141,12 +147,15 @@
             pl.BlockSpec((1, nf, span), lambda t: (t, 0, 0)),
         ],
         scratch_shapes=[pltpu.VMEM((nf, span, axial), current.dtype)],
-        out_specs=[spec(0)] + [pl.BlockSpec((nf, 1, 1, axial), lambda t: (0, t, 0, 0))] * 2,
+        out_specs=[spec(0)]
+        + [pl.BlockSpec((nf, 1, 1, axial), lambda t: (0, t, 0, 0))] * 2
+        + [pl.BlockSpec(block, lambda t: (0, 0, 0, 0))] * 2,
         out_shape=[jax.ShapeDtypeStruct(current.shape, current.dtype)]
-        + [jax.ShapeDtypeStruct((nf, rows, 1, axial), current.dtype)] * 2,
+        + [jax.ShapeDtypeStruct((nf, rows, 1, axial), current.dtype)] * 2
+        + [jax.ShapeDtypeStruct(block, current.dtype)] * 2,
     )(jacobians.reshape(-1), padded, padded, padded, span_up, span_down, previous, rate_cells, inlet_rows)
-    out, first, last = out
-    return out, (first, last)
+    out, first, last, top, bottom = out
+    return out, (first, last, top, bottom)
 
 
 def contract(matrix, values):

time: 84.5 us -> 82.7 us (0.979)
  waiting for transfers between devices: 16.4 us -> 14.7 us
    ppermute x2 -> x4, waiting for transfers between devices: 3.24 us -> 7.67 us  [the longest x2 4.16 us: halo_parts(): lax.ppermute(first, axis, backward)]
    ppermute x3 -> x2, waiting for transfers between devices: 4.26 us -> 0.01 us  [halo_parts(): high = lax.ppermute(lax.slice_in_dim(block, 0, 1, axis=dim), axis, backward)]
    ppermute x2 -> x4, starting transfers between devices: 0.57 us -> 3.55 us  [the longest x2 3.46 us: halo_parts(): lax.ppermute(last, axis, forward)]
    ppermute x3 -> x2, starting transfers between devices: 4.59 us -> 1.62 us  [halo_parts(): lax.ppermute(lax.slice_in_dim(block, block.shape[dim] - 1, None, axis=dim...]
    ppermute x3 -> x2, waiting for transfers between devices: 1.92 us -> 0.01 us  [halo_parts(): lax.ppermute(lax.slice_in_dim(block, block.shape[dim] - 1, None, axis=dim...]
    slice x3 -> x2, local copies, waits for them, and re-layouts: 2.21 us -> 2.16 us  [halo_parts(): lax.slice_in_dim(block, block.shape[dim] - 1, None, axis=dim)]
    ppermute x3 -> x2, starting transfers between devices: 8.57 us -> 8.56 us  [halo_parts(): high = lax.ppermute(lax.slice_in_dim(block, 0, 1, axis=dim), axis, backward)]
  transfers between devices with their start and end apart: 10 -> 10, of which waited for: 4 -> 4; matrix products, arithmetic and copies ran while one was open for 21% -> 22% of each run, Pallas kernels for 0% -> 0%
where the time goes in v11:
time: 82.7 us; the launch traced here: 82.2 us
  starting transfers between devices  25.7 us (31%)
  Pallas kernels  19.2 us (23%)
  waiting for transfers between devices  14.7 us (18%)
  other arithmetic  11.6 us (14%)
  local copies, waits for them, and re-layouts  10.4 us (13%)
    pallas_call x2, Pallas kernels, sweep(): pl.pallas_call(stencil_kernel, grid=(rows,), in_specs=[pl.BlockSpec(memor...  19.2 us
    ppermute x2, starting transfers between devices, halo_parts(): high = lax.ppermute(lax.slice_in_dim(block, 0, 1, axis=dim), axis, backward)  8.56 us
    all_to_all x1, starting transfers between devices, body(): received = lax.all_to_all(payload, 'span', 0, 0, tiled=True)  7.03 us
    all_to_all x1, waiting for transfers between devices, body(): received = lax.all_to_all(payload, 'span', 0, 0, tiled=True)  7.01 us
    all_to_all x1, starting transfers between devices, body(): gathered = lax.all_to_all(copies, 'circ', 0, 0, tiled=True)  4.89 us
    ppermute x2, waiting for transfers between devices, halo_parts(): lax.ppermute(first, axis, backward)  4.16 us
    concatenate x2, other arithmetic, sweep(): padded = jnp.concatenate([circ_low, current, circ_high], axis=1)  4.07 us
    concatenate x2, other arithmetic, sweep(): span_down = jnp.concatenate([span_low, current[:, :, :-1]], axis=2)  3.76 us
  transfers between devices with their start and end apart: 10, of which 4 were waited for; matrix products, arithmetic and copies ran while one was open for 22% of the time, Pallas kernels for 0%

profile of v11, /device:TPU:6, one launch (start us, length us, event | category | flops | bytes accessed | tf_op | source)
XLA Modules:
  0.0 82.2 jit_solution(18208247922227731189)
XLA Ops:
  0.0 1.0 %fusion.5 = (f32[5,4,1,128]{3,2,1,0:T(1,128)S(1)}, f32[5,4,1,128]{3,2,1,0:T(1,128)S(1)}) fusion(f32[5,4,128,128]{3,2,1,0:T(8,128)} %prev_ref.3), kind=kLoop, calls=%fused_computation.45 | loop fusion | bytes 40960 | tf_op jit(solution)/shard_map/slice | solution.py:45
  1.1 8.0 %collective-permute-start.2 = (f32[5,4,1,128]{3,2,1,0:T(1,128)S(1)}, f32[5,4,1,128]{3,2,1,0:T(1,128)S(1)}, u32[]{:S(2)}, u32[]{:S(2)}) collective-permute-start(f32[5,4,1,128]{3,2,1,0:T(1,128)S(1)} %get-tuple-element.20), channel_id=1, source_target_pairs={{1,0},{2,1},{3,2},{4,3},{5,4},{6,5},{7,6},{8,7},{9,8},{10,9},{11,1... | collective-permute-start | bytes 30728 | tf_op jit(solution)/shard_map/ppermute | solution.py:46
  9.1 1.3 %broadcast_in_dim.94 = f32[8,5,4,128]{3,2,1,0:T(4,128)} broadcast(f32[5,4,128]{2,1,0:T(4,128)} %param.12), dimensions={1,2,3} | broadcast | bytes 92160 | tf_op jit(solution)/shard_map/broadcast_in_dim | solution.py:217
  10.5 4.9 %all-to-all-start = ((f32[8,5,4,128]{3,2,1,0:T(4,128)}), f32[8,5,4,128]{3,2,1,0:T(4,128)S(1)}, u32[]{:S(2)}, u32[]{:S(2)}) async-start(f32[8,5,4,128]{3,2,1,0:T(4,128)} %broadcast_in_dim.94), calls=%async_computation | async-start | bytes 163840 | tf_op jit(solution)/shard_map/all_to_all | solution.py:218
  15.4 1.1 %fusion.7 = (f32[5,1,128,128]{3,2,1,0:T(8,128)S(1)}, f32[5,1,128,128]{3,2,1,0:T(8,128)S(1)}) fusion(f32[5,4,128,128]{3,2,1,0:T(8,128)} %prev_ref.3), kind=kLoop, calls=%fused_computation.47 | loop fusion | bytes 1310720 | tf_op jit(solution)/shard_map/slice | solution.py:45
  16.5 1.5 %collective-permute-start = (f32[5,1,128,128]{3,2,1,0:T(8,128)S(1)}, f32[5,1,128,128]{3,2,1,0:T(8,128)}, u32[]{:S(2)}, u32[]{:S(2)}) collective-permute-start(f32[5,1,128,128]{3,2,1,0:T(8,128)S(1)} %get-tuple-element.23), channel_id=1, source_target_pairs={{0,32},{32,64},{64,96},{96,128},{128,160},{160,192},{192,224},{224... | collective-permute-start | bytes 983048 | tf_op jit(solution)/shard_map/ppermute | solution.py:45
  18.7 1.3 %fusion.6 = (f32[5,4,127,128]{3,2,1,0:T(8,128)}, f32[5,4,127,128]{3,2,1,0:T(8,128)S(1)}) fusion(f32[5,4,128,128]{3,2,1,0:T(8,128)S(1)} %copy-done), kind=kLoop, calls=%fused_computation.46 | loop fusion | bytes 5201920 | tf_op jit(solution)/shard_map/slice | solution.py:131
  22.7 0.8 %copy.43 = f32[32,2,641]{2,1,0:T(2,128)} copy(f32[32,2,641]{2,0,1:T(8,128)S(1)} %pad_maximum_fusion.6) | data formatting | bytes 328192 | tf_op jit(solution)/shard_map/concatenate | solution.py:246
  23.5 7.0 %all-to-all-start.1 = ((f32[32,2,641]{2,1,0:T(2,128)}), f32[32,2,641]{2,1,0:T(2,128)S(1)}, u32[]{:S(2)}, u32[]{:S(2)}) async-start(f32[32,2,641]{2,1,0:T(2,128)} %copy.43), calls=%async_computation.1 | async-start | bytes 393216 | tf_op jit(solution)/shard_map/all_to_all | solution.py:249
  30.5 2.5 %pad_maximum_fusion.3.sd_ref = f32[5,4,128,128]{3,2,1,0:T(8,128)} fusion(f32[5,4,127,128]{3,2,1,0:T(8,128)} %get-tuple-element.21, f32[5,4,1,128]{3,2,1,0:T(1,128)S(1)} %broadcast_multiply_fusion.1), kind=kLoop, calls=%fused_computation.3 | loop fusion | flops 327680 | bytes 2621440 | tf_op jit(solution)/shard_map/concatenate | solution.py:131
  33.1 1.2 %pad_maximum_fusion.2.su_ref = f32[5,4,128,128]{3,2,1,0:T(8,128)} fusion(f32[5,4,1,128]{3,2,1,0:T(1,128)S(1)} %broadcast_multiply_fusion.3, f32[5,4,127,128]{3,2,1,0:T(8,128)S(1)} %get-tuple-element.22), kind=kLoop, calls=%fused_computation.2 | loop fusion | flops 327680 | bytes 2621440 | tf_op jit(solution)/shard_map/concatenate | solution.py:130
  34.2 2.6 %pad_maximum_fusion.c_ref.cu_ref.cd_ref = f32[5,6,128,128]{3,2,1,0:T(8,128)} fusion(f32[5,1,128,128]{3,2,1,0:T(8,128)} %collective-permute-done.1, f32[5,4,128,128]{3,2,1,0:T(8,128)S(1)} %copy-done, f32[5,1,128,128]{3,2,1,0:T(8,128)} %collective-permute-done), kind=kLoop, calls=%fused_computation | loop fusion | flops 983040 | bytes 3932160 | tf_op jit(solution)/shard_map/concatenate | solution.py:129
  36.8 7.0 %all-to-all-done.1 = f32[32,2,641]{2,1,0:T(2,128)S(1)} async-done(((f32[32,2,641]{2,1,0:T(2,128)}), f32[32,2,641]{2,1,0:T(2,128)S(1)}, u32[]{:S(2)}, u32[]{:S(2)}) %all-to-all-start.1) | async-done | bytes 164128 | tf_op jit(solution)/shard_map/all_to_all | solution.py:249
  45.3 0.6 copy.45.inlet_ref
  45.9 9.6 %shard_map.91 = (f32[5,4,128,128]{3,2,1,0:T(8,128)}, f32[5,4,1,128]{3,2,1,0:T(1,128)}, f32[5,4,1,128]{3,2,1,0:T(1,128)}, f32[5,1,128,128]{3,2,1,0:T(8,128)}, f32[5,1,128,128]{3,2,1,0:T(8,128)}) custom-call(f32[75]{0:T(128)} %reshape.225.j_ref, f32[5,6,128,128]{3,2,1,0:T(8,128)} %pad_maximum_fusion.c_ref.cu_ref.cd_ref, ...), custom_call_target="tpu_custom_call" | custom-call | tf_op jit(solution)/shard_map/pallas_call | solution.py:135
  56.1 3.0 %collective-permute-start.4 = (f32[5,1,128,128]{3,2,1,0:T(8,128)}, f32[5,1,128,128]{3,2,1,0:T(8,128)S(1)}, u32[]{:S(2)}, u32[]{:S(2)}) collective-permute-start(f32[5,1,128,128]{3,2,1,0:T(8,128)} %get-tuple-element.11), channel_id=1, source_target_pairs={{0,32},{32,64},{64,96},{96,128},{128,160},{160,192},{192,224},{224... | collective-permute-start | bytes 983048 | tf_op jit(solution)/shard_map/ppermute | solution.py:40
  59.1 1.9 %fusion.4 = (f32[5,4,127,128]{3,2,1,0:T(8,128)S(1)}, f32[5,4,127,128]{3,2,1,0:T(8,128)S(1)}) fusion(f32[5,4,128,128]{3,2,1,0:T(8,128)} %get-tuple-element.12), kind=kLoop, calls=%fused_computation.44 | loop fusion | bytes 5201920 | tf_op jit(solution)/shard_map/slice | solution.py:131
  61.1 1.6 %collective-permute-done.7 = f32[5,4,1,128]{3,2,1,0:T(1,128)S(1)} collective-permute-done((f32[5,4,1,128]{3,2,1,0:T(1,128)}, f32[5,4,1,128]{3,2,1,0:T(1,128)S(1)}, u32[]{:S(2)}, u32[]{:S(2)}) %collective-permute-start.7) | collective-permute-done | bytes 10272 | tf_op jit(solution)/shard_map/ppermute | solution.py:40
  62.6 1.2 %pad_maximum_fusion.5.sd_ref = f32[5,4,128,128]{3,2,1,0:T(8,128)} fusion(f32[5,4,127,128]{3,2,1,0:T(8,128)S(1)} %get-tuple-element.17, f32[5,4,1,128]{3,2,1,0:T(1,128)S(1)} %broadcast_multiply_fusion), kind=kLoop, calls=%fused_computation.5 | loop fusion | flops 327680 | bytes 2621440 | tf_op jit(solution)/shard_map/concatenate | solution.py:131
  63.8 1.2 %pad_maximum_fusion.4.su_ref = f32[5,4,128,128]{3,2,1,0:T(8,128)} fusion(f32[5,4,1,128]{3,2,1,0:T(1,128)S(1)} %broadcast_multiply_fusion.2, f32[5,4,127,128]{3,2,1,0:T(8,128)S(1)} %get-tuple-element.18), kind=kLoop, calls=%fused_computation.4 | loop fusion | flops 327680 | bytes 2621440 | tf_op jit(solution)/shard_map/concatenate | solution.py:130
  65.0 2.0 %collective-permute-done.4 = f32[5,1,128,128]{3,2,1,0:T(8,128)S(1)} collective-permute-done((f32[5,1,128,128]{3,2,1,0:T(8,128)}, f32[5,1,128,128]{3,2,1,0:T(8,128)S(1)}, u32[]{:S(2)}, u32[]{:S(2)}) %collective-permute-start.4) | collective-permute-done | bytes 327712 | tf_op jit(solution)/shard_map/ppermute | solution.py:40
  67.0 4.2 %collective-permute-done.5 = f32[5,1,128,128]{3,2,1,0:T(8,128)S(1)} collective-permute-done((f32[5,1,128,128]{3,2,1,0:T(8,128)}, f32[5,1,128,128]{3,2,1,0:T(8,128)S(1)}, u32[]{:S(2)}, u32[]{:S(2)}) %collective-permute-start.5) | collective-permute-done | bytes 327712 | tf_op jit(solution)/shard_map/ppermute | solution.py:40
  71.1 1.5 %pad_maximum_fusion.1.c_ref.cu_ref.cd_ref = f32[5,6,128,128]{3,2,1,0:T(8,128)} fusion(f32[5,1,128,128]{3,2,1,0:T(8,128)S(1)} %collective-permute-done.5, f32[5,4,128,128]{3,2,1,0:T(8,128)S(1)} %copy-done.1, f32[5,1,128,128]{3,2,1,0:T(8,128)S(1)} %collective-permute-done.4), kind=kLoop, calls=%fused_computation.1 | loop fusion | flops 983040 | bytes 3932160 | tf_op jit(solution)/shard_map/concatenate | solution.py:129
  72.6 9.6 %shard_map.92 = (f32[5,4,128,128]{3,2,1,0:T(8,128)}, f32[5,4,1,128]{3,2,1,0:T(1,128)}, f32[5,4,1,128]{3,2,1,0:T(1,128)}, f32[5,1,128,128]{3,2,1,0:T(8,128)}, f32[5,1,128,128]{3,2,1,0:T(8,128)}) custom-call(f32[75]{0:T(128)} %reshape.225.j_ref, f32[5,6,128,128]{3,2,1,0:T(8,128)} %pad_maximum_fusion.1.c_ref.cu_ref.cd_ref, ...), custom_call_target="tpu_custom_call" | custom-call | tf_op jit(solution)/shard_map/pallas_call | solution.py:135
  (68 shorter events, 5.3 us)
Async XLA Ops:
  0.0 18.6 %copy-start = (f32[5,4,128,128]{3,2,1,0:T(8,128)S(1)}, f32[5,4,128,128]{3,2,1,0:T(8,128)}, u32[]{:S(2)}) copy-start(f32[5,4,128,128]{3,2,1,0:T(8,128)} %prev_ref.3) | copy-start | bytes 3932164
  1.1 20.8 %collective-permute-start.3 = (f32[5,4,1,128]{3,2,1,0:T(1,128)S(1)}, f32[5,4,1,128]{3,2,1,0:T(1,128)S(1)}, u32[]{:S(2)}, u32[]{:S(2)}) collective-permute-start(f32[5,4,1,128]{3,2,1,0:T(1,128)S(1)} %get-tuple-element.19), channel_id=1, source_target_pairs={{0,1},{1,2},{2,3},{3,4},{4,5},{5,6},{6,7},{7,8},{8,9},{9,10},{10,1... | collective-permute-start | bytes 30728 | tf_op jit(solution)/shard_map/ppermute | solution.py:45
  1.1 20.8 %collective-permute-start.2 = (f32[5,4,1,128]{3,2,1,0:T(1,128)S(1)}, f32[5,4,1,128]{3,2,1,0:T(1,128)S(1)}, u32[]{:S(2)}, u32[]{:S(2)}) collective-permute-start(f32[5,4,1,128]{3,2,1,0:T(1,128)S(1)} %get-tuple-element.20), channel_id=1, source_target_pairs={{1,0},{2,1},{3,2},{4,3},{5,4},{6,5},{7,6},{8,7},{9,8},{10,9},{11,1... | collective-permute-start | bytes 30728 | tf_op jit(solution)/shard_map/ppermute | solution.py:46
  10.5 11.5 %all-to-all-start = ((f32[8,5,4,128]{3,2,1,0:T(4,128)}), f32[8,5,4,128]{3,2,1,0:T(4,128)S(1)}, u32[]{:S(2)}, u32[]{:S(2)}) async-start(f32[8,5,4,128]{3,2,1,0:T(4,128)} %broadcast_in_dim.94), calls=%async_computation | async-start | bytes 163840 | tf_op jit(solution)/shard_map/all_to_all | solution.py:218
  16.5 17.7 %collective-permute-start = (f32[5,1,128,128]{3,2,1,0:T(8,128)S(1)}, f32[5,1,128,128]{3,2,1,0:T(8,128)}, u32[]{:S(2)}, u32[]{:S(2)}) collective-permute-start(f32[5,1,128,128]{3,2,1,0:T(8,128)S(1)} %get-tuple-element.23), channel_id=1, source_target_pairs={{0,32},{32,64},{64,96},{96,128},{128,160},{160,192},{192,224},{224... | collective-permute-start | bytes 983048 | tf_op jit(solution)/shard_map/ppermute | solution.py:45
  18.0 16.2 %collective-permute-start.1 = (f32[5,1,128,128]{3,2,1,0:T(8,128)S(1)}, f32[5,1,128,128]{3,2,1,0:T(8,128)}, u32[]{:S(2)}, u32[]{:S(2)}) collective-permute-start(f32[5,1,128,128]{3,2,1,0:T(8,128)S(1)} %get-tuple-element.24), channel_id=1, source_target_pairs={{32,0},{64,32},{96,64},{128,96},{160,128},{192,160},{224,192},{0,2... | collective-permute-start | bytes 983048 | tf_op jit(solution)/shard_map/ppermute | solution.py:46
  18.6 1.4 %copy-start.3 = (s32[1,4,4]{2,1,0:T(4,128)S(1)}, s32[1,4,4]{2,1,0:T(4,128)}, u32[]{:S(2)}) copy-start(s32[1,4,4]{2,1,0:T(4,128)} %param.14) | copy-start | bytes 196
  18.6 1.7 %copy-start.4 = (s32[1,4,4]{2,1,0:T(4,128)S(1)}, s32[1,4,4]{2,1,0:T(4,128)}, u32[]{:S(2)}) copy-start(s32[1,4,4]{2,1,0:T(4,128)} %param.15) | copy-start | bytes 196
  18.7 1.9 %copy-start.5 = (s32[1,4,4]{2,1,0:T(4,128)S(1)}, s32[1,4,4]{2,1,0:T(4,128)}, u32[]{:S(2)}) copy-start(s32[1,4,4]{2,1,0:T(4,128)} %param.16) | copy-start | bytes 196
  18.7 1.9 %copy-start.6 = (f32[16]{0:T(128)S(1)}, f32[16]{0:T(128)}, u32[]{:S(2)}) copy-start(f32[16]{0:T(128)} %param.17) | copy-start | bytes 196
  18.7 2.2 %copy-start.7 = (s32[128]{0:T(128)S(1)}, s32[128]{0:T(128)}, u32[]{:S(2)}) copy-start(s32[128]{0:T(128)} %param.13) | copy-start | bytes 1540
  18.7 2.5 %copy-start.2 = (f32[3,5,5]{2,0,1:T(4,128)S(1)}, f32[3,5,5]{2,0,1:T(4,128)}, u32[]{:S(2)}) copy-start(f32[3,5,5]{2,0,1:T(4,128)} %param.11) | copy-start | bytes 904
  23.5 20.3 %all-to-all-start.1 = ((f32[32,2,641]{2,1,0:T(2,128)}), f32[32,2,641]{2,1,0:T(2,128)S(1)}, u32[]{:S(2)}, u32[]{:S(2)}) async-start(f32[32,2,641]{2,1,0:T(2,128)} %copy.43), calls=%async_computation.1 | async-start | bytes 393216 | tf_op jit(solution)/shard_map/all_to_all | solution.py:249
  55.5 5.5 %collective-permute-start.6 = (f32[5,4,1,128]{3,2,1,0:T(1,128)}, f32[5,4,1,128]{3,2,1,0:T(1,128)S(1)}, u32[]{:S(2)}, u32[]{:S(2)}) collective-permute-start(f32[5,4,1,128]{3,2,1,0:T(1,128)} %get-tuple-element.14), channel_id=1, source_target_pairs={{1,0},{2,1},{3,2},{4,3},{5,4},{6,5},{7,6},{8,7},{9,8},{10,9},{11,1... | collective-permute-start | bytes 30728 | tf_op jit(solution)/shard_map/ppermute | solution.py:40
  55.6 7.0 %collective-permute-start.7 = (f32[5,4,1,128]{3,2,1,0:T(1,128)}, f32[5,4,1,128]{3,2,1,0:T(1,128)S(1)}, u32[]{:S(2)}, u32[]{:S(2)}) collective-permute-start(f32[5,4,1,128]{3,2,1,0:T(1,128)} %get-tuple-element.15), channel_id=1, source_target_pairs={{0,1},{1,2},{2,3},{3,4},{4,5},{5,6},{6,7},{7,8},{8,9},{9,10},{10,1... | collective-permute-start | bytes 30728 | tf_op jit(solution)/shard_map/ppermute | solution.py:40
  56.1 10.9 %collective-permute-start.4 = (f32[5,1,128,128]{3,2,1,0:T(8,128)}, f32[5,1,128,128]{3,2,1,0:T(8,128)S(1)}, u32[]{:S(2)}, u32[]{:S(2)}) collective-permute-start(f32[5,1,128,128]{3,2,1,0:T(8,128)} %get-tuple-element.11), channel_id=1, source_target_pairs={{0,32},{32,64},{64,96},{96,128},{128,160},{160,192},{192,224},{224... | collective-permute-start | bytes 983048 | tf_op jit(solution)/shard_map/ppermute | solution.py:40
  59.1 12.1 %collective-permute-start.5 = (f32[5,1,128,128]{3,2,1,0:T(8,128)}, f32[5,1,128,128]{3,2,1,0:T(8,128)S(1)}, u32[]{:S(2)}, u32[]{:S(2)}) collective-permute-start(f32[5,1,128,128]{3,2,1,0:T(8,128)} %get-tuple-element.13), channel_id=1, source_target_pairs={{32,0},{64,32},{96,64},{128,96},{160,128},{192,160},{224,192},{0,2... | collective-permute-start | bytes 983048 | tf_op jit(solution)/shard_map/ppermute | solution.py:40
  63.8 7.3 %copy-start.1 = (f32[5,4,128,128]{3,2,1,0:T(8,128)S(1)}, f32[5,4,128,128]{3,2,1,0:T(8,128)}, u32[]{:S(2)}) copy-start(f32[5,4,128,128]{3,2,1,0:T(8,128)} %get-tuple-element.12) | copy-start | bytes 3932164

commit v12 on v11

--- a/solution.py
+++ b/solution.py
@@ -127,8 +127,9 @@
         parts = halo_parts(current)
     circ_low, circ_high, span_low, span_high = parts
     padded = jnp.concatenate([circ_low, current, circ_high], axis=1)
-    span_up = jnp.concatenate([current[:, :, 1:], span_high], axis=2)
-    span_down = jnp.concatenate([span_low, current[:, :, :-1]], axis=2)
+    span_row = lax.broadcasted_iota(jnp.int32, current.shape, 2)
+    span_up = jnp.where(span_row == current.shape[2] - 1, span_high, jnp.roll(current, -1, axis=2))
+    span_down = jnp.where(span_row == 0, span_low, jnp.roll(current, 1, axis=2))
     nf, rows, span, axial = current.shape
     block = (nf, 1, span, axial)
     spec = lambda shift: pl.BlockSpec(block, lambda t: (0, t + shift, 0, 0))

time: 82.7 us -> 87.4 us (1.057)
  waiting for transfers between devices: 14.7 us -> 19.3 us
    concatenate x4 -> x0, other arithmetic: 6.08 us -> none  [the longest x2 3.76 us: sweep(): span_down = jnp.concatenate([span_low, current[:, :, :-1]], axis=2)]
    select_n x0 -> x3, other arithmetic: none -> 5.87 us  [the longest x2 3.19 us: sweep(): jnp.where(span_row == current.shape[2] - 1, span_high, jnp.roll(current,...]
    all_to_all x1, waiting for transfers between devices: 7.01 us -> 9.44 us  [body(): received = lax.all_to_all(payload, 'span', 0, 0, tiled=True)]
    ppermute x2, waiting for transfers between devices: 3.51 us -> 5.57 us  [halo_parts(): lax.ppermute(last, axis, forward)]
    slice x2 -> x3, local copies, waits for them, and re-layouts: 3.24 us -> 3.45 us  [sweep(): span_down = jnp.where(span_row == 0, span_low, jnp.roll(current, 1, axis=2))]
  transfers between devices with their start and end apart: 10 -> 10, of which waited for: 4 -> 4; matrix products, arithmetic and copies ran while one was open for 22% -> 20% of each run, Pallas kernels for 0% -> 0%
where the time goes in v12:
time: 87.4 us; the launch traced here: 87 us
  starting transfers between devices  25.7 us (29%)
  waiting for transfers between devices  19.3 us (22%)
  Pallas kernels  19.2 us (22%)
  other arithmetic  11.4 us (13%)
  local copies, waits for them, and re-layouts  10.6 us (12%)
    pallas_call x2, Pallas kernels, sweep(): pl.pallas_call(stencil_kernel, grid=(rows,), in_specs=[pl.BlockSpec(memor...  19.2 us
    all_to_all x1, waiting for transfers between devices, body(): received = lax.all_to_all(payload, 'span', 0, 0, tiled=True)  9.44 us
    ppermute x2, starting transfers between devices, halo_parts(): high = lax.ppermute(lax.slice_in_dim(block, 0, 1, axis=dim), axis, backward)  8.56 us
    all_to_all x1, starting transfers between devices, body(): received = lax.all_to_all(payload, 'span', 0, 0, tiled=True)  7.03 us
    ppermute x2, waiting for transfers between devices, halo_parts(): lax.ppermute(last, axis, forward)  5.57 us
    all_to_all x1, starting transfers between devices, body(): gathered = lax.all_to_all(copies, 'circ', 0, 0, tiled=True)  4.89 us
    ppermute x2, waiting for transfers between devices, halo_parts(): lax.ppermute(first, axis, backward)  4.26 us
    concatenate x2, other arithmetic, sweep(): padded = jnp.concatenate([circ_low, current, circ_high], axis=1)  4.09 us
  transfers between devices with their start and end apart: 10, of which 4 were waited for; matrix products, arithmetic and copies ran while one was open for 20% of the time, Pallas kernels for 0%

profile of v12, /device:TPU:6, one launch (start us, length us, event | category | flops | bytes accessed | tf_op | source)
XLA Modules:
  0.0 87.0 jit_solution(14185191509549478301)
XLA Ops:
  0.0 1.0 %fusion.6 = (f32[5,4,1,128]{3,2,1,0:T(1,128)S(1)}, f32[5,4,1,128]{3,2,1,0:T(1,128)S(1)}) fusion(f32[5,4,128,128]{3,2,1,0:T(8,128)} %prev_ref.3), kind=kLoop, calls=%fused_computation.48 | loop fusion | bytes 40960 | tf_op jit(solution)/shard_map/slice | solution.py:45
  1.1 8.0 %collective-permute-start.2 = (f32[5,4,1,128]{3,2,1,0:T(1,128)S(1)}, f32[5,4,1,128]{3,2,1,0:T(1,128)S(1)}, u32[]{:S(2)}, u32[]{:S(2)}) collective-permute-start(f32[5,4,1,128]{3,2,1,0:T(1,128)S(1)} %get-tuple-element.22), channel_id=1, source_target_pairs={{1,0},{2,1},{3,2},{4,3},{5,4},{6,5},{7,6},{8,7},{9,8},{10,9},{11,1... | collective-permute-start | bytes 30728 | tf_op jit(solution)/shard_map/ppermute | solution.py:46
  9.1 1.3 %broadcast_in_dim.129 = f32[8,5,4,128]{3,2,1,0:T(4,128)} broadcast(f32[5,4,128]{2,1,0:T(4,128)} %param.12), dimensions={1,2,3} | broadcast | bytes 92160 | tf_op jit(solution)/shard_map/broadcast_in_dim | solution.py:218
  10.5 4.9 %all-to-all-start = ((f32[8,5,4,128]{3,2,1,0:T(4,128)}), f32[8,5,4,128]{3,2,1,0:T(4,128)S(1)}, u32[]{:S(2)}, u32[]{:S(2)}) async-start(f32[8,5,4,128]{3,2,1,0:T(4,128)} %broadcast_in_dim.129), calls=%async_computation | async-start | bytes 163840 | tf_op jit(solution)/shard_map/all_to_all | solution.py:219
  15.4 1.1 %fusion.8 = (f32[5,1,128,128]{3,2,1,0:T(8,128)S(1)}, f32[5,1,128,128]{3,2,1,0:T(8,128)S(1)}) fusion(f32[5,4,128,128]{3,2,1,0:T(8,128)} %prev_ref.3), kind=kLoop, calls=%fused_computation.50 | loop fusion | bytes 1310720 | tf_op jit(solution)/shard_map/slice | solution.py:45
  16.5 1.5 %collective-permute-start = (f32[5,1,128,128]{3,2,1,0:T(8,128)S(1)}, f32[5,1,128,128]{3,2,1,0:T(8,128)}, u32[]{:S(2)}, u32[]{:S(2)}) collective-permute-start(f32[5,1,128,128]{3,2,1,0:T(8,128)S(1)} %get-tuple-element.25), channel_id=1, source_target_pairs={{0,32},{32,64},{64,96},{96,128},{128,160},{160,192},{192,224},{224... | collective-permute-start | bytes 983048 | tf_op jit(solution)/shard_map/ppermute | solution.py:45
  18.7 1.3 %fusion.7 = (f32[5,4,127,128]{3,2,1,0:T(8,128)}, f32[5,4,127,128]{3,2,1,0:T(8,128)S(1)}) fusion(f32[5,4,128,128]{3,2,1,0:T(8,128)S(1)} %copy-done), kind=kLoop, calls=%fused_computation.49 | loop fusion | bytes 5201920 | tf_op jit(solution)/shard_map/jit(_roll_static)/slice | solution.py:132
  21.2 0.6 reshape.225.j_ref
  22.0 2.7 %maximum_select_fusion.1.sd_ref = f32[5,4,128,128]{3,2,1,0:T(8,128)} fusion(f32[5,4,127,128]{3,2,1,0:T(8,128)} %get-tuple-element.23, f32[5,4,1,128]{3,2,1,0:T(1,128)S(1)} %get-tuple-element.21, f32[5,4,128]{2,1,0:T(4,128)S(1)} %bitcast.20, pred[128]{0:T(512)(128)(4,1)S(1)} %iota_compare_fusion.6), kind=kLoop, calls=%fused_computation.3 | loop fusion | flops 655360 | bytes 2631808 | tf_op jit(solution)/shard_map/jit(_where)/select_n | solution.py:132
  25.4 0.8 copy.43
  26.2 7.0 %all-to-all-start.1 = ((f32[32,2,641]{2,1,0:T(2,128)}), f32[32,2,641]{2,1,0:T(2,128)S(1)}, u32[]{:S(2)}, u32[]{:S(2)}) async-start(f32[32,2,641]{2,1,0:T(2,128)} %copy.43), calls=%async_computation.1 | async-start | bytes 393216 | tf_op jit(solution)/shard_map/all_to_all | solution.py:250
  33.2 1.3 %maximum_select_fusion.su_ref = f32[5,4,128,128]{3,2,1,0:T(8,128)} fusion(f32[5,4,1,128]{3,2,1,0:T(1,128)S(1)} %get-tuple-element.22, f32[5,4,127,128]{3,2,1,0:T(8,128)S(1)} %get-tuple-element.24, f32[5,4,128]{2,1,0:T(4,128)S(1)} %bitcast.19, pred[128]{0:T(512)(128)(4,1)S(1)} %iota_compare_fusion.7), kind=kLoop, calls=%fused_computation.2 | loop fusion | flops 655360 | bytes 2631808 | tf_op jit(solution)/shard_map/jit(_where)/select_n | solution.py:131
  34.5 2.6 %pad_maximum_fusion.c_ref.cu_ref.cd_ref = f32[5,6,128,128]{3,2,1,0:T(8,128)} fusion(f32[5,1,128,128]{3,2,1,0:T(8,128)} %collective-permute-done.1, f32[5,4,128,128]{3,2,1,0:T(8,128)S(1)} %copy-done, f32[5,1,128,128]{3,2,1,0:T(8,128)} %collective-permute-done), kind=kLoop, calls=%fused_computation | loop fusion | flops 983040 | bytes 3932160 | tf_op jit(solution)/shard_map/concatenate | solution.py:129
  37.1 9.4 %all-to-all-done.1 = f32[32,2,641]{2,1,0:T(2,128)S(1)} async-done(((f32[32,2,641]{2,1,0:T(2,128)}), f32[32,2,641]{2,1,0:T(2,128)S(1)}, u32[]{:S(2)}, u32[]{:S(2)}) %all-to-all-start.1) | async-done | bytes 164128 | tf_op jit(solution)/shard_map/all_to_all | solution.py:250
  48.0 0.6 copy.45.inlet_ref
  48.6 9.6 %shard_map.91 = (f32[5,4,128,128]{3,2,1,0:T(8,128)}, f32[5,4,1,128]{3,2,1,0:T(1,128)}, f32[5,4,1,128]{3,2,1,0:T(1,128)}, f32[5,1,128,128]{3,2,1,0:T(8,128)}, f32[5,1,128,128]{3,2,1,0:T(8,128)}) custom-call(f32[75]{0:T(128)} %reshape.225.j_ref, f32[5,6,128,128]{3,2,1,0:T(8,128)} %pad_maximum_fusion.c_ref.cu_ref.cd_ref, ...), custom_call_target="tpu_custom_call" | custom-call | tf_op jit(solution)/shard_map/pallas_call | solution.py:136
  58.4 2.1 %fusion.5 = (f32[5,4,127,128]{3,2,1,0:T(8,128)S(1)}, f32[5,4,127,128]{3,2,1,0:T(8,128)S(1)}) fusion(f32[5,4,128,128]{3,2,1,0:T(8,128)} %get-tuple-element.12), kind=kLoop, calls=%fused_computation.47 | loop fusion | bytes 5201920 | tf_op jit(solution)/shard_map/jit(_roll_static)/slice | solution.py:132
  61.1 3.0 %collective-permute-start.4 = (f32[5,1,128,128]{3,2,1,0:T(8,128)S(1)}, f32[5,1,128,128]{3,2,1,0:T(8,128)S(1)}, u32[]{:S(2)}, u32[]{:S(2)}) collective-permute-start(f32[5,1,128,128]{3,2,1,0:T(8,128)S(1)} %copy-done.9), channel_id=1, source_target_pairs={{0,32},{32,64},{64,96},{96,128},{128,160},{160,192},{192,224},{224... | collective-permute-start | bytes 983048 | tf_op jit(solution)/shard_map/ppermute | solution.py:40
  64.1 3.2 %collective-permute-done.7 = f32[5,4,1,128]{3,2,1,0:T(1,128)S(1)} collective-permute-done((f32[5,4,1,128]{3,2,1,0:T(1,128)S(1)}, f32[5,4,1,128]{3,2,1,0:T(1,128)S(1)}, u32[]{:S(2)}, u32[]{:S(2)}) %collective-permute-start.7) | collective-permute-done | bytes 10272 | tf_op jit(solution)/shard_map/ppermute | solution.py:40
  67.4 1.9 %maximum_select_fusion.2 = (f32[5,4,128,128]{3,2,1,0:T(8,128)}, f32[5,4,128,128]{3,2,1,0:T(8,128)}) fusion(f32[5,4,1,128]{3,2,1,0:T(1,128)S(1)} %get-tuple-element.18, f32[5,4,127,128]{3,2,1,0:T(8,128)S(1)} %get-tuple-element.20, f32[5,4,128]{2,1,0:T(4,128)S(1)} %bitcast.17, pred[128]{0:T(512)(128)(4,1)S(1)} %iota_compare_fusion.7, ...), kind=kLoop, calls=%fused_computation.4 | loop fusion | flops 1310720 | bytes 5263616 | tf_op jit(solution)/shard_map/jit(_where)/select_n | solution.py:131
  69.3 2.3 %collective-permute-done.4 = f32[5,1,128,128]{3,2,1,0:T(8,128)S(1)} collective-permute-done((f32[5,1,128,128]{3,2,1,0:T(8,128)S(1)}, f32[5,1,128,128]{3,2,1,0:T(8,128)S(1)}, u32[]{:S(2)}, u32[]{:S(2)}) %collective-permute-start.4) | collective-permute-done | bytes 327712 | tf_op jit(solution)/shard_map/ppermute | solution.py:40
  71.6 4.3 %collective-permute-done.5 = f32[5,1,128,128]{3,2,1,0:T(8,128)S(1)} collective-permute-done((f32[5,1,128,128]{3,2,1,0:T(8,128)S(1)}, f32[5,1,128,128]{3,2,1,0:T(8,128)S(1)}, u32[]{:S(2)}, u32[]{:S(2)}) %collective-permute-start.5) | collective-permute-done | bytes 327712 | tf_op jit(solution)/shard_map/ppermute | solution.py:40
  75.9 1.5 %pad_maximum_fusion.1.c_ref.cu_ref.cd_ref = f32[5,6,128,128]{3,2,1,0:T(8,128)} fusion(f32[5,1,128,128]{3,2,1,0:T(8,128)S(1)} %collective-permute-done.5, f32[5,4,128,128]{3,2,1,0:T(8,128)S(1)} %copy-done.1, f32[5,1,128,128]{3,2,1,0:T(8,128)S(1)} %collective-permute-done.4), kind=kLoop, calls=%fused_computation.1 | loop fusion | flops 983040 | bytes 3932160 | tf_op jit(solution)/shard_map/concatenate | solution.py:129
  77.4 9.6 %shard_map.92 = (f32[5,4,128,128]{3,2,1,0:T(8,128)}, f32[5,4,1,128]{3,2,1,0:T(1,128)}, f32[5,4,1,128]{3,2,1,0:T(1,128)}, f32[5,1,128,128]{3,2,1,0:T(8,128)}, f32[5,1,128,128]{3,2,1,0:T(8,128)}) custom-call(f32[75]{0:T(128)} %reshape.225.j_ref, f32[5,6,128,128]{3,2,1,0:T(8,128)} %pad_maximum_fusion.1.c_ref.cu_ref.cd_ref, ...), custom_call_target="tpu_custom_call" | custom-call | tf_op jit(solution)/shard_map/pallas_call | solution.py:136
  (76 shorter events, 4.8 us)
Async XLA Ops:
  0.0 18.6 %copy-start = (f32[5,4,128,128]{3,2,1,0:T(8,128)S(1)}, f32[5,4,128,128]{3,2,1,0:T(8,128)}, u32[]{:S(2)}) copy-start(f32[5,4,128,128]{3,2,1,0:T(8,128)} %prev_ref.3) | copy-start | bytes 3932164
  1.1 20.9 %collective-permute-start.3 = (f32[5,4,1,128]{3,2,1,0:T(1,128)S(1)}, f32[5,4,1,128]{3,2,1,0:T(1,128)S(1)}, u32[]{:S(2)}, u32[]{:S(2)}) collective-permute-start(f32[5,4,1,128]{3,2,1,0:T(1,128)S(1)} %get-tuple-element.21), channel_id=1, source_target_pairs={{0,1},{1,2},{2,3},{3,4},{4,5},{5,6},{6,7},{7,8},{8,9},{9,10},{10,1... | collective-permute-start | bytes 30728 | tf_op jit(solution)/shard_map/ppermute | solution.py:45
  1.1 23.5 %collective-permute-start.2 = (f32[5,4,1,128]{3,2,1,0:T(1,128)S(1)}, f32[5,4,1,128]{3,2,1,0:T(1,128)S(1)}, u32[]{:S(2)}, u32[]{:S(2)}) collective-permute-start(f32[5,4,1,128]{3,2,1,0:T(1,128)S(1)} %get-tuple-element.22), channel_id=1, source_target_pairs={{1,0},{2,1},{3,2},{4,3},{5,4},{6,5},{7,6},{8,7},{9,8},{10,9},{11,1... | collective-permute-start | bytes 30728 | tf_op jit(solution)/shard_map/ppermute | solution.py:46
  10.5 14.2 %all-to-all-start = ((f32[8,5,4,128]{3,2,1,0:T(4,128)}), f32[8,5,4,128]{3,2,1,0:T(4,128)S(1)}, u32[]{:S(2)}, u32[]{:S(2)}) async-start(f32[8,5,4,128]{3,2,1,0:T(4,128)} %broadcast_in_dim.129), calls=%async_computation | async-start | bytes 163840 | tf_op jit(solution)/shard_map/all_to_all | solution.py:219
  16.5 18.0 %collective-permute-start = (f32[5,1,128,128]{3,2,1,0:T(8,128)S(1)}, f32[5,1,128,128]{3,2,1,0:T(8,128)}, u32[]{:S(2)}, u32[]{:S(2)}) collective-permute-start(f32[5,1,128,128]{3,2,1,0:T(8,128)S(1)} %get-tuple-element.25), channel_id=1, source_target_pairs={{0,32},{32,64},{64,96},{96,128},{128,160},{160,192},{192,224},{224... | collective-permute-start | bytes 983048 | tf_op jit(solution)/shard_map/ppermute | solution.py:45
  18.0 16.5 %collective-permute-start.1 = (f32[5,1,128,128]{3,2,1,0:T(8,128)S(1)}, f32[5,1,128,128]{3,2,1,0:T(8,128)}, u32[]{:S(2)}, u32[]{:S(2)}) collective-permute-start(f32[5,1,128,128]{3,2,1,0:T(8,128)S(1)} %get-tuple-element.26), channel_id=1, source_target_pairs={{32,0},{64,32},{96,64},{128,96},{160,128},{192,160},{224,192},{0,2... | collective-permute-start | bytes 983048 | tf_op jit(solution)/shard_map/ppermute | solution.py:46
  18.6 1.4 %copy-start.3 = (s32[1,4,4]{2,1,0:T(4,128)S(1)}, s32[1,4,4]{2,1,0:T(4,128)}, u32[]{:S(2)}) copy-start(s32[1,4,4]{2,1,0:T(4,128)} %param.14) | copy-start | bytes 196
  18.7 1.7 %copy-start.4 = (s32[1,4,4]{2,1,0:T(4,128)S(1)}, s32[1,4,4]{2,1,0:T(4,128)}, u32[]{:S(2)}) copy-start(s32[1,4,4]{2,1,0:T(4,128)} %param.15) | copy-start | bytes 196
  18.7 1.9 %copy-start.5 = (s32[1,4,4]{2,1,0:T(4,128)S(1)}, s32[1,4,4]{2,1,0:T(4,128)}, u32[]{:S(2)}) copy-start(s32[1,4,4]{2,1,0:T(4,128)} %param.16) | copy-start | bytes 196
  18.7 1.9 %copy-start.6 = (f32[16]{0:T(128)S(1)}, f32[16]{0:T(128)}, u32[]{:S(2)}) copy-start(f32[16]{0:T(128)} %param.17) | copy-start | bytes 196
  18.7 2.2 %copy-start.7 = (s32[128]{0:T(128)S(1)}, s32[128]{0:T(128)}, u32[]{:S(2)}) copy-start(s32[128]{0:T(128)} %param.13) | copy-start | bytes 1540
  18.7 2.5 %copy-start.2 = (f32[3,5,5]{2,0,1:T(4,128)S(1)}, f32[3,5,5]{2,0,1:T(4,128)}, u32[]{:S(2)}) copy-start(f32[3,5,5]{2,0,1:T(4,128)} %param.11) | copy-start | bytes 904
  26.2 20.3 %all-to-all-start.1 = ((f32[32,2,641]{2,1,0:T(2,128)}), f32[32,2,641]{2,1,0:T(2,128)S(1)}, u32[]{:S(2)}, u32[]{:S(2)}) async-start(f32[32,2,641]{2,1,0:T(2,128)} %copy.43), calls=%async_computation.1 | async-start | bytes 393216 | tf_op jit(solution)/shard_map/all_to_all | solution.py:250
  58.2 5.8 %collective-permute-start.6 = (f32[5,4,1,128]{3,2,1,0:T(1,128)}, f32[5,4,1,128]{3,2,1,0:T(1,128)S(1)}, u32[]{:S(2)}, u32[]{:S(2)}) collective-permute-start(f32[5,4,1,128]{3,2,1,0:T(1,128)} %get-tuple-element.14), channel_id=1, source_target_pairs={{1,0},{2,1},{3,2},{4,3},{5,4},{6,5},{7,6},{8,7},{9,8},{10,9},{11,1... | collective-permute-start | bytes 30728 | tf_op jit(solution)/shard_map/ppermute | solution.py:40
  58.3 2.2 %copy-start.1 = (f32[5,4,128,128]{3,2,1,0:T(8,128)S(1)}, f32[5,4,128,128]{3,2,1,0:T(8,128)}, u32[]{:S(2)}) copy-start(f32[5,4,128,128]{3,2,1,0:T(8,128)} %get-tuple-element.12) | copy-start | bytes 3932164
  58.3 2.2 %copy-start.10 = (f32[5,4,1,128]{3,2,1,0:T(1,128)S(1)}, f32[5,4,1,128]{3,2,1,0:T(1,128)}, u32[]{:S(2)}) copy-start(f32[5,4,1,128]{3,2,1,0:T(1,128)} %get-tuple-element.15) | copy-start | bytes 30724
  58.3 2.8 %copy-start.9 = (f32[5,1,128,128]{3,2,1,0:T(8,128)S(1)}, f32[5,1,128,128]{3,2,1,0:T(8,128)}, u32[]{:S(2)}) copy-start(f32[5,1,128,128]{3,2,1,0:T(8,128)} %get-tuple-element.11) | copy-start | bytes 983044
  58.4 5.7 %copy-start.8 = (f32[5,1,128,128]{3,2,1,0:T(8,128)S(1)}, f32[5,1,128,128]{3,2,1,0:T(8,128)}, u32[]{:S(2)}) copy-start(f32[5,1,128,128]{3,2,1,0:T(8,128)} %get-tuple-element.13) | copy-start | bytes 983044
  60.5 6.8 %collective-permute-start.7 = (f32[5,4,1,128]{3,2,1,0:T(1,128)S(1)}, f32[5,4,1,128]{3,2,1,0:T(1,128)S(1)}, u32[]{:S(2)}, u32[]{:S(2)}) collective-permute-start(f32[5,4,1,128]{3,2,1,0:T(1,128)S(1)} %copy-done.10), channel_id=1, source_target_pairs={{0,1},{1,2},{2,3},{3,4},{4,5},{5,6},{6,7},{7,8},{8,9},{9,10},{10,1... | collective-permute-start | bytes 30728 | tf_op jit(solution)/shard_map/ppermute | solution.py:40
  61.1 10.5 %collective-permute-start.4 = (f32[5,1,128,128]{3,2,1,0:T(8,128)S(1)}, f32[5,1,128,128]{3,2,1,0:T(8,128)S(1)}, u32[]{:S(2)}, u32[]{:S(2)}) collective-permute-start(f32[5,1,128,128]{3,2,1,0:T(8,128)S(1)} %copy-done.9), channel_id=1, source_target_pairs={{0,32},{32,64},{64,96},{96,128},{128,160},{160,192},{192,224},{224... | collective-permute-start | bytes 983048 | tf_op jit(solution)/shard_map/ppermute | solution.py:40
  64.1 11.8 %collective-permute-start.5 = (f32[5,1,128,128]{3,2,1,0:T(8,128)S(1)}, f32[5,1,128,128]{3,2,1,0:T(8,128)S(1)}, u32[]{:S(2)}, u32[]{:S(2)}) collective-permute-start(f32[5,1,128,128]{3,2,1,0:T(8,128)S(1)} %copy-done.8), channel_id=1, source_target_pairs={{32,0},{64,32},{96,64},{128,96},{160,128},{192,160},{224,192},{0,2... | collective-permute-start | bytes 983048 | tf_op jit(solution)/shard_map/ppermute | solution.py:40

commit v13 on v11

--- a/solution.py
+++ b/solution.py
@@ -63,7 +63,7 @@
 
 
 def stencil_kernel(
-    j_ref, c_ref, cu_ref, cd_ref, su_ref, sd_ref, prev_ref, rate_ref, inlet_ref,
+    j_ref, c_ref, cu_ref, cd_ref, low_ref, high_ref, su_ref, sd_ref, prev_ref, rate_ref, inlet_ref,
     out_ref, first_ref, last_ref, top_ref, bottom_ref, inlet_scr,
 ):
     span, axial = inlet_scr.shape[1:]
@@ -74,11 +74,14 @@
     probe = pltpu.roll(lane, 1, 1)
     numpy_order = probe == (lane + 127) % 128
 
+    at_bottom = pl.program_id(0) == 0
+    at_top = pl.program_id(0) == pl.num_programs(0) - 1
+
     def chunk(i, carry):
         rows = pl.ds(pl.multiple_of(i * 8, 8), 8)
         cur = [c_ref[g, 0, rows, :] for g in range(NF)]
-        cu = [cu_ref[g, 0, rows, :] for g in range(NF)]
-        cd = [cd_ref[g, 0, rows, :] for g in range(NF)]
+        cu = [jnp.where(at_top, high_ref[g, 0, rows, :], cu_ref[g, 0, rows, :]) for g in range(NF)]
+        cd = [jnp.where(at_bottom, low_ref[g, 0, rows, :], cd_ref[g, 0, rows, :]) for g in range(NF)]
         su = [su_ref[g, 0, rows, :] for g in range(NF)]
         sd = [sd_ref[g, 0, rows, :] for g in range(NF)]
         au, ad = [], []
@@ -126,7 +129,6 @@
     if parts is None:
         parts = halo_parts(current)
     circ_low, circ_high, span_low, span_high = parts
-    padded = jnp.concatenate([circ_low, current, circ_high], axis=1)
     span_up = jnp.concatenate([current[:, :, 1:], span_high], axis=2)
     span_down = jnp.concatenate([span_low, current[:, :, :-1]], axis=2)
     nf, rows, span, axial = current.shape
@@ -137,9 +139,11 @@
         grid=(rows,),
         in_specs=[
             pl.BlockSpec(memory_space=pltpu.SMEM),
-            spec(1),
-            spec(2),
-            spec(0),
+            spec(0),
+            pl.BlockSpec(block, lambda t: (0, jnp.minimum(t + 1, rows - 1), 0, 0)),
+            pl.BlockSpec(block, lambda t: (0, jnp.maximum(t - 1, 0), 0, 0)),
+            pl.BlockSpec(block, lambda t: (0, 0, 0, 0)),
+            pl.BlockSpec(block, lambda t: (0, 0, 0, 0)),
             spec(0),
             spec(0),
             spec(0),
@@ -153,7 +157,10 @@
         out_shape=[jax.ShapeDtypeStruct(current.shape, current.dtype)]
         + [jax.ShapeDtypeStruct((nf, rows, 1, axial), current.dtype)] * 2
         + [jax.ShapeDtypeStruct(block, current.dtype)] * 2,
-    )(jacobians.reshape(-1), padded, padded, padded, span_up, span_down, previous, rate_cells, inlet_rows)
+    )(
+        jacobians.reshape(-1), current, current, current, circ_low, circ_high,
+        span_up, span_down, previous, rate_cells, inlet_rows,
+    )
     out, first, last, top, bottom = out
     return out, (first, last, top, bottom)
 

time: 82.7 us -> 84.8 us (1.025)
  other arithmetic: 11.6 us -> 6.14 us
  local copies, waits for them, and re-layouts: 10.4 us -> 13.5 us
  waiting for transfers between devices: 14.7 us -> 17 us
  starting transfers between devices: 25.7 us -> 26.7 us
    concatenate x2 -> x0, other arithmetic: 4.07 us -> none  [sweep(): padded = jnp.concatenate([circ_low, current, circ_high], axis=1)]
    all_to_all x1, waiting for transfers between devices: 7.01 us -> 10.9 us  [body(): received = lax.all_to_all(payload, 'span', 0, 0, tiled=True)]
    ppermute x2, starting transfers between devices: 3.46 us -> 0.5 us  [halo_parts(): lax.ppermute(last, axis, forward)]
    unnamed x17 -> x25, local copies, waits for them, and re-layouts: 0.05 us -> 2.25 us
    ppermute x2, starting transfers between devices: 0.09 us -> 2.11 us  [halo_parts(): lax.ppermute(first, axis, backward)]
    slice x0 -> x1, local copies, waits for them, and re-layouts: none -> 1.96 us  [halo_parts(): high = lax.ppermute(lax.slice_in_dim(block, 0, 1, axis=dim), axis, backward)]
    ppermute x2, waiting for transfers between devices: 4.16 us -> 2.22 us  [halo_parts(): lax.ppermute(first, axis, backward)]
    ppermute x2, starting transfers between devices: 1.62 us -> 3.36 us  [halo_parts(): lax.ppermute(lax.slice_in_dim(block, block.shape[dim] - 1, None, axis=dim...]
  transfers between devices with their start and end apart: 10 -> 10, of which waited for: 4 -> 4; matrix products, arithmetic and copies ran while one was open for 22% -> 20% of each run, Pallas kernels for 0% -> 0%
where the time goes in v13:
time: 84.8 us; the launch traced here: 83.8 us
  starting transfers between devices  26.7 us (31%)
  Pallas kernels  19.7 us (23%)
  waiting for transfers between devices  17 us (20%)
  local copies, waits for them, and re-layouts  13.5 us (16%)
  other arithmetic  6.14 us (7%)
    pallas_call x2, Pallas kernels, sweep(): pl.pallas_call(stencil_kernel, grid=(rows,), in_specs=[pl.BlockSpec(memor...  19.7 us
    all_to_all x1, waiting for transfers between devices, body(): received = lax.all_to_all(payload, 'span', 0, 0, tiled=True)  10.9 us
    ppermute x2, starting transfers between devices, halo_parts(): high = lax.ppermute(lax.slice_in_dim(block, 0, 1, axis=dim), axis, backward)  8.86 us
    all_to_all x1, starting transfers between devices, body(): received = lax.all_to_all(payload, 'span', 0, 0, tiled=True)  7.03 us
    all_to_all x1, starting transfers between devices, body(): gathered = lax.all_to_all(copies, 'circ', 0, 0, tiled=True)  4.89 us
    ppermute x2, waiting for transfers between devices, halo_parts(): lax.ppermute(last, axis, forward)  3.8 us
    ppermute x2, starting transfers between devices, halo_parts(): lax.ppermute(lax.slice_in_dim(block, block.shape[dim] - 1, None, axis=dim...  3.36 us
    slice x2, local copies, waits for them, and re-layouts, sweep(): span_down = jnp.concatenate([span_low, current[:, :, :-1]], axis=2)  3.28 us
  transfers between devices with their start and end apart: 10, of which 4 were waited for; matrix products, arithmetic and copies ran while one was open for 20% of the time, Pallas kernels for 0%

profile of v13, /device:TPU:6, one launch (start us, length us, event | category | flops | bytes accessed | tf_op | source)
XLA Modules:
  0.0 83.8 jit_solution(11602738612810351648)
XLA Ops:
  0.0 1.0 %fusion.5 = (f32[5,4,1,128]{3,2,1,0:T(1,128)S(1)}, f32[5,4,1,128]{3,2,1,0:T(1,128)S(1)}) fusion(f32[5,4,128,128]{3,2,1,0:T(8,128)} %prev_ref.3), kind=kLoop, calls=%fused_computation.43 | loop fusion | bytes 40960 | tf_op jit(solution)/shard_map/slice | solution.py:45
  1.1 8.0 %collective-permute-start.2 = (f32[5,4,1,128]{3,2,1,0:T(1,128)S(1)}, f32[5,4,1,128]{3,2,1,0:T(1,128)S(1)}, u32[]{:S(2)}, u32[]{:S(2)}) collective-permute-start(f32[5,4,1,128]{3,2,1,0:T(1,128)S(1)} %get-tuple-element.20), channel_id=1, source_target_pairs={{1,0},{2,1},{3,2},{4,3},{5,4},{6,5},{7,6},{8,7},{9,8},{10,9},{11,1... | collective-permute-start | bytes 30728 | tf_op jit(solution)/shard_map/ppermute | solution.py:46
  9.1 1.3 %broadcast_in_dim.94 = f32[8,5,4,128]{3,2,1,0:T(4,128)} broadcast(f32[5,4,128]{2,1,0:T(4,128)} %param.12), dimensions={1,2,3} | broadcast | bytes 92160 | tf_op jit(solution)/shard_map/broadcast_in_dim | solution.py:224
  10.5 4.9 %all-to-all-start = ((f32[8,5,4,128]{3,2,1,0:T(4,128)}), f32[8,5,4,128]{3,2,1,0:T(4,128)S(1)}, u32[]{:S(2)}, u32[]{:S(2)}) async-start(f32[8,5,4,128]{3,2,1,0:T(4,128)} %broadcast_in_dim.94), calls=%async_computation | async-start | bytes 163840 | tf_op jit(solution)/shard_map/all_to_all | solution.py:225
  15.4 2.0 %fusion.7 = (f32[5,1,128,128]{3,2,1,0:T(8,128)}, f32[5,1,128,128]{3,2,1,0:T(8,128)}) fusion(f32[5,4,128,128]{3,2,1,0:T(8,128)} %prev_ref.3), kind=kLoop, calls=%fused_computation.45 | loop fusion | bytes 1310720 | tf_op jit(solution)/shard_map/slice | solution.py:46
  17.3 0.9 %collective-permute-start.1 = (f32[5,1,128,128]{3,2,1,0:T(8,128)}, f32[5,1,128,128]{3,2,1,0:T(8,128)S(1)}, u32[]{:S(2)}, u32[]{:S(2)}) collective-permute-start(f32[5,1,128,128]{3,2,1,0:T(8,128)} %get-tuple-element.23), channel_id=1, source_target_pairs={{32,0},{64,32},{96,64},{128,96},{160,128},{192,160},{224,192},{0,2... | collective-permute-start | bytes 983048 | tf_op jit(solution)/shard_map/ppermute | solution.py:46
  18.2 3.3 %collective-permute-start = (f32[5,1,128,128]{3,2,1,0:T(8,128)}, f32[5,1,128,128]{3,2,1,0:T(8,128)S(1)}, u32[]{:S(2)}, u32[]{:S(2)}) collective-permute-start(f32[5,1,128,128]{3,2,1,0:T(8,128)} %get-tuple-element.24), channel_id=1, source_target_pairs={{0,32},{32,64},{64,96},{96,128},{128,160},{160,192},{192,224},{224... | collective-permute-start | bytes 983048 | tf_op jit(solution)/shard_map/ppermute | solution.py:45
  21.6 1.3 %fusion.6 = (f32[5,4,127,128]{3,2,1,0:T(8,128)}, f32[5,4,127,128]{3,2,1,0:T(8,128)S(1)}) fusion(f32[5,4,128,128]{3,2,1,0:T(8,128)S(1)} %copy-done), kind=kLoop, calls=%fused_computation.44 | loop fusion | bytes 5201920 | tf_op jit(solution)/shard_map/slice | solution.py:133
  25.5 0.8 copy.43
  26.3 7.0 %all-to-all-start.1 = ((f32[32,2,641]{2,1,0:T(2,128)}), f32[32,2,641]{2,1,0:T(2,128)S(1)}, u32[]{:S(2)}, u32[]{:S(2)}) async-start(f32[32,2,641]{2,1,0:T(2,128)} %copy.43), calls=%async_computation.1 | async-start | bytes 393216 | tf_op jit(solution)/shard_map/all_to_all | solution.py:256
  33.4 1.2 %pad_maximum_fusion.1.sd_ref = f32[5,4,128,128]{3,2,1,0:T(8,128)} fusion(f32[5,4,127,128]{3,2,1,0:T(8,128)S(1)} %copy-done.1, f32[5,4,1,128]{3,2,1,0:T(1,128)S(1)} %broadcast_multiply_fusion.1), kind=kLoop, calls=%fused_computation.1 | loop fusion | flops 327680 | bytes 2621440 | tf_op jit(solution)/shard_map/concatenate | solution.py:133
  34.6 1.1 %pad_maximum_fusion.su_ref = f32[5,4,128,128]{3,2,1,0:T(8,128)} fusion(f32[5,4,1,128]{3,2,1,0:T(1,128)S(1)} %broadcast_multiply_fusion.3, f32[5,4,127,128]{3,2,1,0:T(8,128)S(1)} %get-tuple-element.22), kind=kLoop, calls=%fused_computation | loop fusion | flops 327680 | bytes 2621440 | tf_op jit(solution)/shard_map/concatenate | solution.py:132
  35.7 10.9 %all-to-all-done.1 = f32[32,2,641]{2,1,0:T(2,128)S(1)} async-done(((f32[32,2,641]{2,1,0:T(2,128)}), f32[32,2,641]{2,1,0:T(2,128)S(1)}, u32[]{:S(2)}, u32[]{:S(2)}) %all-to-all-start.1) | async-done | bytes 164128 | tf_op jit(solution)/shard_map/all_to_all | solution.py:256
  49.5 0.7 copy-done.3
  50.2 9.9 %shard_map.91 = (f32[5,4,128,128]{3,2,1,0:T(8,128)}, f32[5,4,1,128]{3,2,1,0:T(1,128)}, f32[5,4,1,128]{3,2,1,0:T(1,128)}, f32[5,1,128,128]{3,2,1,0:T(8,128)}, f32[5,1,128,128]{3,2,1,0:T(8,128)}) custom-call(f32[75]{0:T(128)} %reshape.225.j_ref, f32[5,4,128,128]{3,2,1,0:T(8,128)} %prev_ref.3, f32[5,4,128,128]{3,2,1,0:T(8,128)} %prev_ref.3, ...), custom_call_target="tpu_custom_call" | custom-call | tf_op jit(solution)/shard_map/pallas_call | solution.py:137
  60.7 2.0 %collective-permute-start.5 = (f32[5,1,128,128]{3,2,1,0:T(8,128)}, f32[5,1,128,128]{3,2,1,0:T(8,128)S(1)}, u32[]{:S(2)}, u32[]{:S(2)}) collective-permute-start(f32[5,1,128,128]{3,2,1,0:T(8,128)} %get-tuple-element.13), channel_id=1, source_target_pairs={{32,0},{64,32},{96,64},{128,96},{160,128},{192,160},{224,192},{0,2... | collective-permute-start | bytes 983048 | tf_op jit(solution)/shard_map/ppermute | solution.py:40
  62.8 2.0 %fusion.4 = (f32[5,4,127,128]{3,2,1,0:T(8,128)S(1)}, f32[5,4,127,128]{3,2,1,0:T(8,128)S(1)}) fusion(f32[5,4,128,128]{3,2,1,0:T(8,128)} %get-tuple-element.11.c_ref.cu_ref.cd_ref), kind=kLoop, calls=%fused_computation.42 | loop fusion | bytes 5201920 | tf_op jit(solution)/shard_map/slice | solution.py:133
  64.8 2.5 %collective-permute-done.7 = f32[5,4,1,128]{3,2,1,0:T(1,128)S(1)} collective-permute-done((f32[5,4,1,128]{3,2,1,0:T(1,128)}, f32[5,4,1,128]{3,2,1,0:T(1,128)S(1)}, u32[]{:S(2)}, u32[]{:S(2)}) %collective-permute-start.7) | collective-permute-done | bytes 10272 | tf_op jit(solution)/shard_map/ppermute | solution.py:40
  67.4 1.2 %pad_maximum_fusion.3.sd_ref = f32[5,4,128,128]{3,2,1,0:T(8,128)} fusion(f32[5,4,127,128]{3,2,1,0:T(8,128)S(1)} %get-tuple-element.17, f32[5,4,1,128]{3,2,1,0:T(1,128)S(1)} %broadcast_multiply_fusion), kind=kLoop, calls=%fused_computation.3 | loop fusion | flops 327680 | bytes 2621440 | tf_op jit(solution)/shard_map/concatenate | solution.py:133
  68.6 1.2 %pad_maximum_fusion.2.su_ref = f32[5,4,128,128]{3,2,1,0:T(8,128)} fusion(f32[5,4,1,128]{3,2,1,0:T(1,128)S(1)} %broadcast_multiply_fusion.2, f32[5,4,127,128]{3,2,1,0:T(8,128)S(1)} %get-tuple-element.18), kind=kLoop, calls=%fused_computation.2 | loop fusion | flops 327680 | bytes 2621440 | tf_op jit(solution)/shard_map/concatenate | solution.py:132
  69.7 1.3 %collective-permute-done.4.low_ref = f32[5,1,128,128]{3,2,1,0:T(8,128)S(1)} collective-permute-done((f32[5,1,128,128]{3,2,1,0:T(8,128)}, f32[5,1,128,128]{3,2,1,0:T(8,128)S(1)}, u32[]{:S(2)}, u32[]{:S(2)}) %collective-permute-start.4) | collective-permute-done | bytes 327712 | tf_op jit(solution)/shard_map/ppermute | solution.py:40
  71.0 2.2 %collective-permute-done.5.high_ref = f32[5,1,128,128]{3,2,1,0:T(8,128)S(1)} collective-permute-done((f32[5,1,128,128]{3,2,1,0:T(8,128)}, f32[5,1,128,128]{3,2,1,0:T(8,128)S(1)}, u32[]{:S(2)}, u32[]{:S(2)}) %collective-permute-start.5) | collective-permute-done | bytes 327712 | tf_op jit(solution)/shard_map/ppermute | solution.py:40
  73.2 0.7 copy-done.5
  73.9 9.8 %shard_map.92 = (f32[5,4,128,128]{3,2,1,0:T(8,128)}, f32[5,4,1,128]{3,2,1,0:T(1,128)}, f32[5,4,1,128]{3,2,1,0:T(1,128)}, f32[5,1,128,128]{3,2,1,0:T(8,128)}, f32[5,1,128,128]{3,2,1,0:T(8,128)}) custom-call(f32[75]{0:T(128)} %reshape.225.j_ref, f32[5,4,128,128]{3,2,1,0:T(8,128)} %get-tuple-element.11.c_ref.cu_ref.cd_ref, ...), custom_call_target="tpu_custom_call" | custom-call | tf_op jit(solution)/shard_map/pallas_call | solution.py:137
  (74 shorter events, 6.1 us)
Async XLA Ops:
  0.0 21.5 %copy-start = (f32[5,4,128,128]{3,2,1,0:T(8,128)S(1)}, f32[5,4,128,128]{3,2,1,0:T(8,128)}, u32[]{:S(2)}) copy-start(f32[5,4,128,128]{3,2,1,0:T(8,128)} %prev_ref.3) | copy-start | bytes 3932164
  1.1 23.7 %collective-permute-start.3 = (f32[5,4,1,128]{3,2,1,0:T(1,128)S(1)}, f32[5,4,1,128]{3,2,1,0:T(1,128)S(1)}, u32[]{:S(2)}, u32[]{:S(2)}) collective-permute-start(f32[5,4,1,128]{3,2,1,0:T(1,128)S(1)} %get-tuple-element.19), channel_id=1, source_target_pairs={{0,1},{1,2},{2,3},{3,4},{4,5},{5,6},{6,7},{7,8},{8,9},{9,10},{10,1... | collective-permute-start | bytes 30728 | tf_op jit(solution)/shard_map/ppermute | solution.py:45
  1.1 32.2 %collective-permute-start.2 = (f32[5,4,1,128]{3,2,1,0:T(1,128)S(1)}, f32[5,4,1,128]{3,2,1,0:T(1,128)S(1)}, u32[]{:S(2)}, u32[]{:S(2)}) collective-permute-start(f32[5,4,1,128]{3,2,1,0:T(1,128)S(1)} %get-tuple-element.20), channel_id=1, source_target_pairs={{1,0},{2,1},{3,2},{4,3},{5,4},{6,5},{7,6},{8,7},{9,8},{10,9},{11,1... | collective-permute-start | bytes 30728 | tf_op jit(solution)/shard_map/ppermute | solution.py:46
  10.5 14.3 %all-to-all-start = ((f32[8,5,4,128]{3,2,1,0:T(4,128)}), f32[8,5,4,128]{3,2,1,0:T(4,128)S(1)}, u32[]{:S(2)}, u32[]{:S(2)}) async-start(f32[8,5,4,128]{3,2,1,0:T(4,128)} %broadcast_in_dim.94), calls=%async_computation | async-start | bytes 163840 | tf_op jit(solution)/shard_map/all_to_all | solution.py:225
  17.3 31.4 %collective-permute-start.1 = (f32[5,1,128,128]{3,2,1,0:T(8,128)}, f32[5,1,128,128]{3,2,1,0:T(8,128)S(1)}, u32[]{:S(2)}, u32[]{:S(2)}) collective-permute-start(f32[5,1,128,128]{3,2,1,0:T(8,128)} %get-tuple-element.23), channel_id=1, source_target_pairs={{32,0},{64,32},{96,64},{128,96},{160,128},{192,160},{224,192},{0,2... | collective-permute-start | bytes 983048 | tf_op jit(solution)/shard_map/ppermute | solution.py:46
  18.2 30.6 %collective-permute-start = (f32[5,1,128,128]{3,2,1,0:T(8,128)}, f32[5,1,128,128]{3,2,1,0:T(8,128)S(1)}, u32[]{:S(2)}, u32[]{:S(2)}) collective-permute-start(f32[5,1,128,128]{3,2,1,0:T(8,128)} %get-tuple-element.24), channel_id=1, source_target_pairs={{0,32},{32,64},{64,96},{96,128},{128,160},{160,192},{192,224},{224... | collective-permute-start | bytes 983048 | tf_op jit(solution)/shard_map/ppermute | solution.py:45
  21.5 1.4 %copy-start.7 = (s32[1,4,4]{2,1,0:T(4,128)S(1)}, s32[1,4,4]{2,1,0:T(4,128)}, u32[]{:S(2)}) copy-start(s32[1,4,4]{2,1,0:T(4,128)} %param.14) | copy-start | bytes 196
  21.5 1.7 %copy-start.8 = (s32[1,4,4]{2,1,0:T(4,128)S(1)}, s32[1,4,4]{2,1,0:T(4,128)}, u32[]{:S(2)}) copy-start(s32[1,4,4]{2,1,0:T(4,128)} %param.15) | copy-start | bytes 196
  21.5 1.9 %copy-start.9 = (s32[1,4,4]{2,1,0:T(4,128)S(1)}, s32[1,4,4]{2,1,0:T(4,128)}, u32[]{:S(2)}) copy-start(s32[1,4,4]{2,1,0:T(4,128)} %param.16) | copy-start | bytes 196
  21.5 1.9 %copy-start.10 = (f32[16]{0:T(128)S(1)}, f32[16]{0:T(128)}, u32[]{:S(2)}) copy-start(f32[16]{0:T(128)} %param.17) | copy-start | bytes 196
  21.5 2.2 %copy-start.11 = (s32[128]{0:T(128)S(1)}, s32[128]{0:T(128)}, u32[]{:S(2)}) copy-start(s32[128]{0:T(128)} %param.13) | copy-start | bytes 1540
  21.6 2.5 %copy-start.6 = (f32[3,5,5]{2,0,1:T(4,128)S(1)}, f32[3,5,5]{2,0,1:T(4,128)}, u32[]{:S(2)}) copy-start(f32[3,5,5]{2,0,1:T(4,128)} %param.11) | copy-start | bytes 904
  22.8 10.6 %copy-start.1 = (f32[5,4,127,128]{3,2,1,0:T(8,128)S(1)}, f32[5,4,127,128]{3,2,1,0:T(8,128)}, u32[]{:S(2)}) copy-start(f32[5,4,127,128]{3,2,1,0:T(8,128)} %get-tuple-element.21) | copy-start | bytes 3901444
  26.3 20.3 %all-to-all-start.1 = ((f32[32,2,641]{2,1,0:T(2,128)}), f32[32,2,641]{2,1,0:T(2,128)S(1)}, u32[]{:S(2)}, u32[]{:S(2)}) async-start(f32[32,2,641]{2,1,0:T(2,128)} %copy.43), calls=%async_computation.1 | async-start | bytes 393216 | tf_op jit(solution)/shard_map/all_to_all | solution.py:256
  48.8 0.7 copy-start.2
  49.5 0.7 copy-start.3
  60.2 4.6 %collective-permute-start.6 = (f32[5,4,1,128]{3,2,1,0:T(1,128)}, f32[5,4,1,128]{3,2,1,0:T(1,128)S(1)}, u32[]{:S(2)}, u32[]{:S(2)}) collective-permute-start(f32[5,4,1,128]{3,2,1,0:T(1,128)} %get-tuple-element.14), channel_id=1, source_target_pairs={{1,0},{2,1},{3,2},{4,3},{5,4},{6,5},{7,6},{8,7},{9,8},{10,9},{11,1... | collective-permute-start | bytes 30728 | tf_op jit(solution)/shard_map/ppermute | solution.py:40
  60.2 7.1 %collective-permute-start.7 = (f32[5,4,1,128]{3,2,1,0:T(1,128)}, f32[5,4,1,128]{3,2,1,0:T(1,128)S(1)}, u32[]{:S(2)}, u32[]{:S(2)}) collective-permute-start(f32[5,4,1,128]{3,2,1,0:T(1,128)} %get-tuple-element.15), channel_id=1, source_target_pairs={{0,1},{1,2},{2,3},{3,4},{4,5},{5,6},{6,7},{7,8},{8,9},{9,10},{10,1... | collective-permute-start | bytes 30728 | tf_op jit(solution)/shard_map/ppermute | solution.py:40
  60.7 10.2 %collective-permute-start.4 = (f32[5,1,128,128]{3,2,1,0:T(8,128)}, f32[5,1,128,128]{3,2,1,0:T(8,128)S(1)}, u32[]{:S(2)}, u32[]{:S(2)}) collective-permute-start(f32[5,1,128,128]{3,2,1,0:T(8,128)} %get-tuple-element.12), channel_id=1, source_target_pairs={{0,32},{32,64},{64,96},{96,128},{128,160},{160,192},{192,224},{224... | collective-permute-start | bytes 983048 | tf_op jit(solution)/shard_map/ppermute | solution.py:40
  60.7 12.4 %collective-permute-start.5 = (f32[5,1,128,128]{3,2,1,0:T(8,128)}, f32[5,1,128,128]{3,2,1,0:T(8,128)S(1)}, u32[]{:S(2)}, u32[]{:S(2)}) collective-permute-start(f32[5,1,128,128]{3,2,1,0:T(8,128)} %get-tuple-element.13), channel_id=1, source_target_pairs={{32,0},{64,32},{96,64},{128,96},{160,128},{192,160},{224,192},{0,2... | collective-permute-start | bytes 983048 | tf_op jit(solution)/shard_map/ppermute | solution.py:40
  71.0 2.2 %copy-start.4 = (f32[5,1,128,128]{3,2,1,0:T(8,128)}, f32[5,1,128,128]{3,2,1,0:T(8,128)S(1)}, u32[]{:S(2)}) copy-start(f32[5,1,128,128]{3,2,1,0:T(8,128)S(1)} %collective-permute-done.4.low_ref) | copy-start | bytes 983044
  73.2 0.7 copy-start.5
